TPU v7x, 512 devices: a whole 4x4x16 slice. The times are simulated.
512 devices in a mesh: blk: 128 (over x, z, y_lo), frq: 4 (over y_hi, core).
Axes of the slice: x: 4, y: 4 (y_hi: 2, y_lo: 2; y = y_hi * 2 + y_lo), z: 16, core: 2. Of those that a mesh axis runs over, the one named last changes fastest.
Arguments:
- spectra: bfloat16 [2, 3, 2048, 512], P(None, None, 'blk', 'frq'), may hold values from -6 to 6
- observed: bfloat16 [32768, 3, 3, 1024], P(('blk', 'frq')), may hold values from -6 to 6
- own_station: int32 [128, 128, 2], P('blk'), may hold values from 0 to 15
- partner_station: int32 [128, 128, 2], P('blk'), may hold values from 0 to 15, as said below
- pair_count: int32 [128, 128], P('blk'), may hold values from 1 to 2, as said below
Outputs:
- adjoint: float32 [1024, 3, 2048], P('frq', None, 'blk')
Inputs may be any that keep to these rules, and one draw needn't show every extreme that they name: `partner_station`: within the reading block's own block pair, a slot's two stations differ. `pair_count`: the live slots of a block pair are its first ones; every reading block has a block pair with all 2 slots live.
All inputs are finite; a program needn't handle non-finite values.
Results may differ from a plain program's by a relative error of at most 0.003.
Values may be sent and summed in bfloat16 or wider, within the bound.
No kernel may reach another device: no remote copies, remote signals or barrier semaphores. Data moves between devices by JAX's collectives and lax.ppermute only.
A program may use at most 64 MiB of HBM per device.

v0:
```python
import math

import jax
import jax.numpy as jnp
from jax import lax
from jax.sharding import PartitionSpec as P

NF = 512
NT = 1024


def phase_table(freq_start, freq_count, time_count):
    freq_index = lax.iota(jnp.int32, freq_count) + freq_start
    time_index = lax.iota(jnp.int32, time_count)
    phase_num = (2 * freq_index + 1)[:, None] * time_index[None, :] % (2 * NT)
    return phase_num.astype(jnp.float32) * (math.pi / NT)


def lag_window():
    time_index = lax.iota(jnp.int32, NT)
    lag_size = jnp.minimum(time_index, NT - time_index)
    return ((lag_size >= NT // 32) & (lag_size < NT // 4)).astype(jnp.float32)


def cross_spectra(first_rows, second_rows):
    real_part = (
        first_rows[:, 0, :, None] * second_rows[:, 0, None, :]
        + first_rows[:, 1, :, None] * second_rows[:, 1, None, :]
    )
    imag_part = (
        first_rows[:, 1, :, None] * second_rows[:, 0, None, :]
        - first_rows[:, 0, :, None] * second_rows[:, 1, None, :]
    )
    return jnp.stack([real_part, imag_part], axis=3)


def pair_gradients(adjoint_rows, first_rows, second_rows):
    adj_real = adjoint_rows[:, :, :, 0]
    adj_imag = adjoint_rows[:, :, :, 1]
    own_real = jnp.sum(
        adj_real * second_rows[:, 0, None] - adj_imag * second_rows[:, 1, None], axis=2
    )
    own_imag = jnp.sum(
        adj_real * second_rows[:, 1, None] + adj_imag * second_rows[:, 0, None], axis=2
    )
    far_real = jnp.sum(
        adj_real * first_rows[:, 0, :, None] + adj_imag * first_rows[:, 1, :, None], axis=1
    )
    far_imag = jnp.sum(
        adj_real * first_rows[:, 1, :, None] - adj_imag * first_rows[:, 0, :, None], axis=1
    )
    return (jnp.stack([own_real, own_imag], axis=1), jnp.stack([far_real, far_imag], axis=1))


def local(spectra, observed, own_station, partner_station, pair_count):
    block_total = lax.axis_size("blk")
    band_total = lax.axis_size("frq")
    per_block = spectra.shape[2]
    freq_dev = spectra.shape[3]
    slot_cap = own_station.shape[2]
    slot_total = block_total * slot_cap
    item_count = slot_total // band_total
    band_index = lax.axis_index("frq")
    spec_rows = jnp.transpose(spectra, (2, 0, 1, 3))
    own_ids = own_station[0].reshape(slot_total)
    partner_local = partner_station[0]
    partner_ids = partner_local.reshape(slot_total)
    alive_mask = (
        (lax.iota(jnp.int32, slot_cap)[None, :] < pair_count[0][:, None])
        .reshape(slot_total)
        .astype(jnp.float32)
    )
    asked_ids = lax.all_to_all(partner_local, "blk", split_axis=0, concat_axis=0, tiled=True)
    asked_rows = jnp.take(spec_rows, asked_ids.reshape(slot_total), axis=0, mode="clip")
    rows_new = lax.all_to_all(
        asked_rows.reshape(block_total, slot_cap * 2 * 3 * freq_dev),
        "blk",
        split_axis=0,
        concat_axis=0,
        tiled=True,
    ).reshape(band_total, item_count, 2, 3, freq_dev)
    own_table = jnp.broadcast_to(spec_rows[None], (band_total, per_block, 2, 3, freq_dev))
    sent = jnp.concatenate([rows_new, own_table], axis=1)
    whole_band = lax.all_to_all(sent, "frq", split_axis=0, concat_axis=0, tiled=True)
    whole_band = jnp.transpose(whole_band, (2, 3, 1, 0, 4)).reshape(
        2, 3, item_count + per_block, NF
    )
    second_rows = whole_band[:, :, :item_count].astype(jnp.float32)
    own_group = lax.dynamic_slice_in_dim(own_ids, band_index * item_count, item_count)
    first_rows = jnp.take(
        whole_band[:, :, item_count:], own_group, axis=2, mode="clip"
    ).astype(jnp.float32)
    alive_band = lax.dynamic_slice_in_dim(alive_mask, band_index * item_count, item_count)
    first_re = first_rows[0][:, None]
    first_im = first_rows[1][:, None]
    second_re = second_rows[0][None]
    second_im = second_rows[1][None]
    alive_col = alive_band[None, None, :, None]
    cross = (
        jnp.concatenate(
            [
                first_re * second_re + first_im * second_im,
                first_im * second_re - first_re * second_im,
            ],
            axis=3,
        )
        * alive_col
    ).astype(jnp.bfloat16)
    lag_low = NT // 32
    lag_high = NT // 4
    lag_index = jnp.concatenate(
        [
            lax.iota(jnp.int32, lag_high - lag_low) + lag_low,
            lax.iota(jnp.int32, lag_high - lag_low) + (NT - lag_high + 1),
        ]
    )
    phase = (2 * lax.iota(jnp.int32, NF) + 1)[:, None] * lag_index[None, :] % (2 * NT)
    phase = phase.astype(jnp.float32) * (math.pi / NT)
    basis = jnp.concatenate(
        [
            (jnp.cos(phase) / math.sqrt(NF)).astype(jnp.bfloat16),
            -(jnp.sin(phase) / math.sqrt(NF)).astype(jnp.bfloat16),
        ],
        axis=0,
    )
    window = lag_window()[lag_index]
    observed_all = jnp.transpose(observed, (1, 2, 0, 3)).reshape(9 * item_count, NT)
    observed_rows = jnp.concatenate(
        [
            observed_all[:, lag_low:lag_high],
            observed_all[:, NT - lag_high + 1 : NT - lag_low + 1],
        ],
        axis=1,
    ).astype(jnp.float32)
    station_iota = lax.iota(jnp.int32, per_block)
    correlation = jnp.dot(
        cross.reshape(9 * item_count, 2 * NF), basis, preferred_element_type=jnp.float32
    )
    residual = (
        (correlation - observed_rows) * jnp.tile(alive_band, 9)[:, None] * window[None, :]
    ).astype(jnp.bfloat16)
    adjoint_rows = lax.reduce_precision(
        lax.dot_general(
            residual, basis, (((1,), (1,)), ((), ())), preferred_element_type=jnp.float32
        ),
        exponent_bits=8,
        mantissa_bits=7,
    ).reshape(3, 3, item_count, 2 * NF)
    adj_re = adjoint_rows[..., :NF]
    adj_im = adjoint_rows[..., NF:]
    own_re = jnp.sum(adj_re * second_re - adj_im * second_im, axis=1)
    own_im = jnp.sum(adj_re * second_im + adj_im * second_re, axis=1)
    far_re = jnp.sum(adj_re * first_re + adj_im * first_im, axis=0)
    far_im = jnp.sum(adj_re * first_im - adj_im * first_re, axis=0)
    own_onehot = (own_group[None, :] == station_iota[:, None]).astype(jnp.float32)
    grad_group = lax.dot_general(
        own_onehot,
        jnp.stack([own_re, own_im]),
        (((1,), (2,)), ((), ())),
        precision=lax.Precision.HIGHEST,
        preferred_element_type=jnp.float32,
    )
    grad_high = lax.reduce_precision(grad_group, exponent_bits=8, mantissa_bits=7)
    grad_low = (grad_group - grad_high).astype(jnp.bfloat16)
    far_grad = jnp.transpose(jnp.stack([far_re, far_im]), (2, 0, 1, 3)).astype(jnp.bfloat16)
    back_sent = jnp.concatenate([far_grad, grad_high.astype(jnp.bfloat16), grad_low], axis=0)
    back_sent = jnp.transpose(
        back_sent.reshape(item_count + 2 * per_block, 2, 3, band_total, freq_dev), (3, 0, 1, 2, 4)
    )
    band_back = lax.all_to_all(back_sent, "frq", split_axis=0, concat_axis=0, tiled=True)
    far_band = band_back[:, :item_count].reshape(block_total, slot_cap * 2 * 3 * freq_dev)
    grad_local = jnp.sum(
        band_back[:, item_count : item_count + per_block].astype(jnp.float32)
        + band_back[:, item_count + per_block :].astype(jnp.float32),
        axis=0,
    ).reshape(per_block, 6 * freq_dev)
    back_grad = lax.all_to_all(far_band, "blk", split_axis=0, concat_axis=0, tiled=True).astype(
        jnp.float32
    )
    back_onehot = (asked_ids.reshape(slot_total)[None, :] == station_iota[:, None]).astype(
        jnp.float32
    )
    station_grad = grad_local + jnp.dot(
        back_onehot,
        back_grad.reshape(slot_total, 6 * freq_dev),
        precision=lax.Precision.HIGHEST,
        preferred_element_type=jnp.float32,
    )
    grad_matrix = jnp.transpose(
        station_grad.reshape(per_block, 2, 3, freq_dev), (1, 3, 2, 0)
    ).reshape(2 * freq_dev, 3 * per_block)
    output_scale = 1.0 / math.sqrt(2.0 * block_total * slot_cap / per_block)
    phase_part = phase_table(
        band_index * freq_dev, freq_dev, NT // band_total * lax.axis_size("frq")
    )
    basis_part = jnp.concatenate(
        [jnp.cos(phase_part) / math.sqrt(NF), -(jnp.sin(phase_part) / math.sqrt(NF))], axis=0
    )
    product = lax.dot_general(
        basis_part,
        grad_matrix,
        (((0,), (0,)), ((), ())),
        precision=lax.Precision.HIGHEST,
        preferred_element_type=jnp.float32,
    )
    lag_parts = lax.all_to_all(
        product.reshape(band_total, NT // band_total, 3, per_block) * output_scale,
        "frq",
        split_axis=0,
        concat_axis=0,
        tiled=True,
    )
    return jnp.sum(lag_parts, axis=0)


def solution(mesh):
    return jax.shard_map(
        local,
        mesh=mesh,
        in_specs=(
            P(None, None, "blk", "frq"),
            P(("blk", "frq"), None, None, None),
            P("blk", None, None),
            P("blk", None, None),
            P("blk", None),
        ),
        out_specs=P("frq", None, "blk"),
        check_vma=False,
    )
```

profile of v0, /device:TPU:1, one launch (start us, length us, event | category | flops | bytes accessed | tf_op | source)
XLA Modules:
  0.0 180.5 jit_solution(1068259572857024030)
XLA Ops:
  0.0 1.4 copy.39
  1.4 21.3 %all-to-all-start = ((s32[128,1,2]{2,1,0:T(1,128)}), s32[128,1,2]{2,1,0:T(1,128)S(1)}, u32[]{:S(2)}, u32[]{:S(2)}) async-start(s32[128,1,2]{2,1,0:T(1,128)} %bitcast.5), calls=%async_computation | async-start | bytes 131072 | tf_op jit(solution)/shard_map/all_to_all | solution.py:73
  23.5 13.5 %all-to-all-done = s32[128,1,2]{2,1,0:T(1,128)S(1)} async-done(((s32[128,1,2]{2,1,0:T(1,128)}), s32[128,1,2]{2,1,0:T(1,128)S(1)}, u32[]{:S(2)}, u32[]{:S(2)}) %all-to-all-start) | async-done | bytes 1056 | tf_op jit(solution)/shard_map/all_to_all | solution.py:73
  38.5 1.5 gather_fusion
  41.1 3.1 %reduce.6 = bf16[128,1536]{1,0:T(8,128)(2,1)S(1)} reduce(bf16[128,1,1536]{2,1,0:T(2,128)(2,1)S(1)} %all_to_all.36, bf16[]{:T(256)} %broadcast.134), dimensions={1}, to_apply=%all_to_all.36.reduce_sub_computation | reduce | bytes 786434 | tf_op jit(solution)/shard_map/all_to_all | solution.py:75
  45.1 6.4 %all-to-all-start.1 = ((bf16[128,2,768]{2,1,0:T(2,128)(2,1)}), bf16[128,2,768]{2,1,0:T(2,128)(2,1)S(1)}, u32[]{:S(2)}, u32[]{:S(2)}) async-start(bf16[128,2,768]{2,1,0:T(2,128)(2,1)} %reshape.196), calls=%async_computation.1 | async-start | bytes 786432 | tf_op jit(solution)/shard_map/all_to_all | solution.py:75
  51.7 4.3 %fusion.30 = bf16[512,448]{1,0:T(8,128)(2,1)S(1)} fusion(s32[448]{0:T(512)S(1)} %pad_add_fusion, s32[512]{0:T(512)S(1)} %multiply_add_fusion.1), kind=kLoop, calls=%fused_computation.52 | loop fusion | flops 4358144 | bytes 462592 | tf_op jit(solution)/shard_map/neg | solution.py:122
  56.3 19.0 %all-to-all-done.1 = bf16[128,2,768]{2,1,0:T(2,128)(2,1)S(1)} async-done(((bf16[128,2,768]{2,1,0:T(2,128)(2,1)}), bf16[128,2,768]{2,1,0:T(2,128)(2,1)S(1)}, u32[]{:S(2)}, u32[]{:S(2)}) %all-to-all-start.1) | async-done | bytes 393248 | tf_op jit(solution)/shard_map/all_to_all | solution.py:75
  75.6 2.5 %reduce.1 = bf16[128,1536]{1,0:T(8,128)(2,1)S(1)} reduce(bf16[128,1,1536]{2,1,0:T(2,128)(2,1)S(1)} %reshape.197, bf16[]{:T(256)} %constant.70), dimensions={1}, to_apply=%all_to_all.30.reduce_sub_computation | reduce | bytes 786434 | tf_op jit(solution)/shard_map/all_to_all | solution.py:75
  79.7 9.5 %all-to-all-start.2 = ((bf16[4,80,2,3,128]{4,1,3,2,0:T(8,128)(2,1)}), bf16[4,80,2,3,128]{4,1,3,2,0:T(8,128)(2,1)S(1)}, u32[]{:S(2)}, u32[]{:S(2)}) async-start(bf16[4,80,2,3,128]{4,1,3,2,0:T(8,128)(2,1)} %copy.43), calls=%async_computation.2 | async-start | bytes 983040 | tf_op jit(solution)/shard_map/all_to_all | solution.py:84
  91.6 2.1 %gather_fusion.2 = f32[448]{0:T(512)S(1)} fusion(f32[1024]{0:T(1024)S(1)} %fusion.43, s32[1024]{0:T(1024)S(1)} %pad_clamp_fusion), kind=kCustom, calls=%fused_computation.2 | custom fusion | bytes 5376 | tf_op jit(solution)/shard_map/gather | solution.py:126
  93.7 4.9 %multiply_convert_fusion.1 = bf16[512,448]{1,0:T(8,128)(2,1)} fusion(s32[448]{0:T(512)S(1)} %pad_add_fusion, s32[512]{0:T(512)S(1)} %multiply_add_fusion.1), kind=kLoop, calls=%fused_computation.33 | loop fusion | flops 3670016 | bytes 462592 | tf_op jit(solution)/shard_map/convert_element_type | solution.py:121
  99.4 1.4 gather_fusion.1
  102.5 1.4 multiply_add_fusion
  103.9 5.3 %convolution_reduce-precision_fusion = f32[576,1024]{1,0:T(8,128)} fusion(f32[576,512]{1,0:T(8,128)} %bitcast.81, f32[576,512]{1,0:T(8,128)S(1)} %bitcast.80, f32[576]{0:T(1024)S(1)} %mul.232, bf16[512,448]{1,0:T(8,128)(2,1)S(1)} %fusion.30, bf16[512,448]{1,0:T(8,128)(2,1)} %multiply_convert_fusion.1, bf16[576,224]{0,1:T(8,128)(2,1)} %copy.62, ...), kind=kOutput, calls=%fused_computation.8 | convolution fusion | flops 1065058304 | bytes 6158592 | tf_op jit(solution)/shard_map/dot_general | solution.py:143
  109.1 2.4 %add_reduce_fusion.1 = (bf16[3,64,512]{2,1,0:T(8,128)(2,1)S(1)}, bf16[3,64,512]{2,1,0:T(8,128)(2,1)S(1)}, f32[3,64,512]{2,1,0:T(8,128)S(1)}, f32[3,64,512]{2,1,0:T(8,128)S(1)}) fusion(f32[3,3,64,1024]{3,2,1,0:T(8,128)} %bitcast.75, f32[3,64,512]{2,1,0:T(8,128)S(1)} %get-tuple-element.25, f32[3,64,512]{2,1,0:T(8,128)S(1)} %get-tuple-element.26, ...), kind=kLoop, calls=%fused_computation.18 | loop fusion | flops 4325376 | bytes 5111808 | tf_op jit(solution)/shard_map/reduce_sum | solution.py:153
  112.3 14.9 %all_to_all.44 = bf16[4,96,2,3,128]{4,1,3,2,0:T(8,128)(2,1)S(1)} all-to-all(bf16[4,96,2,3,128]{4,1,3,2,0:T(8,128)(2,1)S(1)} %copy.50), channel_id=1, replica_groups=mesh['blk'=128,'frq'=4] {'frq'}, dimensions={0} | all-to-all | bytes 1179648 | tf_op jit(solution)/shard_map/all_to_all | solution.py:170
  128.0 3.0 %reduce.7 = bf16[128,1536]{1,0:T(8,128)(2,1)S(1)} reduce(bf16[128,1,1536]{2,1,0:T(2,128)(2,1)S(1)} %all_to_all.37, bf16[]{:T(256)} %broadcast.134), dimensions={1}, to_apply=%all_to_all.37.reduce_sub_computation | reduce | bytes 786434 | tf_op jit(solution)/shard_map/all_to_all | solution.py:177
  131.8 6.2 %all-to-all-start.4 = ((bf16[128,2,768]{2,1,0:T(2,128)(2,1)}), bf16[128,2,768]{2,1,0:T(2,128)(2,1)S(1)}, u32[]{:S(2)}, u32[]{:S(2)}) async-start(bf16[128,2,768]{2,1,0:T(2,128)(2,1)} %reshape.198), calls=%async_computation.4 | async-start | bytes 786432 | tf_op jit(solution)/shard_map/all_to_all | solution.py:177
  138.0 2.1 %cosine_multiply_fusion = (f32[128,1024]{0,1:T(8,128)S(1)}, f32[128,1024]{0,1:T(8,128)S(1)}) fusion(s32[128]{0:T(128)S(1)} %multiply_add_fusion.2), kind=kLoop, calls=%fused_computation.54 | loop fusion | flops 2228224 | bytes 1049088 | tf_op jit(solution)/shard_map/div | solution.py:197
  140.3 23.4 %all-to-all-done.4 = bf16[128,2,768]{2,1,0:T(2,128)(2,1)S(1)} async-done(((bf16[128,2,768]{2,1,0:T(2,128)(2,1)}), bf16[128,2,768]{2,1,0:T(2,128)(2,1)S(1)}, u32[]{:S(2)}, u32[]{:S(2)}) %all-to-all-start.4) | async-done | bytes 393248 | tf_op jit(solution)/shard_map/all_to_all | solution.py:177
  164.0 2.4 %reduce.2 = bf16[128,1536]{1,0:T(8,128)(2,1)S(1)} reduce(bf16[128,1,1536]{2,1,0:T(2,128)(2,1)S(1)} %reshape.199, bf16[]{:T(256)} %constant.70), dimensions={1}, to_apply=%all_to_all.34.reduce_sub_computation | reduce | bytes 786434 | tf_op jit(solution)/shard_map/all_to_all | solution.py:177
  166.8 1.1 convolution_multiply_fusion
  167.9 12.0 %all_to_all.45 = f32[4,256,3,16]{1,3,2,0:T(8,128)S(1)} all-to-all(f32[4,256,3,16]{1,3,2,0:T(8,128)S(1)} %convolution_multiply_fusion), channel_id=1, replica_groups=mesh['blk'=128,'frq'=4] {'frq'}, dimensions={0} | all-to-all | bytes 393216 | tf_op jit(solution)/shard_map/all_to_all | solution.py:206
  (72 shorter events, 15.2 us)
Async XLA Ops:
  1.4 35.6 %all-to-all-start = ((s32[128,1,2]{2,1,0:T(1,128)}), s32[128,1,2]{2,1,0:T(1,128)S(1)}, u32[]{:S(2)}, u32[]{:S(2)}) async-start(s32[128,1,2]{2,1,0:T(1,128)} %bitcast.5), calls=%async_computation | async-start | bytes 131072 | tf_op jit(solution)/shard_map/all_to_all | solution.py:73
  41.1 10.5 %copy-start.2 = (s32[1,128]{1,0:T(1,128)S(1)}, s32[1,128]{1,0:T(1,128)}, u32[]{:S(2)}) copy-start(s32[1,128]{1,0:T(1,128)} %param.9) | copy-start | bytes 1540
  44.2 11.8 %copy-start = (bf16[64,3,3,1024]{3,0,2,1:T(8,128)(2,1)S(1)}, bf16[64,3,3,1024]{3,0,2,1:T(8,128)(2,1)}, u32[]{:S(2)}) copy-start(bf16[64,3,3,1024]{3,0,2,1:T(8,128)(2,1)} %param.6) | copy-start | bytes 3538948
  45.1 30.2 %all-to-all-start.1 = ((bf16[128,2,768]{2,1,0:T(2,128)(2,1)}), bf16[128,2,768]{2,1,0:T(2,128)(2,1)S(1)}, u32[]{:S(2)}, u32[]{:S(2)}) async-start(bf16[128,2,768]{2,1,0:T(2,128)(2,1)} %reshape.196), calls=%async_computation.1 | async-start | bytes 786432 | tf_op jit(solution)/shard_map/all_to_all | solution.py:75
  78.8 10.3 %copy-start.1 = (s32[1,128,2]{1,2,0:T(2,128)S(1)}, s32[1,128,2]{1,2,0:T(2,128)}, u32[]{:S(2)}) copy-start(s32[1,128,2]{1,2,0:T(2,128)} %param.7) | copy-start | bytes 3076
  79.7 18.9 %all-to-all-start.2 = ((bf16[4,80,2,3,128]{4,1,3,2,0:T(8,128)(2,1)}), bf16[4,80,2,3,128]{4,1,3,2,0:T(8,128)(2,1)S(1)}, u32[]{:S(2)}, u32[]{:S(2)}) async-start(bf16[4,80,2,3,128]{4,1,3,2,0:T(8,128)(2,1)} %copy.43), calls=%async_computation.2 | async-start | bytes 983040 | tf_op jit(solution)/shard_map/all_to_all | solution.py:84
  131.8 31.9 %all-to-all-start.4 = ((bf16[128,2,768]{2,1,0:T(2,128)(2,1)}), bf16[128,2,768]{2,1,0:T(2,128)(2,1)S(1)}, u32[]{:S(2)}, u32[]{:S(2)}) async-start(bf16[128,2,768]{2,1,0:T(2,128)(2,1)} %reshape.198), calls=%async_computation.4 | async-start | bytes 786432 | tf_op jit(solution)/shard_map/all_to_all | solution.py:177
where the time goes:
time: 181 us
  waiting for transfers between devices  55.9 us (31%)
  starting transfers between devices  43.3 us (24%)
  other arithmetic  28.8 us (16%)
  blocking collectives  26.9 us (15%)
  local copies, waits for them, and re-layouts  18.2 us (10%)
  matrix products  6.92 us (4%)
    all_to_all x1, waiting for transfers between devices, local(): lax.all_to_all(far_band, 'blk', split_axis=0, concat_axis=0, tiled=True)  23.4 us
    all_to_all x1, starting transfers between devices, local(): lax.all_to_all(partner_local, 'blk', split_axis=0, concat_axis=0, tiled=T...  21.3 us
    all_to_all x1, waiting for transfers between devices, local(): lax.all_to_all(asked_rows.reshape(block_total, slot_cap * 2 * 3 * freq_de...  19 us
    all_to_all x1, blocking collectives, local(): lax.all_to_all(back_sent, 'frq', split_axis=0, concat_axis=0, tiled=True)  14.9 us
    all_to_all x1, waiting for transfers between devices, local(): lax.all_to_all(partner_local, 'blk', split_axis=0, concat_axis=0, tiled=T...  13.5 us
    all_to_all x1, blocking collectives, local(): lax.all_to_all(product.reshape(band_total, NT // band_total, 3, per_block...  12 us
    all_to_all x1, starting transfers between devices, local(): lax.all_to_all(sent, 'frq', split_axis=0, concat_axis=0, tiled=True)  9.46 us
    unnamed x17, local copies, waits for them, and re-layouts  6.39 us
  transfers between devices with their start and end apart: 4, of which 3 were waited for; matrix products, arithmetic and copies ran while one was open for 10% of the time, Pallas kernels for 0%

commit v1 on v0

--- a/solution.py
+++ b/solution.py
@@ -50,6 +50,15 @@
         adj_real * first_rows[:, 1, :, None] - adj_imag * first_rows[:, 0, :, None], axis=1
     )
     return (jnp.stack([own_real, own_imag], axis=1), jnp.stack([far_real, far_imag], axis=1))
+
+
+def blk_exchange(chunks):
+    count, width = chunks.shape
+    tile = 16 * 128
+    padded = -(-width // tile) * tile
+    wide = jnp.pad(chunks, ((0, 0), (0, padded - width))).reshape(count, padded // 128, 128)
+    moved = lax.all_to_all(wide, "blk", split_axis=0, concat_axis=0, tiled=True)
+    return moved.reshape(count, padded)[:, :width]
 
 
 def local(spectra, observed, own_station, partner_station, pair_count):
@@ -72,13 +81,9 @@
     )
     asked_ids = lax.all_to_all(partner_local, "blk", split_axis=0, concat_axis=0, tiled=True)
     asked_rows = jnp.take(spec_rows, asked_ids.reshape(slot_total), axis=0, mode="clip")
-    rows_new = lax.all_to_all(
-        asked_rows.reshape(block_total, slot_cap * 2 * 3 * freq_dev),
-        "blk",
-        split_axis=0,
-        concat_axis=0,
-        tiled=True,
-    ).reshape(band_total, item_count, 2, 3, freq_dev)
+    rows_new = blk_exchange(asked_rows.reshape(block_total, -1)).reshape(
+        band_total, item_count, 2, 3, freq_dev
+    )
     own_table = jnp.broadcast_to(spec_rows[None], (band_total, per_block, 2, 3, freq_dev))
     sent = jnp.concatenate([rows_new, own_table], axis=1)
     whole_band = lax.all_to_all(sent, "frq", split_axis=0, concat_axis=0, tiled=True)
@@ -174,9 +179,7 @@
         + band_back[:, item_count + per_block :].astype(jnp.float32),
         axis=0,
     ).reshape(per_block, 6 * freq_dev)
-    back_grad = lax.all_to_all(far_band, "blk", split_axis=0, concat_axis=0, tiled=True).astype(
-        jnp.float32
-    )
+    back_grad = blk_exchange(far_band).astype(jnp.float32)
     back_onehot = (asked_ids.reshape(slot_total)[None, :] == station_iota[:, None]).astype(
         jnp.float32
     )

time: 181 us -> 180 us (level)
  waiting for transfers between devices: 55.9 us -> 67.5 us
  other arithmetic: 28.8 us -> 17.9 us
    all_to_all x2, waiting for transfers between devices: 42.4 us -> 54.1 us  [blk_exchange(): moved = lax.all_to_all(wide, 'blk', split_axis=0, concat_axis=0, tiled=True)]
    all_to_all x4 -> x0, other arithmetic: 10.9 us -> none  [the longest x2 5.57 us: local(): lax.all_to_all(asked_rows.reshape(block_total, slot_cap * 2 * 3 * freq_de...]
    unnamed x17 -> x19, local copies, waits for them, and re-layouts: 6.39 us -> 6.27 us
where the time goes in v1:
time: 180 us
  waiting for transfers between devices  67.5 us (38%)
  starting transfers between devices  42.4 us (24%)
  blocking collectives  27.2 us (15%)
  other arithmetic  17.9 us (10%)
  local copies, waits for them, and re-layouts  17.5 us (10%)
  matrix products  6.91 us (4%)
    all_to_all x2, waiting for transfers between devices, blk_exchange(): moved = lax.all_to_all(wide, 'blk', split_axis=0, concat_axis=0, tiled=True)  54.1 us
    all_to_all x1, starting transfers between devices, local(): lax.all_to_all(partner_local, 'blk', split_axis=0, concat_axis=0, tiled=T...  21.3 us
    all_to_all x1, blocking collectives, local(): lax.all_to_all(back_sent, 'frq', split_axis=0, concat_axis=0, tiled=True)  14.9 us
    all_to_all x1, waiting for transfers between devices, local(): lax.all_to_all(partner_local, 'blk', split_axis=0, concat_axis=0, tiled=T...  13.5 us
    all_to_all x2, starting transfers between devices, blk_exchange(): moved = lax.all_to_all(wide, 'blk', split_axis=0, concat_axis=0, tiled=True)  12.5 us
    all_to_all x1, blocking collectives, local(): lax.all_to_all(product.reshape(band_total, NT // band_total, 3, per_block...  12.3 us
    all_to_all x1, starting transfers between devices, local(): lax.all_to_all(sent, 'frq', split_axis=0, concat_axis=0, tiled=True)  8.48 us
    unnamed x19, local copies, waits for them, and re-layouts  6.27 us
  transfers between devices with their start and end apart: 4, of which 3 were waited for; matrix products, arithmetic and copies ran while one was open for 10% of the time, Pallas kernels for 0%

profile of v1, /device:TPU:1, one launch (start us, length us, event | category | flops | bytes accessed | tf_op | source)
XLA Modules:
  0.0 179.9 jit_solution(11419786024489589427)
XLA Ops:
  0.0 1.4 copy.39
  1.4 21.3 %all-to-all-start = ((s32[128,1,2]{2,1,0:T(1,128)}), s32[128,1,2]{2,1,0:T(1,128)S(1)}, u32[]{:S(2)}, u32[]{:S(2)}) async-start(s32[128,1,2]{2,1,0:T(1,128)} %bitcast.5), calls=%async_computation | async-start | bytes 131072 | tf_op jit(solution)/shard_map/all_to_all | solution.py:82
  23.5 13.5 %all-to-all-done = s32[128,1,2]{2,1,0:T(1,128)S(1)} async-done(((s32[128,1,2]{2,1,0:T(1,128)}), s32[128,1,2]{2,1,0:T(1,128)S(1)}, u32[]{:S(2)}, u32[]{:S(2)}) %all-to-all-start) | async-done | bytes 1056 | tf_op jit(solution)/shard_map/all_to_all | solution.py:82
  38.5 1.5 gather_fusion
  40.6 0.9 copy.61
  41.5 6.2 %all-to-all-start.1 = ((bf16[128,16,128]{2,1,0:T(8,128)(2,1)}), bf16[128,16,128]{2,1,0:T(8,128)(2,1)S(1)}, u32[]{:S(2)}, u32[]{:S(2)}) async-start(bf16[128,16,128]{2,1,0:T(8,128)(2,1)} %bitcast.41), calls=%async_computation.1 | async-start | bytes 1048576 | tf_op jit(solution)/shard_map/all_to_all | solution.py:60
  47.9 4.3 %fusion.30 = bf16[512,448]{1,0:T(8,128)(2,1)S(1)} fusion(s32[448]{0:T(512)S(1)} %pad_add_fusion, s32[512]{0:T(512)S(1)} %multiply_add_fusion.1), kind=kLoop, calls=%fused_computation.52 | loop fusion | flops 4358144 | bytes 462592 | tf_op jit(solution)/shard_map/neg | solution.py:127
  52.5 25.5 %all-to-all-done.1 = bf16[128,16,128]{2,1,0:T(8,128)(2,1)S(1)} async-done(((bf16[128,16,128]{2,1,0:T(8,128)(2,1)}), bf16[128,16,128]{2,1,0:T(8,128)(2,1)S(1)}, u32[]{:S(2)}, u32[]{:S(2)}) %all-to-all-start.1) | async-done | bytes 524320 | tf_op jit(solution)/shard_map/all_to_all | solution.py:60
  79.8 8.5 %all-to-all-start.2 = ((bf16[4,80,2,3,128]{4,1,3,2,0:T(8,128)(2,1)}), bf16[4,80,2,3,128]{4,1,3,2,0:T(8,128)(2,1)S(1)}, u32[]{:S(2)}, u32[]{:S(2)}) async-start(bf16[4,80,2,3,128]{4,1,3,2,0:T(8,128)(2,1)} %copy.42), calls=%async_computation.2 | async-start | bytes 983040 | tf_op jit(solution)/shard_map/all_to_all | solution.py:89
  89.0 0.9 copy.59
  89.9 0.9 copy.60
  90.8 2.1 %gather_fusion.2 = f32[448]{0:T(512)S(1)} fusion(f32[1024]{0:T(1024)S(1)} %fusion.43, s32[1024]{0:T(1024)S(1)} %pad_clamp_fusion), kind=kCustom, calls=%fused_computation.2 | custom fusion | bytes 5376 | tf_op jit(solution)/shard_map/gather | solution.py:131
  92.9 4.9 %multiply_convert_fusion.1 = bf16[512,448]{1,0:T(8,128)(2,1)} fusion(s32[448]{0:T(512)S(1)} %pad_add_fusion, s32[512]{0:T(512)S(1)} %multiply_add_fusion.1), kind=kLoop, calls=%fused_computation.33 | loop fusion | flops 3670016 | bytes 462592 | tf_op jit(solution)/shard_map/convert_element_type | solution.py:126
  98.6 1.4 gather_fusion.1
  101.6 1.4 multiply_add_fusion
  103.0 5.3 %convolution_reduce-precision_fusion = f32[576,1024]{1,0:T(8,128)} fusion(f32[576,512]{1,0:T(8,128)} %bitcast.99, f32[576,512]{1,0:T(8,128)S(1)} %bitcast.98, f32[576]{0:T(1024)S(1)} %mul.232, bf16[512,448]{1,0:T(8,128)(2,1)S(1)} %fusion.30, bf16[512,448]{1,0:T(8,128)(2,1)} %multiply_convert_fusion.1, bf16[576,224]{0,1:T(8,128)(2,1)} %copy.60, ...), kind=kOutput, calls=%fused_computation.8 | convolution fusion | flops 1065058304 | bytes 6158592 | tf_op jit(solution)/shard_map/dot_general | solution.py:148
  108.3 2.4 %add_reduce_fusion.1 = (bf16[3,64,512]{2,1,0:T(8,128)(2,1)S(1)}, bf16[3,64,512]{2,1,0:T(8,128)(2,1)S(1)}, f32[3,64,512]{2,1,0:T(8,128)S(1)}, f32[3,64,512]{2,1,0:T(8,128)S(1)}) fusion(f32[3,3,64,1024]{3,2,1,0:T(8,128)} %bitcast.89, f32[3,64,512]{2,1,0:T(8,128)S(1)} %get-tuple-element.25, f32[3,64,512]{2,1,0:T(8,128)S(1)} %get-tuple-element.26, ...), kind=kLoop, calls=%fused_computation.18 | loop fusion | flops 4325376 | bytes 5111808 | tf_op jit(solution)/shard_map/reduce_sum | solution.py:158
  111.4 14.9 %all_to_all.34 = bf16[4,96,2,3,128]{4,1,3,2,0:T(8,128)(2,1)S(1)} all-to-all(bf16[4,96,2,3,128]{4,1,3,2,0:T(8,128)(2,1)S(1)} %copy.49), channel_id=1, replica_groups=mesh['blk'=128,'frq'=4] {'frq'}, dimensions={0} | all-to-all | bytes 1179648 | tf_op jit(solution)/shard_map/all_to_all | solution.py:175
  127.1 0.9 copy.63
  128.0 6.4 %all-to-all-start.4 = ((bf16[128,16,128]{2,1,0:T(8,128)(2,1)}), bf16[128,16,128]{2,1,0:T(8,128)(2,1)S(1)}, u32[]{:S(2)}, u32[]{:S(2)}) async-start(bf16[128,16,128]{2,1,0:T(8,128)(2,1)} %bitcast.48), calls=%async_computation.4 | async-start | bytes 1048576 | tf_op jit(solution)/shard_map/all_to_all | solution.py:60
  134.4 2.1 %cosine_multiply_fusion = (f32[128,1024]{0,1:T(8,128)S(1)}, f32[128,1024]{0,1:T(8,128)S(1)}) fusion(s32[128]{0:T(128)S(1)} %multiply_add_fusion.2), kind=kLoop, calls=%fused_computation.58 | loop fusion | flops 2228224 | bytes 1049088 | tf_op jit(solution)/shard_map/div | solution.py:200
  136.7 28.5 %all-to-all-done.4 = bf16[128,16,128]{2,1,0:T(8,128)(2,1)S(1)} async-done(((bf16[128,16,128]{2,1,0:T(8,128)(2,1)}), bf16[128,16,128]{2,1,0:T(8,128)(2,1)S(1)}, u32[]{:S(2)}, u32[]{:S(2)}) %all-to-all-start.4) | async-done | bytes 524320 | tf_op jit(solution)/shard_map/all_to_all | solution.py:60
  165.8 1.1 convolution_multiply_fusion
  166.9 12.3 %all_to_all.35 = f32[4,256,3,16]{1,3,2,0:T(8,128)S(1)} all-to-all(f32[4,256,3,16]{1,3,2,0:T(8,128)S(1)} %convolution_multiply_fusion), channel_id=1, replica_groups=mesh['blk'=128,'frq'=4] {'frq'}, dimensions={0} | all-to-all | bytes 393216 | tf_op jit(solution)/shard_map/all_to_all | solution.py:209
  (71 shorter events, 11.0 us)
Async XLA Ops:
  1.4 35.6 %all-to-all-start = ((s32[128,1,2]{2,1,0:T(1,128)}), s32[128,1,2]{2,1,0:T(1,128)S(1)}, u32[]{:S(2)}, u32[]{:S(2)}) async-start(s32[128,1,2]{2,1,0:T(1,128)} %bitcast.5), calls=%async_computation | async-start | bytes 131072 | tf_op jit(solution)/shard_map/all_to_all | solution.py:82
  40.6 7.3 %copy-start.2 = (s32[1,128]{1,0:T(1,128)S(1)}, s32[1,128]{1,0:T(1,128)}, u32[]{:S(2)}) copy-start(s32[1,128]{1,0:T(1,128)} %param.9) | copy-start | bytes 1540
  40.6 11.7 %copy-start = (bf16[64,3,3,1024]{3,0,2,1:T(8,128)(2,1)S(1)}, bf16[64,3,3,1024]{3,0,2,1:T(8,128)(2,1)}, u32[]{:S(2)}) copy-start(bf16[64,3,3,1024]{3,0,2,1:T(8,128)(2,1)} %param.6) | copy-start | bytes 3538948
  41.5 36.5 %all-to-all-start.1 = ((bf16[128,16,128]{2,1,0:T(8,128)(2,1)}), bf16[128,16,128]{2,1,0:T(8,128)(2,1)S(1)}, u32[]{:S(2)}, u32[]{:S(2)}) async-start(bf16[128,16,128]{2,1,0:T(8,128)(2,1)} %bitcast.41), calls=%async_computation.1 | async-start | bytes 1048576 | tf_op jit(solution)/shard_map/all_to_all | solution.py:60
  79.0 9.4 %copy-start.1 = (s32[1,128,2]{1,2,0:T(2,128)S(1)}, s32[1,128,2]{1,2,0:T(2,128)}, u32[]{:S(2)}) copy-start(s32[1,128,2]{1,2,0:T(2,128)} %param.7) | copy-start | bytes 3076
  79.8 17.9 %all-to-all-start.2 = ((bf16[4,80,2,3,128]{4,1,3,2,0:T(8,128)(2,1)}), bf16[4,80,2,3,128]{4,1,3,2,0:T(8,128)(2,1)S(1)}, u32[]{:S(2)}, u32[]{:S(2)}) async-start(bf16[4,80,2,3,128]{4,1,3,2,0:T(8,128)(2,1)} %copy.42), calls=%async_computation.2 | async-start | bytes 983040 | tf_op jit(solution)/shard_map/all_to_all | solution.py:89
  128.0 37.2 %all-to-all-start.4 = ((bf16[128,16,128]{2,1,0:T(8,128)(2,1)}), bf16[128,16,128]{2,1,0:T(8,128)(2,1)S(1)}, u32[]{:S(2)}, u32[]{:S(2)}) async-start(bf16[128,16,128]{2,1,0:T(8,128)(2,1)} %bitcast.48), calls=%async_computation.4 | async-start | bytes 1048576 | tf_op jit(solution)/shard_map/all_to_all | solution.py:60

commit v2 on v1

--- a/solution.py
+++ b/solution.py
@@ -165,25 +165,29 @@
         precision=lax.Precision.HIGHEST,
         preferred_element_type=jnp.float32,
     )
-    grad_high = lax.reduce_precision(grad_group, exponent_bits=8, mantissa_bits=7)
-    grad_low = (grad_group - grad_high).astype(jnp.bfloat16)
+    output_scale = 1.0 / math.sqrt(2.0 * block_total * slot_cap / per_block)
+    phase_full = phase_table(0, NF, NT)
+    cos_full = jnp.cos(phase_full) / math.sqrt(NF)
+    sin_full = jnp.sin(phase_full) / math.sqrt(NF)
+    own_matrix = jnp.transpose(grad_group, (1, 3, 2, 0)).reshape(2 * NF, 3 * per_block)
+    product_own = lax.dot_general(
+        jnp.concatenate([cos_full, -sin_full], axis=0),
+        own_matrix,
+        (((0,), (0,)), ((), ())),
+        precision=lax.Precision.HIGHEST,
+        preferred_element_type=jnp.float32,
+    )
     far_grad = jnp.transpose(jnp.stack([far_re, far_im]), (2, 0, 1, 3)).astype(jnp.bfloat16)
-    back_sent = jnp.concatenate([far_grad, grad_high.astype(jnp.bfloat16), grad_low], axis=0)
     back_sent = jnp.transpose(
-        back_sent.reshape(item_count + 2 * per_block, 2, 3, band_total, freq_dev), (3, 0, 1, 2, 4)
+        far_grad.reshape(item_count, 2, 3, band_total, freq_dev), (3, 0, 1, 2, 4)
     )
     band_back = lax.all_to_all(back_sent, "frq", split_axis=0, concat_axis=0, tiled=True)
-    far_band = band_back[:, :item_count].reshape(block_total, slot_cap * 2 * 3 * freq_dev)
-    grad_local = jnp.sum(
-        band_back[:, item_count : item_count + per_block].astype(jnp.float32)
-        + band_back[:, item_count + per_block :].astype(jnp.float32),
-        axis=0,
-    ).reshape(per_block, 6 * freq_dev)
+    far_band = band_back.reshape(block_total, slot_cap * 2 * 3 * freq_dev)
     back_grad = blk_exchange(far_band).astype(jnp.float32)
     back_onehot = (asked_ids.reshape(slot_total)[None, :] == station_iota[:, None]).astype(
         jnp.float32
     )
-    station_grad = grad_local + jnp.dot(
+    station_grad = jnp.dot(
         back_onehot,
         back_grad.reshape(slot_total, 6 * freq_dev),
         precision=lax.Precision.HIGHEST,
@@ -192,14 +196,14 @@
     grad_matrix = jnp.transpose(
         station_grad.reshape(per_block, 2, 3, freq_dev), (1, 3, 2, 0)
     ).reshape(2 * freq_dev, 3 * per_block)
-    output_scale = 1.0 / math.sqrt(2.0 * block_total * slot_cap / per_block)
-    phase_part = phase_table(
-        band_index * freq_dev, freq_dev, NT // band_total * lax.axis_size("frq")
-    )
     basis_part = jnp.concatenate(
-        [jnp.cos(phase_part) / math.sqrt(NF), -(jnp.sin(phase_part) / math.sqrt(NF))], axis=0
-    )
-    product = lax.dot_general(
+        [
+            lax.dynamic_slice_in_dim(cos_full, band_index * freq_dev, freq_dev),
+            -lax.dynamic_slice_in_dim(sin_full, band_index * freq_dev, freq_dev),
+        ],
+        axis=0,
+    )
+    product = product_own + lax.dot_general(
         basis_part,
         grad_matrix,
         (((0,), (0,)), ((), ())),

time: 180 us -> 185 us (1.028)
  waiting for transfers between devices: 67.5 us -> 56.5 us
  other arithmetic: 17.9 us -> 26.9 us
  matrix products: 6.91 us -> 11.1 us
  local copies, waits for them, and re-layouts: 17.5 us -> 21.5 us
  blocking collectives: 27.2 us -> 24.7 us
    all_to_all x2, waiting for transfers between devices: 54.1 us -> 42.7 us  [blk_exchange(): moved = lax.all_to_all(wide, 'blk', split_axis=0, concat_axis=0, tiled=True)]
    neg x0 -> x2, other arithmetic: none -> 9.88 us  [the longest x1 9.8 us: local(): -sin_full]
    dot_general x0 -> x1, matrix products: none -> 4.28 us  [local(): lax.dot_general(jnp.concatenate([cos_full, -sin_full], axis=0), own_matri...]
    all_to_all x1, blocking collectives: 14.9 us -> 12.2 us  [local(): lax.all_to_all(back_sent, 'frq', split_axis=0, concat_axis=0, tiled=True)]
    div x1 -> x0, other arithmetic: 2.09 us -> none  [local(): jnp.cos(phase_part) / math.sqrt(NF)]
    unnamed x19 -> x23, local copies, waits for them, and re-layouts: 6.27 us -> 8.29 us
  transfers between devices with their start and end apart: 4 -> 4, of which waited for: 3 -> 4; matrix products, arithmetic and copies ran while one was open for 10% -> 14% of each run, Pallas kernels for 0% -> 0%
where the time goes in v2:
time: 185 us
  waiting for transfers between devices  56.5 us (31%)
  starting transfers between devices  43.6 us (24%)
  other arithmetic  26.9 us (15%)
  blocking collectives  24.7 us (13%)
  local copies, waits for them, and re-layouts  21.5 us (12%)
  matrix products  11.1 us (6%)
    all_to_all x2, waiting for transfers between devices, blk_exchange(): moved = lax.all_to_all(wide, 'blk', split_axis=0, concat_axis=0, tiled=True)  42.7 us
    all_to_all x1, starting transfers between devices, local(): lax.all_to_all(partner_local, 'blk', split_axis=0, concat_axis=0, tiled=T...  21.3 us
    all_to_all x2, starting transfers between devices, blk_exchange(): moved = lax.all_to_all(wide, 'blk', split_axis=0, concat_axis=0, tiled=True)  13.7 us
    all_to_all x1, waiting for transfers between devices, local(): lax.all_to_all(partner_local, 'blk', split_axis=0, concat_axis=0, tiled=T...  13.5 us
    all_to_all x1, blocking collectives, local(): lax.all_to_all(product.reshape(band_total, NT // band_total, 3, per_block...  12.5 us
    all_to_all x1, blocking collectives, local(): lax.all_to_all(back_sent, 'frq', split_axis=0, concat_axis=0, tiled=True)  12.2 us
    neg x1, other arithmetic, local(): -sin_full  9.8 us
    all_to_all x1, starting transfers between devices, local(): lax.all_to_all(sent, 'frq', split_axis=0, concat_axis=0, tiled=True)  8.57 us
  transfers between devices with their start and end apart: 4, of which 4 were waited for; matrix products, arithmetic and copies ran while one was open for 14% of the time, Pallas kernels for 0%

profile of v2, /device:TPU:1, one launch (start us, length us, event | category | flops | bytes accessed | tf_op | source)
XLA Modules:
  0.0 184.6 jit_solution(2073125909418871316)
XLA Ops:
  0.0 1.4 copy.46
  1.4 21.3 %all-to-all-start = ((s32[128,1,2]{2,1,0:T(1,128)}), s32[128,1,2]{2,1,0:T(1,128)S(1)}, u32[]{:S(2)}, u32[]{:S(2)}) async-start(s32[128,1,2]{2,1,0:T(1,128)} %bitcast.3), calls=%async_computation | async-start | bytes 131072 | tf_op jit(solution)/shard_map/all_to_all | solution.py:82
  23.5 13.5 %all-to-all-done = s32[128,1,2]{2,1,0:T(1,128)S(1)} async-done(((s32[128,1,2]{2,1,0:T(1,128)}), s32[128,1,2]{2,1,0:T(1,128)S(1)}, u32[]{:S(2)}, u32[]{:S(2)}) %all-to-all-start) | async-done | bytes 1056 | tf_op jit(solution)/shard_map/all_to_all | solution.py:82
  38.5 1.5 gather_fusion
  41.5 6.2 %all-to-all-start.1 = ((bf16[128,16,128]{2,1,0:T(8,128)(2,1)}), bf16[128,16,128]{2,1,0:T(8,128)(2,1)S(1)}, u32[]{:S(2)}, u32[]{:S(2)}) async-start(bf16[128,16,128]{2,1,0:T(8,128)(2,1)} %bitcast.35), calls=%async_computation.1 | async-start | bytes 1048576 | tf_op jit(solution)/shard_map/all_to_all | solution.py:60
  48.0 4.9 %fusion.47 = bf16[512,448]{1,0:T(8,128)(2,1)} fusion(s32[448]{0:T(512)S(1)} %pad_add_fusion, s32[512]{0:T(512)S(1)} %multiply_add_fusion.1), kind=kLoop, calls=%fused_computation.65 | loop fusion | flops 4358144 | bytes 462592 | tf_op jit(solution)/shard_map/neg | solution.py:127
  53.2 24.8 %all-to-all-done.1 = bf16[128,16,128]{2,1,0:T(8,128)(2,1)S(1)} async-done(((bf16[128,16,128]{2,1,0:T(8,128)(2,1)}), bf16[128,16,128]{2,1,0:T(8,128)(2,1)S(1)}, u32[]{:S(2)}, u32[]{:S(2)}) %all-to-all-start.1) | async-done | bytes 524320 | tf_op jit(solution)/shard_map/all_to_all | solution.py:60
  79.7 8.6 %all-to-all-start.2 = ((bf16[4,80,2,3,128]{4,1,3,2,0:T(8,128)(2,1)}), bf16[4,80,2,3,128]{4,1,3,2,0:T(8,128)(2,1)S(1)}, u32[]{:S(2)}, u32[]{:S(2)}) async-start(bf16[4,80,2,3,128]{4,1,3,2,0:T(8,128)(2,1)} %copy.49), calls=%async_computation.2 | async-start | bytes 983040 | tf_op jit(solution)/shard_map/all_to_all | solution.py:89
  90.1 2.1 %gather_fusion.2 = f32[448]{0:T(512)S(1)} fusion(f32[1024]{0:T(1024)S(1)} %fusion.60, s32[1024]{0:T(1024)S(1)} %pad_clamp_fusion), kind=kCustom, calls=%fused_computation.2 | custom fusion | bytes 5376 | tf_op jit(solution)/shard_map/gather | solution.py:131
  92.2 4.9 %multiply_convert_fusion.1 = bf16[512,448]{1,0:T(8,128)(2,1)} fusion(s32[448]{0:T(512)S(1)} %pad_add_fusion, s32[512]{0:T(512)S(1)} %multiply_add_fusion.1), kind=kLoop, calls=%fused_computation.53 | loop fusion | flops 3670016 | bytes 462592 | tf_op jit(solution)/shard_map/convert_element_type | solution.py:126
  98.9 1.4 gather_fusion.1
  101.3 1.4 multiply_add_fusion
  102.7 5.4 %convolution_reduce-precision_fusion = f32[576,1024]{1,0:T(8,128)} fusion(f32[576,512]{1,0:T(8,128)} %bitcast.101, f32[576,512]{1,0:T(8,128)S(1)} %bitcast.100, f32[576]{0:T(1024)S(1)} %mul.254, bf16[512,448]{1,0:T(8,128)(2,1)} %fusion.47, bf16[512,448]{1,0:T(8,128)(2,1)} %multiply_convert_fusion.1, bf16[576,224]{0,1:T(8,128)(2,1)S(1)} %copy-done.2, ...), kind=kOutput, calls=%fused_computation.23 | convolution fusion | flops 1065058304 | bytes 6158592 | tf_op jit(solution)/shard_map/dot_general | solution.py:148
  108.1 3.1 %subtract_reduce_fusion.1 = (f32[3,64,512]{2,1,0:T(8,128)S(1)}, f32[3,64,512]{2,1,0:T(8,128)}, bf16[3,64,512]{2,1,0:T(8,128)(2,1)S(1)}, bf16[3,64,512]{2,1,0:T(8,128)(2,1)S(1)}) fusion(f32[3,3,64,1024]{3,2,1,0:T(8,128)} %bitcast.90, f32[3,64,512]{2,1,0:T(8,128)S(1)} %get-tuple-element.24, f32[3,64,512]{2,1,0:T(8,128)S(1)} %get-tuple-element.25, ...), kind=kLoop, calls=%fused_computation.33 | loop fusion | flops 4325376 | bytes 5111808 | tf_op jit(solution)/shard_map/reduce_sum | solution.py:156
  111.4 12.2 %all_to_all.34 = bf16[4,64,2,3,128]{4,1,3,2,0:T(8,128)(2,1)S(1)} all-to-all(bf16[4,64,2,3,128]{4,1,3,2,0:T(8,128)(2,1)S(1)} %copy.56), channel_id=1, replica_groups=mesh['blk'=128,'frq'=4] {'frq'}, dimensions={0} | all-to-all | bytes 786432 | tf_op jit(solution)/shard_map/all_to_all | solution.py:184
  124.3 0.9 copy.70
  125.2 7.5 %all-to-all-start.4 = ((bf16[128,16,128]{2,1,0:T(8,128)(2,1)}), bf16[128,16,128]{2,1,0:T(8,128)(2,1)}, u32[]{:S(2)}, u32[]{:S(2)}) async-start(bf16[128,16,128]{2,1,0:T(8,128)(2,1)} %bitcast.47), calls=%async_computation.4 | async-start | bytes 1048576 | tf_op jit(solution)/shard_map/all_to_all | solution.py:60
  132.8 9.8 %fusion.38 = (f32[512,1024]{1,0:T(8,128)}, f32[512,1024]{1,0:T(8,128)S(1)}, f32[512,1024]{1,0:T(8,128)S(1)}) fusion(s32[512]{0:T(512)S(1)} %multiply_add_fusion.1), kind=kLoop, calls=%fused_computation.54 | loop fusion | flops 8912896 | bytes 6293504 | tf_op jit(solution)/shard_map/neg | solution.py:174
  142.7 0.9 copy-done
  144.8 17.9 %all-to-all-done.4 = bf16[128,16,128]{2,1,0:T(8,128)(2,1)} async-done(((bf16[128,16,128]{2,1,0:T(8,128)(2,1)}), bf16[128,16,128]{2,1,0:T(8,128)(2,1)}, u32[]{:S(2)}, u32[]{:S(2)}) %all-to-all-start.4) | async-done | bytes 524320 | tf_op jit(solution)/shard_map/all_to_all | solution.py:60
  162.7 1.2 copy.84
  164.8 1.2 copy.58
  167.0 4.3 %fusion.19 = f32[1024,48]{0,1:T(8,128)S(1)} fusion(f32[1024,48]{0,1:T(8,128)S(1)} %fusion.34, f32[1024,48]{0,1:T(8,128)} %bitcast.102, f32[512,1024]{1,0:T(8,128)} %get-tuple-element.19, f32[512,1024]{1,0:T(8,128)S(1)} %get-tuple-element.21), kind=kOutput, calls=%fused_computation.38 | convolution fusion | flops 605126656 | bytes 4784128 | tf_op jit(solution)/shard_map/dot_general | solution.py:173
  171.5 12.5 %all_to_all.35 = f32[4,256,3,16]{1,3,2,0:T(8,128)S(1)} all-to-all(f32[4,256,3,16]{1,3,2,0:T(8,128)S(1)} %copy.60), channel_id=1, replica_groups=mesh['blk'=128,'frq'=4] {'frq'}, dimensions={0} | all-to-all | bytes 393216 | tf_op jit(solution)/shard_map/all_to_all | solution.py:213
  (73 shorter events, 15.5 us)
Async XLA Ops:
  1.4 35.6 %all-to-all-start = ((s32[128,1,2]{2,1,0:T(1,128)}), s32[128,1,2]{2,1,0:T(1,128)S(1)}, u32[]{:S(2)}, u32[]{:S(2)}) async-start(s32[128,1,2]{2,1,0:T(1,128)} %bitcast.3), calls=%async_computation | async-start | bytes 131072 | tf_op jit(solution)/shard_map/all_to_all | solution.py:82
  40.1 7.7 %copy-start.4 = (s32[1,128]{1,0:T(1,128)S(1)}, s32[1,128]{1,0:T(1,128)}, u32[]{:S(2)}) copy-start(s32[1,128]{1,0:T(1,128)} %param.9) | copy-start | bytes 1540
  40.2 12.7 %copy-start.1 = (bf16[64,3,3,1024]{3,0,2,1:T(8,128)(2,1)S(1)}, bf16[64,3,3,1024]{3,0,2,1:T(8,128)(2,1)}, u32[]{:S(2)}) copy-start(bf16[64,3,3,1024]{3,0,2,1:T(8,128)(2,1)} %param.6) | copy-start | bytes 3538948
  41.5 36.5 %all-to-all-start.1 = ((bf16[128,16,128]{2,1,0:T(8,128)(2,1)}), bf16[128,16,128]{2,1,0:T(8,128)(2,1)S(1)}, u32[]{:S(2)}, u32[]{:S(2)}) async-start(bf16[128,16,128]{2,1,0:T(8,128)(2,1)} %bitcast.35), calls=%async_computation.1 | async-start | bytes 1048576 | tf_op jit(solution)/shard_map/all_to_all | solution.py:60
  78.1 10.2 %copy-start.3 = (s32[1,128,2]{1,2,0:T(2,128)S(1)}, s32[1,128,2]{1,2,0:T(2,128)}, u32[]{:S(2)}) copy-start(s32[1,128,2]{1,2,0:T(2,128)} %param.7) | copy-start | bytes 3076
  79.7 17.7 %all-to-all-start.2 = ((bf16[4,80,2,3,128]{4,1,3,2,0:T(8,128)(2,1)}), bf16[4,80,2,3,128]{4,1,3,2,0:T(8,128)(2,1)S(1)}, u32[]{:S(2)}, u32[]{:S(2)}) async-start(bf16[4,80,2,3,128]{4,1,3,2,0:T(8,128)(2,1)} %copy.49), calls=%async_computation.2 | async-start | bytes 983040 | tf_op jit(solution)/shard_map/all_to_all | solution.py:89
  101.3 1.4 copy-start.2
  125.2 37.5 %all-to-all-start.4 = ((bf16[128,16,128]{2,1,0:T(8,128)(2,1)}), bf16[128,16,128]{2,1,0:T(8,128)(2,1)}, u32[]{:S(2)}, u32[]{:S(2)}) async-start(bf16[128,16,128]{2,1,0:T(8,128)(2,1)} %bitcast.47), calls=%async_computation.4 | async-start | bytes 1048576 | tf_op jit(solution)/shard_map/all_to_all | solution.py:60
  142.6 1.0 copy-start

commit v3 on v2

--- a/solution.py
+++ b/solution.py
@@ -177,6 +177,7 @@
         precision=lax.Precision.HIGHEST,
         preferred_element_type=jnp.float32,
     )
+    product_own = lax.optimization_barrier(product_own)
     far_grad = jnp.transpose(jnp.stack([far_re, far_im]), (2, 0, 1, 3)).astype(jnp.bfloat16)
     back_sent = jnp.transpose(
         far_grad.reshape(item_count, 2, 3, band_total, freq_dev), (3, 0, 1, 2, 4)

time: 185 us -> 178 us (0.962)
  local copies, waits for them, and re-layouts: 21.5 us -> 19.5 us
  other arithmetic: 26.9 us -> 25 us
    neg x1 -> x0, other arithmetic: 9.8 us -> none  [local(): -sin_full]
    div x0 -> x1, other arithmetic: none -> 8.6 us  [local(): sin_full = jnp.sin(phase_full) / math.sqrt(NF)]
    unnamed x23 -> x27, local copies, waits for them, and re-layouts: 8.29 us -> 6.91 us
  transfers between devices with their start and end apart: 4 -> 4, of which waited for: 4 -> 3; matrix products, arithmetic and copies ran while one was open for 14% -> 16% of each run, Pallas kernels for 0% -> 0%
where the time goes in v3:
time: 178 us
  waiting for transfers between devices  55.8 us (31%)
  starting transfers between devices  42.5 us (24%)
  blocking collectives  25.3 us (14%)
  other arithmetic  25 us (14%)
  local copies, waits for them, and re-layouts  19.5 us (11%)
  matrix products  9.35 us (5%)
    all_to_all x2, waiting for transfers between devices, blk_exchange(): moved = lax.all_to_all(wide, 'blk', split_axis=0, concat_axis=0, tiled=True)  42.3 us
    all_to_all x1, starting transfers between devices, local(): lax.all_to_all(partner_local, 'blk', split_axis=0, concat_axis=0, tiled=T...  21.3 us
    all_to_all x1, waiting for transfers between devices, local(): lax.all_to_all(partner_local, 'blk', split_axis=0, concat_axis=0, tiled=T...  13.5 us
    all_to_all x1, blocking collectives, local(): lax.all_to_all(product.reshape(band_total, NT // band_total, 3, per_block...  12.8 us
    all_to_all x2, starting transfers between devices, blk_exchange(): moved = lax.all_to_all(wide, 'blk', split_axis=0, concat_axis=0, tiled=True)  12.5 us
    all_to_all x1, blocking collectives, local(): lax.all_to_all(back_sent, 'frq', split_axis=0, concat_axis=0, tiled=True)  12.5 us
    all_to_all x1, starting transfers between devices, local(): lax.all_to_all(sent, 'frq', split_axis=0, concat_axis=0, tiled=True)  8.61 us
    div x1, other arithmetic, local(): sin_full = jnp.sin(phase_full) / math.sqrt(NF)  8.6 us
  transfers between devices with their start and end apart: 4, of which 3 were waited for; matrix products, arithmetic and copies ran while one was open for 16% of the time, Pallas kernels for 0%

profile of v3, /device:TPU:1, one launch (start us, length us, event | category | flops | bytes accessed | tf_op | source)
XLA Modules:
  0.0 177.9 jit_solution(4309097797462718142)
XLA Ops:
  0.0 1.4 copy.46
  1.4 21.3 %all-to-all-start = ((s32[128,1,2]{2,1,0:T(1,128)}), s32[128,1,2]{2,1,0:T(1,128)S(1)}, u32[]{:S(2)}, u32[]{:S(2)}) async-start(s32[128,1,2]{2,1,0:T(1,128)} %bitcast.3), calls=%async_computation | async-start | bytes 131072 | tf_op jit(solution)/shard_map/all_to_all | solution.py:82
  23.5 13.5 %all-to-all-done = s32[128,1,2]{2,1,0:T(1,128)S(1)} async-done(((s32[128,1,2]{2,1,0:T(1,128)}), s32[128,1,2]{2,1,0:T(1,128)S(1)}, u32[]{:S(2)}, u32[]{:S(2)}) %all-to-all-start) | async-done | bytes 1056 | tf_op jit(solution)/shard_map/all_to_all | solution.py:82
  38.5 1.5 gather_fusion
  40.6 0.9 copy.67
  41.5 6.2 %all-to-all-start.1 = ((bf16[128,16,128]{2,1,0:T(8,128)(2,1)}), bf16[128,16,128]{2,1,0:T(8,128)(2,1)S(1)}, u32[]{:S(2)}, u32[]{:S(2)}) async-start(bf16[128,16,128]{2,1,0:T(8,128)(2,1)} %bitcast.35), calls=%async_computation.1 | async-start | bytes 1048576 | tf_op jit(solution)/shard_map/all_to_all | solution.py:60
  47.9 4.9 %fusion.41 = bf16[512,448]{1,0:T(8,128)(2,1)} fusion(s32[448]{0:T(512)S(1)} %pad_add_fusion, s32[512]{0:T(512)S(1)} %multiply_add_fusion.1), kind=kLoop, calls=%fused_computation.64 | loop fusion | flops 4358144 | bytes 462592 | tf_op jit(solution)/shard_map/neg | solution.py:127
  53.1 24.8 %all-to-all-done.1 = bf16[128,16,128]{2,1,0:T(8,128)(2,1)S(1)} async-done(((bf16[128,16,128]{2,1,0:T(8,128)(2,1)}), bf16[128,16,128]{2,1,0:T(8,128)(2,1)S(1)}, u32[]{:S(2)}, u32[]{:S(2)}) %all-to-all-start.1) | async-done | bytes 524320 | tf_op jit(solution)/shard_map/all_to_all | solution.py:60
  79.7 8.6 %all-to-all-start.2 = ((bf16[4,80,2,3,128]{4,1,3,2,0:T(8,128)(2,1)}), bf16[4,80,2,3,128]{4,1,3,2,0:T(8,128)(2,1)S(1)}, u32[]{:S(2)}, u32[]{:S(2)}) async-start(bf16[4,80,2,3,128]{4,1,3,2,0:T(8,128)(2,1)} %copy.49), calls=%async_computation.2 | async-start | bytes 983040 | tf_op jit(solution)/shard_map/all_to_all | solution.py:89
  89.0 0.9 copy.65
  89.9 0.9 copy.66
  90.8 3.2 %gather_fusion.2 = f32[448]{0:T(512)} fusion(f32[1024]{0:T(1024)S(1)} %fusion.54, s32[1024]{0:T(1024)S(1)} %pad_clamp_fusion), kind=kCustom, calls=%fused_computation.2 | custom fusion | bytes 5376 | tf_op jit(solution)/shard_map/gather | solution.py:131
  94.0 4.9 %multiply_convert_fusion.1 = bf16[512,448]{1,0:T(8,128)(2,1)} fusion(s32[448]{0:T(512)S(1)} %pad_add_fusion, s32[512]{0:T(512)S(1)} %multiply_add_fusion.1), kind=kLoop, calls=%fused_computation.52 | loop fusion | flops 3670016 | bytes 462592 | tf_op jit(solution)/shard_map/convert_element_type | solution.py:126
  100.3 1.4 gather_fusion.1
  102.8 1.4 multiply_add_fusion
  104.2 5.3 %convolution_reduce-precision_fusion = f32[576,1024]{1,0:T(8,128)} fusion(f32[576,512]{1,0:T(8,128)} %bitcast.102, f32[576,512]{1,0:T(8,128)S(1)} %bitcast.101, f32[576]{0:T(1024)S(1)} %mul.254, bf16[512,448]{1,0:T(8,128)(2,1)S(1)} %copy-done, bf16[512,448]{1,0:T(8,128)(2,1)} %multiply_convert_fusion.1, bf16[576,224]{0,1:T(8,128)(2,1)} %copy.66, ...), kind=kOutput, calls=%fused_computation.23 | convolution fusion | flops 1065058304 | bytes 6158592 | tf_op jit(solution)/shard_map/dot_general | solution.py:148
  109.5 2.4 %add_reduce_fusion = (bf16[3,64,512]{2,1,0:T(8,128)(2,1)S(1)}, bf16[3,64,512]{2,1,0:T(8,128)(2,1)S(1)}, f32[3,64,512]{2,1,0:T(8,128)S(1)}, f32[3,64,512]{2,1,0:T(8,128)S(1)}) fusion(f32[3,3,64,1024]{3,2,1,0:T(8,128)} %bitcast.90, f32[3,64,512]{2,1,0:T(8,128)S(1)} %get-tuple-element.24, f32[3,64,512]{2,1,0:T(8,128)S(1)} %get-tuple-element.25, ...), kind=kLoop, calls=%fused_computation.31 | loop fusion | flops 4325376 | bytes 5111808 | tf_op jit(solution)/shard_map/reduce_sum | solution.py:158
  112.1 12.5 %all_to_all.34 = bf16[4,64,2,3,128]{4,1,3,2,0:T(8,128)(2,1)S(1)} all-to-all(bf16[4,64,2,3,128]{4,1,3,2,0:T(8,128)(2,1)S(1)} %copy.56), channel_id=1, replica_groups=mesh['blk'=128,'frq'=4] {'frq'}, dimensions={0} | all-to-all | bytes 786432 | tf_op jit(solution)/shard_map/all_to_all | solution.py:185
  125.3 0.9 copy.70
  126.2 6.4 %all-to-all-start.4 = ((bf16[128,16,128]{2,1,0:T(8,128)(2,1)}), bf16[128,16,128]{2,1,0:T(8,128)(2,1)S(1)}, u32[]{:S(2)}, u32[]{:S(2)}) async-start(bf16[128,16,128]{2,1,0:T(8,128)(2,1)} %bitcast.47), calls=%async_computation.4 | async-start | bytes 1048576 | tf_op jit(solution)/shard_map/all_to_all | solution.py:60
  132.6 8.6 %sine_multiply_fusion = (f32[512,1024]{1,0:T(8,128)S(1)}, f32[512,1024]{1,0:T(8,128)S(1)}, f32[512,1024]{1,0:T(8,128)S(1)}) fusion(s32[512]{0:T(512)S(1)} %multiply_add_fusion.1), kind=kLoop, calls=%fused_computation.15 | loop fusion | flops 8912896 | bytes 6293504 | tf_op jit(solution)/shard_map/div | solution.py:171
  142.5 2.7 %fusion = f32[1024,48]{0,1:T(8,128)S(1)} fusion(f32[1024,48]{0,1:T(8,128)S(1)} %bitcast.103, f32[512,1024]{1,0:T(8,128)S(1)} %get-tuple-element.20, f32[512,1024]{1,0:T(8,128)S(1)} %get-tuple-element.21), kind=kOutput, calls=%fused_computation.3 | convolution fusion | flops 605028352 | bytes 4587520 | tf_op jit(solution)/shard_map/dot_general | solution.py:173
  145.2 17.6 %all-to-all-done.4 = bf16[128,16,128]{2,1,0:T(8,128)(2,1)S(1)} async-done(((bf16[128,16,128]{2,1,0:T(8,128)(2,1)}), bf16[128,16,128]{2,1,0:T(8,128)(2,1)S(1)}, u32[]{:S(2)}, u32[]{:S(2)}) %all-to-all-start.4) | async-done | bytes 524320 | tf_op jit(solution)/shard_map/all_to_all | solution.py:60
  164.5 12.8 %all_to_all.35 = f32[4,256,3,16]{1,3,2,0:T(8,128)S(1)} all-to-all(f32[4,256,3,16]{1,3,2,0:T(8,128)S(1)} %copy.60), channel_id=1, replica_groups=mesh['blk'=128,'frq'=4] {'frq'}, dimensions={0} | all-to-all | bytes 393216 | tf_op jit(solution)/shard_map/all_to_all | solution.py:214
  (77 shorter events, 12.7 us)
Async XLA Ops:
  1.4 35.6 %all-to-all-start = ((s32[128,1,2]{2,1,0:T(1,128)}), s32[128,1,2]{2,1,0:T(1,128)S(1)}, u32[]{:S(2)}, u32[]{:S(2)}) async-start(s32[128,1,2]{2,1,0:T(1,128)} %bitcast.3), calls=%async_computation | async-start | bytes 131072 | tf_op jit(solution)/shard_map/all_to_all | solution.py:82
  40.1 7.7 %copy-start.6 = (s32[1,128]{1,0:T(1,128)S(1)}, s32[1,128]{1,0:T(1,128)}, u32[]{:S(2)}) copy-start(s32[1,128]{1,0:T(1,128)} %param.9) | copy-start | bytes 1540
  40.2 12.7 %copy-start.1 = (bf16[64,3,3,1024]{3,0,2,1:T(8,128)(2,1)S(1)}, bf16[64,3,3,1024]{3,0,2,1:T(8,128)(2,1)}, u32[]{:S(2)}) copy-start(bf16[64,3,3,1024]{3,0,2,1:T(8,128)(2,1)} %param.6) | copy-start | bytes 3538948
  41.5 36.4 %all-to-all-start.1 = ((bf16[128,16,128]{2,1,0:T(8,128)(2,1)}), bf16[128,16,128]{2,1,0:T(8,128)(2,1)S(1)}, u32[]{:S(2)}, u32[]{:S(2)}) async-start(bf16[128,16,128]{2,1,0:T(8,128)(2,1)} %bitcast.35), calls=%async_computation.1 | async-start | bytes 1048576 | tf_op jit(solution)/shard_map/all_to_all | solution.py:60
  78.1 10.2 %copy-start.5 = (s32[1,128,2]{1,2,0:T(2,128)S(1)}, s32[1,128,2]{1,2,0:T(2,128)}, u32[]{:S(2)}) copy-start(s32[1,128,2]{1,2,0:T(2,128)} %param.7) | copy-start | bytes 3076
  79.7 19.2 %all-to-all-start.2 = ((bf16[4,80,2,3,128]{4,1,3,2,0:T(8,128)(2,1)}), bf16[4,80,2,3,128]{4,1,3,2,0:T(8,128)(2,1)S(1)}, u32[]{:S(2)}, u32[]{:S(2)}) async-start(bf16[4,80,2,3,128]{4,1,3,2,0:T(8,128)(2,1)} %copy.49), calls=%async_computation.2 | async-start | bytes 983040 | tf_op jit(solution)/shard_map/all_to_all | solution.py:89
  88.8 10.3 %copy-start.2 = (s32[64]{0:T(128)}, s32[64]{0:T(128)S(1)}, u32[]{:S(2)}) copy-start(s32[64]{0:T(128)S(1)} %dynamic_slice.12) | copy-start | bytes 772
  102.8 1.4 copy-start
  102.8 1.4 copy-start.4
  126.2 36.5 %all-to-all-start.4 = ((bf16[128,16,128]{2,1,0:T(8,128)(2,1)}), bf16[128,16,128]{2,1,0:T(8,128)(2,1)S(1)}, u32[]{:S(2)}, u32[]{:S(2)}) async-start(bf16[128,16,128]{2,1,0:T(8,128)(2,1)} %bitcast.47), calls=%async_computation.4 | async-start | bytes 1048576 | tf_op jit(solution)/shard_map/all_to_all | solution.py:60
  141.2 0.7 copy-start.3

commit v4 on v3

--- a/solution.py
+++ b/solution.py
@@ -83,6 +83,36 @@
     asked_rows = jnp.take(spec_rows, asked_ids.reshape(slot_total), axis=0, mode="clip")
     rows_new = blk_exchange(asked_rows.reshape(block_total, -1)).reshape(
         band_total, item_count, 2, 3, freq_dev
+    )
+    lag_low = NT // 32
+    lag_high = NT // 4
+    lag_index = jnp.concatenate(
+        [
+            lax.iota(jnp.int32, lag_high - lag_low) + lag_low,
+            lax.iota(jnp.int32, lag_high - lag_low) + (NT - lag_high + 1),
+        ]
+    )
+    phase = (2 * lax.iota(jnp.int32, NF) + 1)[:, None] * lag_index[None, :] % (2 * NT)
+    phase = phase.astype(jnp.float32) * (math.pi / NT)
+    basis = jnp.concatenate(
+        [
+            (jnp.cos(phase) / math.sqrt(NF)).astype(jnp.bfloat16),
+            -(jnp.sin(phase) / math.sqrt(NF)).astype(jnp.bfloat16),
+        ],
+        axis=0,
+    )
+    lag_size = jnp.minimum(lag_index, NT - lag_index)
+    window = ((lag_size >= lag_low) & (lag_size < lag_high)).astype(jnp.float32)
+    observed_all = jnp.transpose(observed, (1, 2, 0, 3)).reshape(9 * item_count, NT)
+    observed_rows = jnp.concatenate(
+        [
+            observed_all[:, lag_low:lag_high],
+            observed_all[:, NT - lag_high + 1 : NT - lag_low + 1],
+        ],
+        axis=1,
+    ).astype(jnp.float32)
+    basis, observed_rows, window, rows_new = lax.optimization_barrier(
+        (basis, observed_rows, window, rows_new)
     )
     own_table = jnp.broadcast_to(spec_rows[None], (band_total, per_block, 2, 3, freq_dev))
     sent = jnp.concatenate([rows_new, own_table], axis=1)
@@ -111,32 +141,6 @@
         )
         * alive_col
     ).astype(jnp.bfloat16)
-    lag_low = NT // 32
-    lag_high = NT // 4
-    lag_index = jnp.concatenate(
-        [
-            lax.iota(jnp.int32, lag_high - lag_low) + lag_low,
-            lax.iota(jnp.int32, lag_high - lag_low) + (NT - lag_high + 1),
-        ]
-    )
-    phase = (2 * lax.iota(jnp.int32, NF) + 1)[:, None] * lag_index[None, :] % (2 * NT)
-    phase = phase.astype(jnp.float32) * (math.pi / NT)
-    basis = jnp.concatenate(
-        [
-            (jnp.cos(phase) / math.sqrt(NF)).astype(jnp.bfloat16),
-            -(jnp.sin(phase) / math.sqrt(NF)).astype(jnp.bfloat16),
-        ],
-        axis=0,
-    )
-    window = lag_window()[lag_index]
-    observed_all = jnp.transpose(observed, (1, 2, 0, 3)).reshape(9 * item_count, NT)
-    observed_rows = jnp.concatenate(
-        [
-            observed_all[:, lag_low:lag_high],
-            observed_all[:, NT - lag_high + 1 : NT - lag_low + 1],
-        ],
-        axis=1,
-    ).astype(jnp.float32)
     station_iota = lax.iota(jnp.int32, per_block)
     correlation = jnp.dot(
         cross.reshape(9 * item_count, 2 * NF), basis, preferred_element_type=jnp.float32

time: 178 us -> 177 us (level)
  local copies, waits for them, and re-layouts: 19.5 us -> 15.1 us
  waiting for transfers between devices: 55.8 us -> 58.7 us
    all_to_all x1, waiting for transfers between devices: 0.01 us -> 8.31 us  [local(): lax.all_to_all(sent, 'frq', split_axis=0, concat_axis=0, tiled=True)]
    all_to_all x2, waiting for transfers between devices: 42.3 us -> 36.9 us  [blk_exchange(): moved = lax.all_to_all(wide, 'blk', split_axis=0, concat_axis=0, tiled=True)]
    gather x1 -> x0, local copies, waits for them, and re-layouts: 3.21 us -> none  [local(): window = lag_window()[lag_index]]
    unnamed x27 -> x22, local copies, waits for them, and re-layouts: 6.91 us -> 4.97 us
  transfers between devices with their start and end apart: 4 -> 4, of which waited for: 3 -> 4; matrix products, arithmetic and copies ran while one was open for 16% -> 14% of each run, Pallas kernels for 0% -> 0%
where the time goes in v4:
time: 177 us; the launch traced here: 176 us
  waiting for transfers between devices  58.7 us (33%)
  starting transfers between devices  42.4 us (24%)
  other arithmetic  25.9 us (15%)
  blocking collectives  23.9 us (14%)
  local copies, waits for them, and re-layouts  15.1 us (9%)
  matrix products  9.88 us (6%)
    all_to_all x2, waiting for transfers between devices, blk_exchange(): moved = lax.all_to_all(wide, 'blk', split_axis=0, concat_axis=0, tiled=True)  36.9 us
    all_to_all x1, starting transfers between devices, local(): lax.all_to_all(partner_local, 'blk', split_axis=0, concat_axis=0, tiled=T...  21.3 us
    all_to_all x1, waiting for transfers between devices, local(): lax.all_to_all(partner_local, 'blk', split_axis=0, concat_axis=0, tiled=T...  13.5 us
    all_to_all x1, blocking collectives, local(): lax.all_to_all(product.reshape(band_total, NT // band_total, 3, per_block...  12.8 us
    all_to_all x2, starting transfers between devices, blk_exchange(): moved = lax.all_to_all(wide, 'blk', split_axis=0, concat_axis=0, tiled=True)  12.6 us
    all_to_all x1, blocking collectives, local(): lax.all_to_all(back_sent, 'frq', split_axis=0, concat_axis=0, tiled=True)  11.2 us
    div x1, other arithmetic, local(): sin_full = jnp.sin(phase_full) / math.sqrt(NF)  8.6 us
    all_to_all x1, starting transfers between devices, local(): lax.all_to_all(sent, 'frq', split_axis=0, concat_axis=0, tiled=True)  8.48 us
  transfers between devices with their start and end apart: 4, of which 4 were waited for; matrix products, arithmetic and copies ran while one was open for 14% of the time, Pallas kernels for 0%

profile of v4, /device:TPU:1, one launch (start us, length us, event | category | flops | bytes accessed | tf_op | source)
XLA Modules:
  0.0 176.4 jit_solution(16435483459305629430)
XLA Ops:
  0.0 1.4 copy.48
  1.4 21.3 %all-to-all-start = ((s32[128,1,2]{2,1,0:T(1,128)}), s32[128,1,2]{2,1,0:T(1,128)S(1)}, u32[]{:S(2)}, u32[]{:S(2)}) async-start(s32[128,1,2]{2,1,0:T(1,128)} %bitcast.6), calls=%async_computation | async-start | bytes 131072 | tf_op jit(solution)/shard_map/all_to_all | solution.py:82
  23.5 13.5 %all-to-all-done = s32[128,1,2]{2,1,0:T(1,128)S(1)} async-done(((s32[128,1,2]{2,1,0:T(1,128)}), s32[128,1,2]{2,1,0:T(1,128)S(1)}, u32[]{:S(2)}, u32[]{:S(2)}) %all-to-all-start) | async-done | bytes 1056 | tf_op jit(solution)/shard_map/all_to_all | solution.py:82
  38.5 1.5 gather_fusion
  40.6 0.9 copy.67
  41.5 6.2 %all-to-all-start.1 = ((bf16[128,16,128]{2,1,0:T(8,128)(2,1)}), bf16[128,16,128]{2,1,0:T(8,128)(2,1)S(1)}, u32[]{:S(2)}, u32[]{:S(2)}) async-start(bf16[128,16,128]{2,1,0:T(8,128)(2,1)} %bitcast.32), calls=%async_computation.1 | async-start | bytes 1048576 | tf_op jit(solution)/shard_map/all_to_all | solution.py:60
  48.5 4.3 %fusion.31 = bf16[512,448]{1,0:T(8,128)(2,1)S(1)} fusion(s32[448]{0:T(512)S(1)} %pad_add_fusion, s32[512]{0:T(512)S(1)} %multiply_add_fusion.1), kind=kLoop, calls=%fused_computation.58 | loop fusion | flops 4358144 | bytes 462592 | tf_op jit(solution)/shard_map/neg | solution.py:100
  52.8 4.2 %multiply_convert_fusion.1 = bf16[512,448]{1,0:T(8,128)(2,1)S(1)} fusion(s32[448]{0:T(512)S(1)} %pad_add_fusion, s32[512]{0:T(512)S(1)} %multiply_add_fusion.1), kind=kLoop, calls=%fused_computation.48 | loop fusion | flops 3670016 | bytes 462592 | tf_op jit(solution)/shard_map/convert_element_type | solution.py:99
  57.0 1.2 pad_maximum_fusion
  58.2 1.1 maximum_convert_fusion
  59.3 18.7 %all-to-all-done.1 = bf16[128,16,128]{2,1,0:T(8,128)(2,1)S(1)} async-done(((bf16[128,16,128]{2,1,0:T(8,128)(2,1)}), bf16[128,16,128]{2,1,0:T(8,128)(2,1)S(1)}, u32[]{:S(2)}, u32[]{:S(2)}) %all-to-all-start.1) | async-done | bytes 524320 | tf_op jit(solution)/shard_map/all_to_all | solution.py:60
  79.8 8.5 %all-to-all-start.2 = ((bf16[4,80,2,3,128]{4,1,3,2,0:T(8,128)(2,1)}), bf16[4,80,2,3,128]{4,1,3,2,0:T(8,128)(2,1)S(1)}, u32[]{:S(2)}, u32[]{:S(2)}) async-start(bf16[4,80,2,3,128]{4,1,3,2,0:T(8,128)(2,1)} %copy.51), calls=%async_computation.2 | async-start | bytes 983040 | tf_op jit(solution)/shard_map/all_to_all | solution.py:119
  89.1 8.3 %all-to-all-done.2 = bf16[4,80,2,3,128]{4,1,3,2,0:T(8,128)(2,1)S(1)} async-done(((bf16[4,80,2,3,128]{4,1,3,2,0:T(8,128)(2,1)}), bf16[4,80,2,3,128]{4,1,3,2,0:T(8,128)(2,1)S(1)}, u32[]{:S(2)}, u32[]{:S(2)}) %all-to-all-start.2) | async-done | bytes 491552 | tf_op jit(solution)/shard_map/all_to_all | solution.py:119
  99.7 1.4 gather_fusion.1
  102.1 1.4 multiply_add_fusion
  103.5 5.8 %convolution_reduce-precision_fusion = f32[576,1024]{1,0:T(8,128)} fusion(bf16[1024,448]{1,0:T(8,128)(2,1)} %pad_maximum_fusion, f32[576,448]{0,1:T(8,128)} %maximum_convert_fusion, f32[576,512]{1,0:T(8,128)} %bitcast.113, f32[576,512]{1,0:T(8,128)S(1)} %bitcast.112, f32[576]{0:T(1024)S(1)} %mul.259, f32[448]{0:T(512)S(1)} %and_convert_fusion, ...), kind=kOutput, calls=%fused_computation.22 | convolution fusion | flops 1060356096 | bytes 6674688 | tf_op jit(solution)/shard_map/dot_general | solution.py:152
  109.3 2.4 %add_reduce_fusion = (bf16[3,64,512]{2,1,0:T(8,128)(2,1)S(1)}, bf16[3,64,512]{2,1,0:T(8,128)(2,1)S(1)}, f32[3,64,512]{2,1,0:T(8,128)S(1)}, f32[3,64,512]{2,1,0:T(8,128)S(1)}) fusion(f32[3,3,64,1024]{3,2,1,0:T(8,128)} %bitcast.101, f32[3,64,512]{2,1,0:T(8,128)S(1)} %bitcast.100, f32[3,64,512]{2,1,0:T(8,128)S(1)} %bitcast.98, f32[3,64,512]{2,1,0:T(8,128)S(1)} %bitcast.94, ...), kind=kLoop, calls=%fused_computation.30 | loop fusion | flops 4325376 | bytes 5111808 | tf_op jit(solution)/shard_map/reduce_sum | solution.py:162
  111.9 11.2 %all_to_all.34 = bf16[4,64,2,3,128]{4,1,3,2,0:T(8,128)(2,1)S(1)} all-to-all(bf16[4,64,2,3,128]{4,1,3,2,0:T(8,128)(2,1)S(1)} %copy.56), channel_id=1, replica_groups=mesh['blk'=128,'frq'=4] {'frq'}, dimensions={0} | all-to-all | bytes 786432 | tf_op jit(solution)/shard_map/all_to_all | solution.py:189
  123.8 0.9 copy.70
  124.7 6.4 %all-to-all-start.4 = ((bf16[128,16,128]{2,1,0:T(8,128)(2,1)}), bf16[128,16,128]{2,1,0:T(8,128)(2,1)S(1)}, u32[]{:S(2)}, u32[]{:S(2)}) async-start(bf16[128,16,128]{2,1,0:T(8,128)(2,1)} %bitcast.44), calls=%async_computation.4 | async-start | bytes 1048576 | tf_op jit(solution)/shard_map/all_to_all | solution.py:60
  131.1 8.6 %sine_multiply_fusion = (f32[512,1024]{1,0:T(8,128)S(1)}, f32[512,1024]{1,0:T(8,128)S(1)}, f32[512,1024]{1,0:T(8,128)S(1)}) fusion(s32[512]{0:T(512)S(1)} %multiply_add_fusion.1), kind=kLoop, calls=%fused_computation.14 | loop fusion | flops 8912896 | bytes 6293504 | tf_op jit(solution)/shard_map/div | solution.py:175
  140.4 2.7 %fusion = f32[1024,48]{0,1:T(8,128)S(1)} fusion(f32[1024,48]{0,1:T(8,128)S(1)} %bitcast.114, f32[512,1024]{1,0:T(8,128)S(1)} %get-tuple-element.28, f32[512,1024]{1,0:T(8,128)S(1)} %get-tuple-element.29), kind=kOutput, calls=%fused_computation.2 | convolution fusion | flops 605028352 | bytes 4587520 | tf_op jit(solution)/shard_map/dot_general | solution.py:177
  143.1 18.1 %all-to-all-done.4 = bf16[128,16,128]{2,1,0:T(8,128)(2,1)S(1)} async-done(((bf16[128,16,128]{2,1,0:T(8,128)(2,1)}), bf16[128,16,128]{2,1,0:T(8,128)(2,1)S(1)}, u32[]{:S(2)}, u32[]{:S(2)}) %all-to-all-start.4) | async-done | bytes 524320 | tf_op jit(solution)/shard_map/all_to_all | solution.py:60
  163.0 12.8 %all_to_all.35 = f32[4,256,3,16]{1,3,2,0:T(8,128)S(1)} all-to-all(f32[4,256,3,16]{1,3,2,0:T(8,128)S(1)} %copy.60), channel_id=1, replica_groups=mesh['blk'=128,'frq'=4] {'frq'}, dimensions={0} | all-to-all | bytes 393216 | tf_op jit(solution)/shard_map/all_to_all | solution.py:218
  (73 shorter events, 13.2 us)
Async XLA Ops:
  1.4 35.6 %all-to-all-start = ((s32[128,1,2]{2,1,0:T(1,128)}), s32[128,1,2]{2,1,0:T(1,128)S(1)}, u32[]{:S(2)}, u32[]{:S(2)}) async-start(s32[128,1,2]{2,1,0:T(1,128)} %bitcast.6), calls=%async_computation | async-start | bytes 131072 | tf_op jit(solution)/shard_map/all_to_all | solution.py:82
  40.6 7.1 %copy-start.1 = (bf16[64,3,3,1024]{3,0,2,1:T(8,128)(2,1)S(1)}, bf16[64,3,3,1024]{3,0,2,1:T(8,128)(2,1)}, u32[]{:S(2)}) copy-start(bf16[64,3,3,1024]{3,0,2,1:T(8,128)(2,1)} %param.6) | copy-start | bytes 3538948
  41.5 36.6 %all-to-all-start.1 = ((bf16[128,16,128]{2,1,0:T(8,128)(2,1)}), bf16[128,16,128]{2,1,0:T(8,128)(2,1)S(1)}, u32[]{:S(2)}, u32[]{:S(2)}) async-start(bf16[128,16,128]{2,1,0:T(8,128)(2,1)} %bitcast.32), calls=%async_computation.1 | async-start | bytes 1048576 | tf_op jit(solution)/shard_map/all_to_all | solution.py:60
  79.0 9.4 %copy-start.2 = (s32[1,128,2]{1,2,0:T(2,128)S(1)}, s32[1,128,2]{1,2,0:T(2,128)}, u32[]{:S(2)}) copy-start(s32[1,128,2]{1,2,0:T(2,128)} %param.7) | copy-start | bytes 3076
  79.0 9.6 %copy-start.3 = (s32[1,128]{1,0:T(1,128)S(1)}, s32[1,128]{1,0:T(1,128)}, u32[]{:S(2)}) copy-start(s32[1,128]{1,0:T(1,128)} %param.9) | copy-start | bytes 1540
  79.8 17.6 %all-to-all-start.2 = ((bf16[4,80,2,3,128]{4,1,3,2,0:T(8,128)(2,1)}), bf16[4,80,2,3,128]{4,1,3,2,0:T(8,128)(2,1)S(1)}, u32[]{:S(2)}, u32[]{:S(2)}) async-start(bf16[4,80,2,3,128]{4,1,3,2,0:T(8,128)(2,1)} %copy.51), calls=%async_computation.2 | async-start | bytes 983040 | tf_op jit(solution)/shard_map/all_to_all | solution.py:119
  97.9 0.9 copy-start
  98.8 0.9 slice-start
  124.7 36.6 %all-to-all-start.4 = ((bf16[128,16,128]{2,1,0:T(8,128)(2,1)}), bf16[128,16,128]{2,1,0:T(8,128)(2,1)S(1)}, u32[]{:S(2)}, u32[]{:S(2)}) async-start(bf16[128,16,128]{2,1,0:T(8,128)(2,1)} %bitcast.44), calls=%async_computation.4 | async-start | bytes 1048576 | tf_op jit(solution)/shard_map/all_to_all | solution.py:60

commit v5 on v4

--- a/solution.py
+++ b/solution.py
@@ -80,6 +80,17 @@
         .astype(jnp.float32)
     )
     asked_ids = lax.all_to_all(partner_local, "blk", split_axis=0, concat_axis=0, tiled=True)
+    own_table = lax.all_to_all(
+        jnp.broadcast_to(spec_rows[None], (band_total, per_block, 2, 3, freq_dev)),
+        "frq",
+        split_axis=0,
+        concat_axis=0,
+        tiled=True,
+    )
+    own_table = jnp.transpose(own_table, (2, 3, 1, 0, 4)).reshape(2, 3, per_block, NF)
+    own_group = lax.dynamic_slice_in_dim(own_ids, band_index * item_count, item_count)
+    first_rows = jnp.take(own_table, own_group, axis=2, mode="clip").astype(jnp.float32)
+    first_rows, asked_ids = lax.optimization_barrier((first_rows, asked_ids))
     asked_rows = jnp.take(spec_rows, asked_ids.reshape(slot_total), axis=0, mode="clip")
     rows_new = blk_exchange(asked_rows.reshape(block_total, -1)).reshape(
         band_total, item_count, 2, 3, freq_dev
@@ -114,17 +125,10 @@
     basis, observed_rows, window, rows_new = lax.optimization_barrier(
         (basis, observed_rows, window, rows_new)
     )
-    own_table = jnp.broadcast_to(spec_rows[None], (band_total, per_block, 2, 3, freq_dev))
-    sent = jnp.concatenate([rows_new, own_table], axis=1)
-    whole_band = lax.all_to_all(sent, "frq", split_axis=0, concat_axis=0, tiled=True)
-    whole_band = jnp.transpose(whole_band, (2, 3, 1, 0, 4)).reshape(
-        2, 3, item_count + per_block, NF
-    )
-    second_rows = whole_band[:, :, :item_count].astype(jnp.float32)
-    own_group = lax.dynamic_slice_in_dim(own_ids, band_index * item_count, item_count)
-    first_rows = jnp.take(
-        whole_band[:, :, item_count:], own_group, axis=2, mode="clip"
-    ).astype(jnp.float32)
+    whole_band = lax.all_to_all(rows_new, "frq", split_axis=0, concat_axis=0, tiled=True)
+    second_rows = (
+        jnp.transpose(whole_band, (2, 3, 1, 0, 4)).reshape(2, 3, item_count, NF).astype(jnp.float32)
+    )
     alive_band = lax.dynamic_slice_in_dim(alive_mask, band_index * item_count, item_count)
     first_re = first_rows[0][:, None]
     first_im = first_rows[1][:, None]

time: 177 us -> 179 us (1.011)
  starting transfers between devices: 42.4 us -> 46.4 us
  waiting for transfers between devices: 58.7 us -> 56.3 us
    all_to_all x1 -> x2, starting transfers between devices: 8.48 us -> 18.2 us  [the longest x1 10.1 us: local(): lax.all_to_all(jnp.broadcast_to(spec_rows[None], (band_total, per_block,...]
    all_to_all x1, starting transfers between devices: 21.3 us -> 15.4 us  [local(): lax.all_to_all(partner_local, 'blk', split_axis=0, concat_axis=0, tiled=T...]
    all_to_all x2, waiting for transfers between devices: 36.9 us -> 34 us  [blk_exchange(): moved = lax.all_to_all(wide, 'blk', split_axis=0, concat_axis=0, tiled=True)]
    all_to_all x1 -> x2, waiting for transfers between devices: 8.31 us -> 9.84 us  [the longest x1 7.4 us: local(): lax.all_to_all(rows_new, 'frq', split_axis=0, concat_axis=0, tiled=True)]
    unnamed x22 -> x20, local copies, waits for them, and re-layouts: 4.97 us -> 6.1 us
  transfers between devices with their start and end apart: 4 -> 5, of which waited for: 4 -> 5; matrix products, arithmetic and copies ran while one was open for 14% -> 17% of each run, Pallas kernels for 0% -> 0%
where the time goes in v5:
time: 179 us
  waiting for transfers between devices  56.3 us (31%)
  starting transfers between devices  46.4 us (26%)
  other arithmetic  25.1 us (14%)
  blocking collectives  24 us (13%)
  local copies, waits for them, and re-layouts  16.5 us (9%)
  matrix products  9.88 us (6%)
    all_to_all x2, waiting for transfers between devices, blk_exchange(): moved = lax.all_to_all(wide, 'blk', split_axis=0, concat_axis=0, tiled=True)  34 us
    all_to_all x1, starting transfers between devices, local(): lax.all_to_all(partner_local, 'blk', split_axis=0, concat_axis=0, tiled=T...  15.4 us
    all_to_all x1, blocking collectives, local(): lax.all_to_all(product.reshape(band_total, NT // band_total, 3, per_block...  12.8 us
    all_to_all x2, starting transfers between devices, blk_exchange(): moved = lax.all_to_all(wide, 'blk', split_axis=0, concat_axis=0, tiled=True)  12.8 us
    all_to_all x1, waiting for transfers between devices, local(): lax.all_to_all(partner_local, 'blk', split_axis=0, concat_axis=0, tiled=T...  12.4 us
    all_to_all x1, blocking collectives, local(): lax.all_to_all(back_sent, 'frq', split_axis=0, concat_axis=0, tiled=True)  11.2 us
    all_to_all x1, starting transfers between devices, local(): lax.all_to_all(jnp.broadcast_to(spec_rows[None], (band_total, per_block,...  10.1 us
    div x1, other arithmetic, local(): sin_full = jnp.sin(phase_full) / math.sqrt(NF)  8.6 us
  transfers between devices with their start and end apart: 5, of which 5 were waited for; matrix products, arithmetic and copies ran while one was open for 17% of the time, Pallas kernels for 0%

profile of v5, /device:TPU:1, one launch (start us, length us, event | category | flops | bytes accessed | tf_op | source)
XLA Modules:
  0.0 178.5 jit_solution(10011646492117329003)
XLA Ops:
  1.4 10.1 %all-to-all-start = ((bf16[4,16,2,3,128]{4,1,3,2,0:T(8,128)(2,1)}), bf16[4,16,2,3,128]{4,1,3,2,0:T(8,128)(2,1)S(1)}, u32[]{:S(2)}, u32[]{:S(2)}) async-start(bf16[4,16,2,3,128]{4,1,3,2,0:T(8,128)(2,1)} %broadcast_in_dim.10), calls=%async_computation | async-start | bytes 196608 | tf_op jit(solution)/shard_map/all_to_all | solution.py:83
  12.5 1.4 copy.54
  14.0 2.4 %all-to-all-done = bf16[4,16,2,3,128]{4,1,3,2,0:T(8,128)(2,1)S(1)} async-done(((bf16[4,16,2,3,128]{4,1,3,2,0:T(8,128)(2,1)}), bf16[4,16,2,3,128]{4,1,3,2,0:T(8,128)(2,1)S(1)}, u32[]{:S(2)}, u32[]{:S(2)}) %all-to-all-start) | async-done | bytes 98336 | tf_op jit(solution)/shard_map/all_to_all | solution.py:83
  16.4 15.4 %all-to-all-start.1 = ((s32[128,1,2]{2,1,0:T(1,128)}), s32[128,1,2]{2,1,0:T(1,128)S(1)}, u32[]{:S(2)}, u32[]{:S(2)}) async-start(s32[128,1,2]{2,1,0:T(1,128)} %bitcast.5), calls=%async_computation.1 | async-start | bytes 131072 | tf_op jit(solution)/shard_map/all_to_all | solution.py:82
  32.0 1.4 gather_fusion
  33.7 12.4 %all-to-all-done.1 = s32[128,1,2]{2,1,0:T(1,128)S(1)} async-done(((s32[128,1,2]{2,1,0:T(1,128)}), s32[128,1,2]{2,1,0:T(1,128)S(1)}, u32[]{:S(2)}, u32[]{:S(2)}) %all-to-all-start.1) | async-done | bytes 1056 | tf_op jit(solution)/shard_map/all_to_all | solution.py:82
  46.2 1.5 gather_fusion.1
  49.3 6.2 %all-to-all-start.2 = ((bf16[128,16,128]{2,1,0:T(8,128)(2,1)}), bf16[128,16,128]{2,1,0:T(8,128)(2,1)S(1)}, u32[]{:S(2)}, u32[]{:S(2)}) async-start(bf16[128,16,128]{2,1,0:T(8,128)(2,1)} %bitcast.33), calls=%async_computation.2 | async-start | bytes 1048576 | tf_op jit(solution)/shard_map/all_to_all | solution.py:60
  55.9 1.4 fusion.46
  58.4 4.3 %fusion.31 = bf16[512,448]{1,0:T(8,128)(2,1)S(1)} fusion(s32[448]{0:T(512)S(1)} %pad_add_fusion, s32[512]{0:T(512)S(1)} %multiply_add_fusion.1), kind=kLoop, calls=%fused_computation.58 | loop fusion | flops 4358144 | bytes 462592 | tf_op jit(solution)/shard_map/neg | solution.py:111
  62.7 4.2 %multiply_convert_fusion.1 = bf16[512,448]{1,0:T(8,128)(2,1)S(1)} fusion(s32[448]{0:T(512)S(1)} %pad_add_fusion, s32[512]{0:T(512)S(1)} %multiply_add_fusion.1), kind=kLoop, calls=%fused_computation.48 | loop fusion | flops 3670016 | bytes 462592 | tf_op jit(solution)/shard_map/convert_element_type | solution.py:110
  66.9 1.2 pad_maximum_fusion
  69.2 16.4 %all-to-all-done.2 = bf16[128,16,128]{2,1,0:T(8,128)(2,1)S(1)} async-done(((bf16[128,16,128]{2,1,0:T(8,128)(2,1)}), bf16[128,16,128]{2,1,0:T(8,128)(2,1)S(1)}, u32[]{:S(2)}, u32[]{:S(2)}) %all-to-all-start.2) | async-done | bytes 524320 | tf_op jit(solution)/shard_map/all_to_all | solution.py:60
  86.8 8.0 %all-to-all-start.3 = ((bf16[4,64,2,3,128]{4,1,3,2,0:T(8,128)(2,1)}), bf16[4,64,2,3,128]{4,1,3,2,0:T(8,128)(2,1)S(1)}, u32[]{:S(2)}, u32[]{:S(2)}) async-start(bf16[4,64,2,3,128]{4,1,3,2,0:T(8,128)(2,1)} %copy.59), calls=%async_computation.3 | async-start | bytes 786432 | tf_op jit(solution)/shard_map/all_to_all | solution.py:128
  95.5 7.4 %all-to-all-done.3 = bf16[4,64,2,3,128]{4,1,3,2,0:T(8,128)(2,1)S(1)} async-done(((bf16[4,64,2,3,128]{4,1,3,2,0:T(8,128)(2,1)}), bf16[4,64,2,3,128]{4,1,3,2,0:T(8,128)(2,1)S(1)}, u32[]{:S(2)}, u32[]{:S(2)}) %all-to-all-start.3) | async-done | bytes 393248 | tf_op jit(solution)/shard_map/all_to_all | solution.py:128
  104.0 1.4 multiply_add_fusion
  105.4 5.8 %convolution_reduce-precision_fusion = f32[576,1024]{1,0:T(8,128)} fusion(bf16[1024,448]{1,0:T(8,128)(2,1)} %pad_maximum_fusion, f32[576,448]{0,1:T(8,128)} %maximum_convert_fusion, f32[576,512]{1,0:T(8,128)} %bitcast.99, f32[576,512]{1,0:T(8,128)S(1)} %bitcast.98, f32[576]{0:T(1024)S(1)} %mul.259, f32[448]{0:T(512)S(1)} %copy-done.2, f32[576]{0:T(1024)S(1)} %mul.262), kind=kOutput, calls=%fused_computation.22 | convolution fusion | flops 1060356096 | bytes 6674688 | tf_op jit(solution)/shard_map/dot_general | solution.py:156
  111.2 2.4 %add_reduce_fusion = (bf16[3,64,512]{2,1,0:T(8,128)(2,1)S(1)}, bf16[3,64,512]{2,1,0:T(8,128)(2,1)S(1)}, f32[3,64,512]{2,1,0:T(8,128)S(1)}, f32[3,64,512]{2,1,0:T(8,128)S(1)}) fusion(f32[3,3,64,1024]{3,2,1,0:T(8,128)} %bitcast.88, f32[3,64,512]{2,1,0:T(8,128)S(1)} %get-tuple-element.36, f32[3,64,512]{2,1,0:T(8,128)S(1)} %get-tuple-element.37, ...), kind=kLoop, calls=%fused_computation.30 | loop fusion | flops 4325376 | bytes 5111808 | tf_op jit(solution)/shard_map/reduce_sum | solution.py:166
  113.8 11.2 %all_to_all.42 = bf16[4,64,2,3,128]{4,1,3,2,0:T(8,128)(2,1)S(1)} all-to-all(bf16[4,64,2,3,128]{4,1,3,2,0:T(8,128)(2,1)S(1)} %copy.64), channel_id=1, replica_groups=mesh['blk'=128,'frq'=4] {'frq'}, dimensions={0} | all-to-all | bytes 786432 | tf_op jit(solution)/shard_map/all_to_all | solution.py:193
  126.6 6.6 %all-to-all-start.5 = ((bf16[128,16,128]{2,1,0:T(8,128)(2,1)}), bf16[128,16,128]{2,1,0:T(8,128)(2,1)S(1)}, u32[]{:S(2)}, u32[]{:S(2)}) async-start(bf16[128,16,128]{2,1,0:T(8,128)(2,1)} %bitcast.44), calls=%async_computation.5 | async-start | bytes 1048576 | tf_op jit(solution)/shard_map/all_to_all | solution.py:60
  133.2 8.6 %sine_multiply_fusion = (f32[512,1024]{1,0:T(8,128)S(1)}, f32[512,1024]{1,0:T(8,128)S(1)}, f32[512,1024]{1,0:T(8,128)S(1)}) fusion(s32[512]{0:T(512)S(1)} %multiply_add_fusion.1), kind=kLoop, calls=%fused_computation.14 | loop fusion | flops 8912896 | bytes 6293504 | tf_op jit(solution)/shard_map/div | solution.py:179
  143.0 2.7 %fusion = f32[1024,48]{0,1:T(8,128)S(1)} fusion(f32[1024,48]{0,1:T(8,128)S(1)} %bitcast.100, f32[512,1024]{1,0:T(8,128)S(1)} %get-tuple-element.32, f32[512,1024]{1,0:T(8,128)S(1)} %get-tuple-element.33), kind=kOutput, calls=%fused_computation.2 | convolution fusion | flops 605028352 | bytes 4587520 | tf_op jit(solution)/shard_map/dot_general | solution.py:181
  145.7 17.6 %all-to-all-done.5 = bf16[128,16,128]{2,1,0:T(8,128)(2,1)S(1)} async-done(((bf16[128,16,128]{2,1,0:T(8,128)(2,1)}), bf16[128,16,128]{2,1,0:T(8,128)(2,1)S(1)}, u32[]{:S(2)}, u32[]{:S(2)}) %all-to-all-start.5) | async-done | bytes 524320 | tf_op jit(solution)/shard_map/all_to_all | solution.py:60
  165.1 12.8 %all_to_all.43 = f32[4,256,3,16]{1,3,2,0:T(8,128)S(1)} all-to-all(f32[4,256,3,16]{1,3,2,0:T(8,128)S(1)} %copy.68), channel_id=1, replica_groups=mesh['blk'=128,'frq'=4] {'frq'}, dimensions={0} | all-to-all | bytes 393216 | tf_op jit(solution)/shard_map/all_to_all | solution.py:222
  (71 shorter events, 15.3 us)
Async XLA Ops:
  1.4 15.0 %all-to-all-start = ((bf16[4,16,2,3,128]{4,1,3,2,0:T(8,128)(2,1)}), bf16[4,16,2,3,128]{4,1,3,2,0:T(8,128)(2,1)S(1)}, u32[]{:S(2)}, u32[]{:S(2)}) async-start(bf16[4,16,2,3,128]{4,1,3,2,0:T(8,128)(2,1)} %broadcast_in_dim.10), calls=%async_computation | async-start | bytes 196608 | tf_op jit(solution)/shard_map/all_to_all | solution.py:83
  14.0 17.9 %copy-start = (s32[64]{0:T(128)}, s32[64]{0:T(128)S(1)}, u32[]{:S(2)}) copy-start(s32[64]{0:T(128)S(1)} %dynamic_slice.12) | copy-start | bytes 772
  16.4 29.7 %all-to-all-start.1 = ((s32[128,1,2]{2,1,0:T(1,128)}), s32[128,1,2]{2,1,0:T(1,128)S(1)}, u32[]{:S(2)}, u32[]{:S(2)}) async-start(s32[128,1,2]{2,1,0:T(1,128)} %bitcast.5), calls=%async_computation.1 | async-start | bytes 131072 | tf_op jit(solution)/shard_map/all_to_all | solution.py:82
  48.3 7.1 %copy-start.3 = (s32[1,128]{1,0:T(1,128)S(1)}, s32[1,128]{1,0:T(1,128)}, u32[]{:S(2)}) copy-start(s32[1,128]{1,0:T(1,128)} %param.9) | copy-start | bytes 1540
  49.3 36.3 %all-to-all-start.2 = ((bf16[128,16,128]{2,1,0:T(8,128)(2,1)}), bf16[128,16,128]{2,1,0:T(8,128)(2,1)S(1)}, u32[]{:S(2)}, u32[]{:S(2)}) async-start(bf16[128,16,128]{2,1,0:T(8,128)(2,1)} %bitcast.33), calls=%async_computation.2 | async-start | bytes 1048576 | tf_op jit(solution)/shard_map/all_to_all | solution.py:60
  86.8 16.1 %all-to-all-start.3 = ((bf16[4,64,2,3,128]{4,1,3,2,0:T(8,128)(2,1)}), bf16[4,64,2,3,128]{4,1,3,2,0:T(8,128)(2,1)S(1)}, u32[]{:S(2)}, u32[]{:S(2)}) async-start(bf16[4,64,2,3,128]{4,1,3,2,0:T(8,128)(2,1)} %copy.59), calls=%async_computation.3 | async-start | bytes 786432 | tf_op jit(solution)/shard_map/all_to_all | solution.py:128
  104.0 1.4 copy-start.2
  126.6 36.8 %all-to-all-start.5 = ((bf16[128,16,128]{2,1,0:T(8,128)(2,1)}), bf16[128,16,128]{2,1,0:T(8,128)(2,1)S(1)}, u32[]{:S(2)}, u32[]{:S(2)}) async-start(bf16[128,16,128]{2,1,0:T(8,128)(2,1)} %bitcast.44), calls=%async_computation.5 | async-start | bytes 1048576 | tf_op jit(solution)/shard_map/all_to_all | solution.py:60
  141.8 0.6 copy-start.1

commit v6 on v4

--- a/solution.py
+++ b/solution.py
@@ -54,11 +54,10 @@
 
 def blk_exchange(chunks):
     count, width = chunks.shape
-    tile = 16 * 128
-    padded = -(-width // tile) * tile
-    wide = jnp.pad(chunks, ((0, 0), (0, padded - width))).reshape(count, padded // 128, 128)
-    moved = lax.all_to_all(wide, "blk", split_axis=0, concat_axis=0, tiled=True)
-    return moved.reshape(count, padded)[:, :width]
+    moved = lax.all_to_all(
+        chunks.reshape(count, width // 128, 128), "blk", split_axis=0, concat_axis=0, tiled=True
+    )
+    return moved.reshape(count, width)
 
 
 def local(spectra, observed, own_station, partner_station, pair_count):

time: 177 us -> 176 us (level)
    another operation x0 -> x3, local copies, waits for them, and re-layouts: none -> 2.49 us  [the longest x2 2.22 us: blk_exchange(): chunks.reshape(count, width // 128, 128)]
    unnamed x22 -> x16, local copies, waits for them, and re-layouts: 4.97 us -> 2.77 us
where the time goes in v6:
time: 176 us
  waiting for transfers between devices  58.7 us (33%)
  starting transfers between devices  42.4 us (24%)
  other arithmetic  25.9 us (15%)
  blocking collectives  23.9 us (14%)
  local copies, waits for them, and re-layouts  14.7 us (8%)
  matrix products  9.88 us (6%)
    all_to_all x2, waiting for transfers between devices, blk_exchange(): lax.all_to_all(chunks.reshape(count, width // 128, 128), 'blk', split_axi...  36.9 us
    all_to_all x1, starting transfers between devices, local(): lax.all_to_all(partner_local, 'blk', split_axis=0, concat_axis=0, tiled=T...  21.3 us
    all_to_all x1, waiting for transfers between devices, local(): lax.all_to_all(partner_local, 'blk', split_axis=0, concat_axis=0, tiled=T...  13.5 us
    all_to_all x1, blocking collectives, local(): lax.all_to_all(product.reshape(band_total, NT // band_total, 3, per_block...  12.8 us
    all_to_all x2, starting transfers between devices, blk_exchange(): lax.all_to_all(chunks.reshape(count, width // 128, 128), 'blk', split_axi...  12.6 us
    all_to_all x1, blocking collectives, local(): lax.all_to_all(back_sent, 'frq', split_axis=0, concat_axis=0, tiled=True)  11.2 us
    div x1, other arithmetic, local(): sin_full = jnp.sin(phase_full) / math.sqrt(NF)  8.6 us
    all_to_all x1, starting transfers between devices, local(): lax.all_to_all(sent, 'frq', split_axis=0, concat_axis=0, tiled=True)  8.48 us
  transfers between devices with their start and end apart: 4, of which 4 were waited for; matrix products, arithmetic and copies ran while one was open for 14% of the time, Pallas kernels for 0%

profile of v6, /device:TPU:1, one launch (start us, length us, event | category | flops | bytes accessed | tf_op | source)
XLA Modules:
  0.0 175.9 jit_solution(13903311804465542591)
XLA Ops:
  0.0 1.4 copy.48
  1.4 21.3 %all-to-all-start = ((s32[128,1,2]{2,1,0:T(1,128)}), s32[128,1,2]{2,1,0:T(1,128)S(1)}, u32[]{:S(2)}, u32[]{:S(2)}) async-start(s32[128,1,2]{2,1,0:T(1,128)} %bitcast.6), calls=%async_computation | async-start | bytes 131072 | tf_op jit(solution)/shard_map/all_to_all | solution.py:81
  23.5 13.5 %all-to-all-done = s32[128,1,2]{2,1,0:T(1,128)S(1)} async-done(((s32[128,1,2]{2,1,0:T(1,128)}), s32[128,1,2]{2,1,0:T(1,128)S(1)}, u32[]{:S(2)}, u32[]{:S(2)}) %all-to-all-start) | async-done | bytes 1056 | tf_op jit(solution)/shard_map/all_to_all | solution.py:81
  38.5 1.5 gather_fusion
  40.2 1.1 reshape_reshape.9
  41.3 6.2 %all-to-all-start.1 = ((bf16[128,12,128]{2,1,0:T(8,128)(2,1)}), bf16[128,12,128]{2,1,0:T(8,128)(2,1)S(1)}, u32[]{:S(2)}, u32[]{:S(2)}) async-start(bf16[128,12,128]{2,1,0:T(8,128)(2,1)} %reshape_reshape.9), calls=%async_computation.1 | async-start | bytes 1048576 | tf_op jit(solution)/shard_map/all_to_all | solution.py:57
  48.3 4.3 %fusion.31 = bf16[512,448]{1,0:T(8,128)(2,1)S(1)} fusion(s32[448]{0:T(512)S(1)} %pad_add_fusion, s32[512]{0:T(512)S(1)} %multiply_add_fusion.1), kind=kLoop, calls=%fused_computation.58 | loop fusion | flops 4358144 | bytes 462592 | tf_op jit(solution)/shard_map/neg | solution.py:99
  52.6 4.2 %multiply_convert_fusion.1 = bf16[512,448]{1,0:T(8,128)(2,1)S(1)} fusion(s32[448]{0:T(512)S(1)} %pad_add_fusion, s32[512]{0:T(512)S(1)} %multiply_add_fusion.1), kind=kLoop, calls=%fused_computation.48 | loop fusion | flops 3670016 | bytes 462592 | tf_op jit(solution)/shard_map/convert_element_type | solution.py:98
  56.8 1.2 pad_maximum_fusion
  58.0 1.1 maximum_convert_fusion
  59.1 18.7 %all-to-all-done.1 = bf16[128,12,128]{2,1,0:T(8,128)(2,1)S(1)} async-done(((bf16[128,12,128]{2,1,0:T(8,128)(2,1)}), bf16[128,12,128]{2,1,0:T(8,128)(2,1)S(1)}, u32[]{:S(2)}, u32[]{:S(2)}) %all-to-all-start.1) | async-done | bytes 393248 | tf_op jit(solution)/shard_map/all_to_all | solution.py:57
  79.5 8.5 %all-to-all-start.2 = ((bf16[4,80,2,3,128]{4,1,3,2,0:T(8,128)(2,1)}), bf16[4,80,2,3,128]{4,1,3,2,0:T(8,128)(2,1)S(1)}, u32[]{:S(2)}, u32[]{:S(2)}) async-start(bf16[4,80,2,3,128]{4,1,3,2,0:T(8,128)(2,1)} %copy.51), calls=%async_computation.2 | async-start | bytes 983040 | tf_op jit(solution)/shard_map/all_to_all | solution.py:118
  88.8 8.3 %all-to-all-done.2 = bf16[4,80,2,3,128]{4,1,3,2,0:T(8,128)(2,1)S(1)} async-done(((bf16[4,80,2,3,128]{4,1,3,2,0:T(8,128)(2,1)}), bf16[4,80,2,3,128]{4,1,3,2,0:T(8,128)(2,1)S(1)}, u32[]{:S(2)}, u32[]{:S(2)}) %all-to-all-start.2) | async-done | bytes 491552 | tf_op jit(solution)/shard_map/all_to_all | solution.py:118
  99.3 1.4 gather_fusion.1
  101.7 1.4 multiply_add_fusion
  103.1 5.8 %convolution_reduce-precision_fusion = f32[576,1024]{1,0:T(8,128)} fusion(bf16[1024,448]{1,0:T(8,128)(2,1)} %pad_maximum_fusion, f32[576,448]{0,1:T(8,128)} %maximum_convert_fusion, f32[576,512]{1,0:T(8,128)} %bitcast.95, f32[576,512]{1,0:T(8,128)S(1)} %bitcast.94, f32[576]{0:T(1024)S(1)} %mul.259, f32[448]{0:T(512)S(1)} %and_convert_fusion, f32[576]{0:T(1024)S(1)} %mul.262), kind=kOutput, calls=%fused_computation.22 | convolution fusion | flops 1060356096 | bytes 6674688 | tf_op jit(solution)/shard_map/dot_general | solution.py:151
  108.9 2.4 %add_reduce_fusion = (bf16[3,64,512]{2,1,0:T(8,128)(2,1)S(1)}, bf16[3,64,512]{2,1,0:T(8,128)(2,1)S(1)}, f32[3,64,512]{2,1,0:T(8,128)S(1)}, f32[3,64,512]{2,1,0:T(8,128)S(1)}) fusion(f32[3,3,64,1024]{3,2,1,0:T(8,128)} %bitcast.87, f32[3,64,512]{2,1,0:T(8,128)S(1)} %bitcast.86, f32[3,64,512]{2,1,0:T(8,128)S(1)} %bitcast.84, f32[3,64,512]{2,1,0:T(8,128)S(1)} %bitcast.80, ...), kind=kLoop, calls=%fused_computation.30 | loop fusion | flops 4325376 | bytes 5111808 | tf_op jit(solution)/shard_map/reduce_sum | solution.py:161
  111.5 11.2 %all_to_all.34 = bf16[4,64,2,3,128]{4,1,3,2,0:T(8,128)(2,1)S(1)} all-to-all(bf16[4,64,2,3,128]{4,1,3,2,0:T(8,128)(2,1)S(1)} %copy.56), channel_id=1, replica_groups=mesh['blk'=128,'frq'=4] {'frq'}, dimensions={0} | all-to-all | bytes 786432 | tf_op jit(solution)/shard_map/all_to_all | solution.py:188
  123.0 1.1 reshape_reshape.11
  124.1 6.4 %all-to-all-start.4 = ((bf16[128,12,128]{2,1,0:T(8,128)(2,1)}), bf16[128,12,128]{2,1,0:T(8,128)(2,1)S(1)}, u32[]{:S(2)}, u32[]{:S(2)}) async-start(bf16[128,12,128]{2,1,0:T(8,128)(2,1)} %reshape_reshape.11), calls=%async_computation.4 | async-start | bytes 1048576 | tf_op jit(solution)/shard_map/all_to_all | solution.py:57
  130.5 8.6 %sine_multiply_fusion = (f32[512,1024]{1,0:T(8,128)S(1)}, f32[512,1024]{1,0:T(8,128)S(1)}, f32[512,1024]{1,0:T(8,128)S(1)}) fusion(s32[512]{0:T(512)S(1)} %multiply_add_fusion.1), kind=kLoop, calls=%fused_computation.14 | loop fusion | flops 8912896 | bytes 6293504 | tf_op jit(solution)/shard_map/div | solution.py:174
  139.8 2.7 %fusion = f32[1024,48]{0,1:T(8,128)S(1)} fusion(f32[1024,48]{0,1:T(8,128)S(1)} %bitcast.96, f32[512,1024]{1,0:T(8,128)S(1)} %get-tuple-element.28, f32[512,1024]{1,0:T(8,128)S(1)} %get-tuple-element.29), kind=kOutput, calls=%fused_computation.2 | convolution fusion | flops 605028352 | bytes 4587520 | tf_op jit(solution)/shard_map/dot_general | solution.py:176
  142.6 18.1 %all-to-all-done.4 = bf16[128,12,128]{2,1,0:T(8,128)(2,1)S(1)} async-done(((bf16[128,12,128]{2,1,0:T(8,128)(2,1)}), bf16[128,12,128]{2,1,0:T(8,128)(2,1)S(1)}, u32[]{:S(2)}, u32[]{:S(2)}) %all-to-all-start.4) | async-done | bytes 393248 | tf_op jit(solution)/shard_map/all_to_all | solution.py:57
  162.5 12.8 %all_to_all.35 = f32[4,256,3,16]{1,3,2,0:T(8,128)S(1)} all-to-all(f32[4,256,3,16]{1,3,2,0:T(8,128)S(1)} %copy.60), channel_id=1, replica_groups=mesh['blk'=128,'frq'=4] {'frq'}, dimensions={0} | all-to-all | bytes 393216 | tf_op jit(solution)/shard_map/all_to_all | solution.py:217
  (65 shorter events, 12.3 us)
Async XLA Ops:
  1.4 35.6 %all-to-all-start = ((s32[128,1,2]{2,1,0:T(1,128)}), s32[128,1,2]{2,1,0:T(1,128)S(1)}, u32[]{:S(2)}, u32[]{:S(2)}) async-start(s32[128,1,2]{2,1,0:T(1,128)} %bitcast.6), calls=%async_computation | async-start | bytes 131072 | tf_op jit(solution)/shard_map/all_to_all | solution.py:81
  40.2 7.3 %copy-start.1 = (bf16[64,3,3,1024]{3,0,2,1:T(8,128)(2,1)S(1)}, bf16[64,3,3,1024]{3,0,2,1:T(8,128)(2,1)}, u32[]{:S(2)}) copy-start(bf16[64,3,3,1024]{3,0,2,1:T(8,128)(2,1)} %param.6) | copy-start | bytes 3538948
  41.3 36.5 %all-to-all-start.1 = ((bf16[128,12,128]{2,1,0:T(8,128)(2,1)}), bf16[128,12,128]{2,1,0:T(8,128)(2,1)S(1)}, u32[]{:S(2)}, u32[]{:S(2)}) async-start(bf16[128,12,128]{2,1,0:T(8,128)(2,1)} %reshape_reshape.9), calls=%async_computation.1 | async-start | bytes 1048576 | tf_op jit(solution)/shard_map/all_to_all | solution.py:57
  78.6 9.4 %copy-start.2 = (s32[1,128,2]{1,2,0:T(2,128)S(1)}, s32[1,128,2]{1,2,0:T(2,128)}, u32[]{:S(2)}) copy-start(s32[1,128,2]{1,2,0:T(2,128)} %param.7) | copy-start | bytes 3076
  78.6 9.6 %copy-start.3 = (s32[1,128]{1,0:T(1,128)S(1)}, s32[1,128]{1,0:T(1,128)}, u32[]{:S(2)}) copy-start(s32[1,128]{1,0:T(1,128)} %param.9) | copy-start | bytes 1540
  79.5 17.6 %all-to-all-start.2 = ((bf16[4,80,2,3,128]{4,1,3,2,0:T(8,128)(2,1)}), bf16[4,80,2,3,128]{4,1,3,2,0:T(8,128)(2,1)S(1)}, u32[]{:S(2)}, u32[]{:S(2)}) async-start(bf16[4,80,2,3,128]{4,1,3,2,0:T(8,128)(2,1)} %copy.51), calls=%async_computation.2 | async-start | bytes 983040 | tf_op jit(solution)/shard_map/all_to_all | solution.py:118
  97.5 0.9 copy-start
  98.4 0.9 slice-start
  124.1 36.5 %all-to-all-start.4 = ((bf16[128,12,128]{2,1,0:T(8,128)(2,1)}), bf16[128,12,128]{2,1,0:T(8,128)(2,1)S(1)}, u32[]{:S(2)}, u32[]{:S(2)}) async-start(bf16[128,12,128]{2,1,0:T(8,128)(2,1)} %reshape_reshape.11), calls=%async_computation.4 | async-start | bytes 1048576 | tf_op jit(solution)/shard_map/all_to_all | solution.py:57

commit v7 on v6

--- a/solution.py
+++ b/solution.py
@@ -79,7 +79,12 @@
         .astype(jnp.float32)
     )
     asked_ids = lax.all_to_all(partner_local, "blk", split_axis=0, concat_axis=0, tiled=True)
-    asked_rows = jnp.take(spec_rows, asked_ids.reshape(slot_total), axis=0, mode="clip")
+    asked_onehot = (
+        asked_ids.reshape(slot_total)[:, None] == lax.iota(jnp.int32, per_block)[None, :]
+    ).astype(spectra.dtype)
+    asked_rows = jnp.dot(
+        asked_onehot, spec_rows.reshape(per_block, -1), preferred_element_type=jnp.float32
+    ).astype(spectra.dtype)
     rows_new = blk_exchange(asked_rows.reshape(block_total, -1)).reshape(
         band_total, item_count, 2, 3, freq_dev
     )
@@ -121,9 +126,15 @@
     )
     second_rows = whole_band[:, :, :item_count].astype(jnp.float32)
     own_group = lax.dynamic_slice_in_dim(own_ids, band_index * item_count, item_count)
-    first_rows = jnp.take(
-        whole_band[:, :, item_count:], own_group, axis=2, mode="clip"
-    ).astype(jnp.float32)
+    group_onehot = (own_group[:, None] == lax.iota(jnp.int32, per_block)[None, :]).astype(
+        whole_band.dtype
+    )
+    first_rows = jnp.einsum(
+        "pn,rcnk->rcpk",
+        group_onehot,
+        whole_band[:, :, item_count:],
+        preferred_element_type=jnp.float32,
+    )
     alive_band = lax.dynamic_slice_in_dim(alive_mask, band_index * item_count, item_count)
     first_re = first_rows[0][:, None]
     first_im = first_rows[1][:, None]

time: 176 us -> 171 us (0.972)
  local copies, waits for them, and re-layouts: 14.7 us -> 9.24 us
    gather x3 -> x0, local copies, waits for them, and re-layouts: 3.07 us -> none  [the longest x2 1.68 us: local(): jnp.take(spec_rows, asked_ids.reshape(slot_total), axis=0, mode='clip')]
    slice x6 -> x0, local copies, waits for them, and re-layouts: 2.09 us -> none  [the longest x2 0.82 us: local(): whole_band[:, :, item_count:]]
  transfers between devices with their start and end apart: 4 -> 4, of which waited for: 4 -> 4; matrix products, arithmetic and copies ran while one was open for 14% -> 15% of each run, Pallas kernels for 0% -> 0%
where the time goes in v7:
time: 171 us; the launch traced here: 170 us
  waiting for transfers between devices  58.5 us (34%)
  starting transfers between devices  42.6 us (25%)
  other arithmetic  25.4 us (15%)
  blocking collectives  23.9 us (14%)
  matrix products  10.5 us (6%)
  local copies, waits for them, and re-layouts  9.24 us (5%)
    all_to_all x2, waiting for transfers between devices, blk_exchange(): lax.all_to_all(chunks.reshape(count, width // 128, 128), 'blk', split_axi...  36.8 us
    all_to_all x1, starting transfers between devices, local(): lax.all_to_all(partner_local, 'blk', split_axis=0, concat_axis=0, tiled=T...  21.3 us
    all_to_all x1, waiting for transfers between devices, local(): lax.all_to_all(partner_local, 'blk', split_axis=0, concat_axis=0, tiled=T...  13.4 us
    all_to_all x1, blocking collectives, local(): lax.all_to_all(product.reshape(band_total, NT // band_total, 3, per_block...  12.8 us
    all_to_all x2, starting transfers between devices, blk_exchange(): lax.all_to_all(chunks.reshape(count, width // 128, 128), 'blk', split_axi...  12.6 us
    all_to_all x1, blocking collectives, local(): lax.all_to_all(back_sent, 'frq', split_axis=0, concat_axis=0, tiled=True)  11.2 us
    all_to_all x1, starting transfers between devices, local(): lax.all_to_all(sent, 'frq', split_axis=0, concat_axis=0, tiled=True)  8.66 us
    div x1, other arithmetic, local(): sin_full = jnp.sin(phase_full) / math.sqrt(NF)  8.6 us
  transfers between devices with their start and end apart: 4, of which 4 were waited for; matrix products, arithmetic and copies ran while one was open for 15% of the time, Pallas kernels for 0%

profile of v7, /device:TPU:1, one launch (start us, length us, event | category | flops | bytes accessed | tf_op | source)
XLA Modules:
  0.0 170.4 jit_solution(15812205214003893671)
XLA Ops:
  0.0 1.4 copy.39
  1.4 21.3 %all-to-all-start = ((s32[128,1,2]{2,1,0:T(1,128)}), s32[128,1,2]{2,1,0:T(1,128)S(1)}, u32[]{:S(2)}, u32[]{:S(2)}) async-start(s32[128,1,2]{2,1,0:T(1,128)} %bitcast.5), calls=%async_computation | async-start | bytes 131072 | tf_op jit(solution)/shard_map/all_to_all | solution.py:81
  23.5 13.4 %all-to-all-done = s32[128,1,2]{2,1,0:T(1,128)S(1)} async-done(((s32[128,1,2]{2,1,0:T(1,128)}), s32[128,1,2]{2,1,0:T(1,128)S(1)}, u32[]{:S(2)}, u32[]{:S(2)}) %all-to-all-start) | async-done | bytes 1056 | tf_op jit(solution)/shard_map/all_to_all | solution.py:81
  37.4 0.8 reduce.3
  38.7 1.2 reshape_reshape.9
  39.9 6.2 %all-to-all-start.1 = ((bf16[128,12,128]{2,1,0:T(8,128)(2,1)}), bf16[128,12,128]{2,1,0:T(8,128)(2,1)S(1)}, u32[]{:S(2)}, u32[]{:S(2)}) async-start(bf16[128,12,128]{2,1,0:T(8,128)(2,1)} %reshape_reshape.9), calls=%async_computation.1 | async-start | bytes 1048576 | tf_op jit(solution)/shard_map/all_to_all | solution.py:57
  46.9 4.3 %fusion.31 = bf16[512,448]{1,0:T(8,128)(2,1)S(1)} fusion(s32[448]{0:T(512)S(1)} %pad_add_fusion, s32[512]{0:T(512)S(1)} %multiply_add_fusion.1), kind=kLoop, calls=%fused_computation.57 | loop fusion | flops 4358144 | bytes 462592 | tf_op jit(solution)/shard_map/neg | solution.py:104
  51.1 4.2 %multiply_convert_fusion.1 = bf16[512,448]{1,0:T(8,128)(2,1)S(1)} fusion(s32[448]{0:T(512)S(1)} %pad_add_fusion, s32[512]{0:T(512)S(1)} %multiply_add_fusion.1), kind=kLoop, calls=%fused_computation.48 | loop fusion | flops 3670016 | bytes 462592 | tf_op jit(solution)/shard_map/convert_element_type | solution.py:103
  55.4 1.2 pad_maximum_fusion
  56.5 1.1 maximum_convert_fusion
  57.6 18.6 %all-to-all-done.1 = bf16[128,12,128]{2,1,0:T(8,128)(2,1)S(1)} async-done(((bf16[128,12,128]{2,1,0:T(8,128)(2,1)}), bf16[128,12,128]{2,1,0:T(8,128)(2,1)S(1)}, u32[]{:S(2)}, u32[]{:S(2)}) %all-to-all-start.1) | async-done | bytes 393248 | tf_op jit(solution)/shard_map/all_to_all | solution.py:57
  77.0 0.9 copy.42
  77.9 8.7 %all-to-all-start.2 = ((bf16[4,80,2,3,128]{4,1,3,2,0:T(8,128)(2,1)}), bf16[4,80,2,3,128]{4,1,3,2,0:T(8,128)(2,1)S(1)}, u32[]{:S(2)}, u32[]{:S(2)}) async-start(bf16[4,80,2,3,128]{4,1,3,2,0:T(8,128)(2,1)} %copy.42), calls=%async_computation.2 | async-start | bytes 983040 | tf_op jit(solution)/shard_map/all_to_all | solution.py:123
  87.3 8.3 %all-to-all-done.2 = bf16[4,80,2,3,128]{4,1,3,2,0:T(8,128)(2,1)S(1)} async-done(((bf16[4,80,2,3,128]{4,1,3,2,0:T(8,128)(2,1)}), bf16[4,80,2,3,128]{4,1,3,2,0:T(8,128)(2,1)S(1)}, u32[]{:S(2)}, u32[]{:S(2)}) %all-to-all-start.2) | async-done | bytes 491552 | tf_op jit(solution)/shard_map/all_to_all | solution.py:123
  96.3 1.4 multiply_add_fusion
  97.7 5.8 %convolution_reduce-precision_fusion = f32[576,1024]{1,0:T(8,128)} fusion(bf16[1024,448]{1,0:T(8,128)(2,1)} %pad_maximum_fusion, f32[576,448]{0,1:T(8,128)} %maximum_convert_fusion, f32[576,512]{1,0:T(8,128)} %bitcast.87, f32[576,512]{1,0:T(8,128)S(1)} %bitcast.86, f32[576]{0:T(1024)S(1)} %mul.259, f32[448]{0:T(512)S(1)} %and_convert_fusion, f32[576]{0:T(1024)S(1)} %mul.262), kind=kOutput, calls=%fused_computation.20 | convolution fusion | flops 1060356096 | bytes 6674688 | tf_op jit(solution)/shard_map/dot_general | solution.py:162
  103.5 2.4 %add_reduce_fusion = (bf16[3,64,512]{2,1,0:T(8,128)(2,1)S(1)}, bf16[3,64,512]{2,1,0:T(8,128)(2,1)S(1)}, f32[3,64,512]{2,1,0:T(8,128)S(1)}, f32[3,64,512]{2,1,0:T(8,128)S(1)}) fusion(f32[3,3,64,1024]{3,2,1,0:T(8,128)} %bitcast.80, f32[3,64,512]{2,1,0:T(8,128)S(1)} %get-tuple-element.24, f32[3,64,512]{2,1,0:T(8,128)S(1)} %get-tuple-element.23, ...), kind=kLoop, calls=%fused_computation.30 | loop fusion | flops 4325376 | bytes 5111808 | tf_op jit(solution)/shard_map/reduce_sum | solution.py:172
  106.1 11.2 %all_to_all.34 = bf16[4,64,2,3,128]{4,1,3,2,0:T(8,128)(2,1)S(1)} all-to-all(bf16[4,64,2,3,128]{4,1,3,2,0:T(8,128)(2,1)S(1)} %copy.45), channel_id=1, replica_groups=mesh['blk'=128,'frq'=4] {'frq'}, dimensions={0} | all-to-all | bytes 786432 | tf_op jit(solution)/shard_map/all_to_all | solution.py:199
  117.6 1.1 reshape_reshape.11
  118.7 6.4 %all-to-all-start.4 = ((bf16[128,12,128]{2,1,0:T(8,128)(2,1)}), bf16[128,12,128]{2,1,0:T(8,128)(2,1)S(1)}, u32[]{:S(2)}, u32[]{:S(2)}) async-start(bf16[128,12,128]{2,1,0:T(8,128)(2,1)} %reshape_reshape.11), calls=%async_computation.4 | async-start | bytes 1048576 | tf_op jit(solution)/shard_map/all_to_all | solution.py:57
  125.1 8.6 %sine_multiply_fusion = (f32[512,1024]{1,0:T(8,128)S(1)}, f32[512,1024]{1,0:T(8,128)S(1)}, f32[512,1024]{1,0:T(8,128)S(1)}) fusion(s32[512]{0:T(512)S(1)} %multiply_add_fusion.1), kind=kLoop, calls=%fused_computation.12 | loop fusion | flops 8912896 | bytes 6293504 | tf_op jit(solution)/shard_map/div | solution.py:185
  134.4 2.7 %fusion = f32[1024,48]{0,1:T(8,128)S(1)} fusion(f32[1024,48]{0,1:T(8,128)S(1)} %bitcast.88, f32[512,1024]{1,0:T(8,128)S(1)} %get-tuple-element.28, f32[512,1024]{1,0:T(8,128)S(1)} %get-tuple-element.29), kind=kOutput, calls=%fused_computation | convolution fusion | flops 605028352 | bytes 4587520 | tf_op jit(solution)/shard_map/dot_general | solution.py:187
  137.1 18.1 %all-to-all-done.4 = bf16[128,12,128]{2,1,0:T(8,128)(2,1)S(1)} async-done(((bf16[128,12,128]{2,1,0:T(8,128)(2,1)}), bf16[128,12,128]{2,1,0:T(8,128)(2,1)S(1)}, u32[]{:S(2)}, u32[]{:S(2)}) %all-to-all-start.4) | async-done | bytes 393248 | tf_op jit(solution)/shard_map/all_to_all | solution.py:57
  157.0 12.8 %all_to_all.35 = f32[4,256,3,16]{1,3,2,0:T(8,128)S(1)} all-to-all(f32[4,256,3,16]{1,3,2,0:T(8,128)S(1)} %copy.49), channel_id=1, replica_groups=mesh['blk'=128,'frq'=4] {'frq'}, dimensions={0} | all-to-all | bytes 393216 | tf_op jit(solution)/shard_map/all_to_all | solution.py:228
  (52 shorter events, 8.2 us)
Async XLA Ops:
  1.4 35.5 %all-to-all-start = ((s32[128,1,2]{2,1,0:T(1,128)}), s32[128,1,2]{2,1,0:T(1,128)S(1)}, u32[]{:S(2)}, u32[]{:S(2)}) async-start(s32[128,1,2]{2,1,0:T(1,128)} %bitcast.5), calls=%async_computation | async-start | bytes 131072 | tf_op jit(solution)/shard_map/all_to_all | solution.py:81
  38.4 7.7 %copy-start = (bf16[64,3,3,1024]{3,0,2,1:T(8,128)(2,1)S(1)}, bf16[64,3,3,1024]{3,0,2,1:T(8,128)(2,1)}, u32[]{:S(2)}) copy-start(bf16[64,3,3,1024]{3,0,2,1:T(8,128)(2,1)} %param.6) | copy-start | bytes 3538948
  39.9 36.4 %all-to-all-start.1 = ((bf16[128,12,128]{2,1,0:T(8,128)(2,1)}), bf16[128,12,128]{2,1,0:T(8,128)(2,1)S(1)}, u32[]{:S(2)}, u32[]{:S(2)}) async-start(bf16[128,12,128]{2,1,0:T(8,128)(2,1)} %reshape_reshape.9), calls=%async_computation.1 | async-start | bytes 1048576 | tf_op jit(solution)/shard_map/all_to_all | solution.py:57
  77.0 9.5 %copy-start.1 = (s32[1,128,2]{1,2,0:T(2,128)S(1)}, s32[1,128,2]{1,2,0:T(2,128)}, u32[]{:S(2)}) copy-start(s32[1,128,2]{1,2,0:T(2,128)} %param.7) | copy-start | bytes 3076
  77.0 9.8 %copy-start.2 = (s32[1,128]{1,0:T(1,128)S(1)}, s32[1,128]{1,0:T(1,128)}, u32[]{:S(2)}) copy-start(s32[1,128]{1,0:T(1,128)} %param.9) | copy-start | bytes 1540
  77.9 17.8 %all-to-all-start.2 = ((bf16[4,80,2,3,128]{4,1,3,2,0:T(8,128)(2,1)}), bf16[4,80,2,3,128]{4,1,3,2,0:T(8,128)(2,1)S(1)}, u32[]{:S(2)}, u32[]{:S(2)}) async-start(bf16[4,80,2,3,128]{4,1,3,2,0:T(8,128)(2,1)} %copy.42), calls=%async_computation.2 | async-start | bytes 983040 | tf_op jit(solution)/shard_map/all_to_all | solution.py:123
  118.7 36.6 %all-to-all-start.4 = ((bf16[128,12,128]{2,1,0:T(8,128)(2,1)}), bf16[128,12,128]{2,1,0:T(8,128)(2,1)S(1)}, u32[]{:S(2)}, u32[]{:S(2)}) async-start(bf16[128,12,128]{2,1,0:T(8,128)(2,1)} %reshape_reshape.11), calls=%async_computation.4 | async-start | bytes 1048576 | tf_op jit(solution)/shard_map/all_to_all | solution.py:57

commit v8 on v7

--- a/solution.py
+++ b/solution.py
@@ -55,7 +55,7 @@
 def blk_exchange(chunks):
     count, width = chunks.shape
     moved = lax.all_to_all(
-        chunks.reshape(count, width // 128, 128), "blk", split_axis=0, concat_axis=0, tiled=True
+        chunks.reshape(count, 4, width // 4), "blk", split_axis=0, concat_axis=0, tiled=True
     )
     return moved.reshape(count, width)
 

time: 171 us -> 160 us (0.936)
  waiting for transfers between devices: 58.5 us -> 47.3 us
    all_to_all x2, waiting for transfers between devices: 36.8 us -> 25.7 us  [blk_exchange(): lax.all_to_all(chunks.reshape(count, 4, width // 4), 'blk', split_axis=0,...]
  transfers between devices with their start and end apart: 4 -> 4, of which waited for: 4 -> 4; matrix products, arithmetic and copies ran while one was open for 15% -> 16% of each run, Pallas kernels for 0% -> 0%
where the time goes in v8:
time: 160 us; the launch traced here: 159 us
  waiting for transfers between devices  47.3 us (30%)
  starting transfers between devices  43.4 us (27%)
  other arithmetic  25.4 us (16%)
  blocking collectives  23.3 us (15%)
  matrix products  10.5 us (7%)
  local copies, waits for them, and re-layouts  8.9 us (6%)
    all_to_all x2, waiting for transfers between devices, blk_exchange(): lax.all_to_all(chunks.reshape(count, 4, width // 4), 'blk', split_axis=0,...  25.7 us
    all_to_all x1, starting transfers between devices, local(): lax.all_to_all(partner_local, 'blk', split_axis=0, concat_axis=0, tiled=T...  21.3 us
    all_to_all x1, waiting for transfers between devices, local(): lax.all_to_all(partner_local, 'blk', split_axis=0, concat_axis=0, tiled=T...  13.3 us
    all_to_all x2, starting transfers between devices, blk_exchange(): lax.all_to_all(chunks.reshape(count, 4, width // 4), 'blk', split_axis=0,...  12.5 us
    all_to_all x1, blocking collectives, local(): lax.all_to_all(product.reshape(band_total, NT // band_total, 3, per_block...  12.1 us
    all_to_all x1, blocking collectives, local(): lax.all_to_all(back_sent, 'frq', split_axis=0, concat_axis=0, tiled=True)  11.2 us
    all_to_all x1, starting transfers between devices, local(): lax.all_to_all(sent, 'frq', split_axis=0, concat_axis=0, tiled=True)  9.54 us
    div x1, other arithmetic, local(): sin_full = jnp.sin(phase_full) / math.sqrt(NF)  8.6 us
  transfers between devices with their start and end apart: 4, of which 4 were waited for; matrix products, arithmetic and copies ran while one was open for 16% of the time, Pallas kernels for 0%

profile of v8, /device:TPU:1, one launch (start us, length us, event | category | flops | bytes accessed | tf_op | source)
XLA Modules:
  0.0 159.2 jit_solution(13450147851149790136)
XLA Ops:
  0.0 1.4 copy.39
  1.4 21.3 %all-to-all-start = ((s32[128,1,2]{2,1,0:T(1,128)}), s32[128,1,2]{2,1,0:T(1,128)S(1)}, u32[]{:S(2)}, u32[]{:S(2)}) async-start(s32[128,1,2]{2,1,0:T(1,128)} %bitcast.5), calls=%async_computation | async-start | bytes 131072 | tf_op jit(solution)/shard_map/all_to_all | solution.py:81
  22.8 0.8 copy.40
  23.6 13.3 %all-to-all-done = s32[128,1,2]{2,1,0:T(1,128)S(1)} async-done(((s32[128,1,2]{2,1,0:T(1,128)}), s32[128,1,2]{2,1,0:T(1,128)S(1)}, u32[]{:S(2)}, u32[]{:S(2)}) %all-to-all-start) | async-done | bytes 1056 | tf_op jit(solution)/shard_map/all_to_all | solution.py:81
  38.7 1.0 reshape_reshape.9
  39.7 6.2 %all-to-all-start.1 = ((bf16[128,4,384]{2,1,0:T(4,128)(2,1)}), bf16[128,4,384]{2,1,0:T(4,128)(2,1)S(1)}, u32[]{:S(2)}, u32[]{:S(2)}) async-start(bf16[128,4,384]{2,1,0:T(4,128)(2,1)} %reshape_reshape.9), calls=%async_computation.1 | async-start | bytes 786432 | tf_op jit(solution)/shard_map/all_to_all | solution.py:57
  46.7 4.3 %fusion.31 = bf16[512,448]{1,0:T(8,128)(2,1)S(1)} fusion(s32[448]{0:T(512)S(1)} %pad_add_fusion, s32[512]{0:T(512)S(1)} %multiply_add_fusion.1), kind=kLoop, calls=%fused_computation.57 | loop fusion | flops 4358144 | bytes 462592 | tf_op jit(solution)/shard_map/neg | solution.py:104
  50.9 4.2 %multiply_convert_fusion.1 = bf16[512,448]{1,0:T(8,128)(2,1)S(1)} fusion(s32[448]{0:T(512)S(1)} %pad_add_fusion, s32[512]{0:T(512)S(1)} %multiply_add_fusion.1), kind=kLoop, calls=%fused_computation.48 | loop fusion | flops 3670016 | bytes 462592 | tf_op jit(solution)/shard_map/convert_element_type | solution.py:103
  55.2 1.2 pad_maximum_fusion
  56.4 1.1 maximum_convert_fusion
  57.4 12.4 %all-to-all-done.1 = bf16[128,4,384]{2,1,0:T(4,128)(2,1)S(1)} async-done(((bf16[128,4,384]{2,1,0:T(4,128)(2,1)}), bf16[128,4,384]{2,1,0:T(4,128)(2,1)S(1)}, u32[]{:S(2)}, u32[]{:S(2)}) %all-to-all-start.1) | async-done | bytes 393248 | tf_op jit(solution)/shard_map/all_to_all | solution.py:57
  70.4 0.9 copy.42
  71.3 9.5 %all-to-all-start.2 = ((bf16[4,80,2,3,128]{4,1,3,2,0:T(8,128)(2,1)}), bf16[4,80,2,3,128]{4,1,3,2,0:T(8,128)(2,1)S(1)}, u32[]{:S(2)}, u32[]{:S(2)}) async-start(bf16[4,80,2,3,128]{4,1,3,2,0:T(8,128)(2,1)} %copy.42), calls=%async_computation.2 | async-start | bytes 983040 | tf_op jit(solution)/shard_map/all_to_all | solution.py:123
  81.7 8.3 %all-to-all-done.2 = bf16[4,80,2,3,128]{4,1,3,2,0:T(8,128)(2,1)S(1)} async-done(((bf16[4,80,2,3,128]{4,1,3,2,0:T(8,128)(2,1)}), bf16[4,80,2,3,128]{4,1,3,2,0:T(8,128)(2,1)S(1)}, u32[]{:S(2)}, u32[]{:S(2)}) %all-to-all-start.2) | async-done | bytes 491552 | tf_op jit(solution)/shard_map/all_to_all | solution.py:123
  90.6 1.4 multiply_add_fusion
  92.0 5.8 %convolution_reduce-precision_fusion = f32[576,1024]{1,0:T(8,128)} fusion(bf16[1024,448]{1,0:T(8,128)(2,1)} %pad_maximum_fusion, f32[576,448]{0,1:T(8,128)} %maximum_convert_fusion, f32[576,512]{1,0:T(8,128)} %bitcast.87, f32[576,512]{1,0:T(8,128)S(1)} %bitcast.86, f32[576]{0:T(1024)S(1)} %mul.259, f32[448]{0:T(512)S(1)} %and_convert_fusion, f32[576]{0:T(1024)S(1)} %mul.262), kind=kOutput, calls=%fused_computation.20 | convolution fusion | flops 1060356096 | bytes 6674688 | tf_op jit(solution)/shard_map/dot_general | solution.py:162
  97.8 2.4 %add_reduce_fusion = (bf16[3,64,512]{2,1,0:T(8,128)(2,1)S(1)}, bf16[3,64,512]{2,1,0:T(8,128)(2,1)S(1)}, f32[3,64,512]{2,1,0:T(8,128)S(1)}, f32[3,64,512]{2,1,0:T(8,128)S(1)}) fusion(f32[3,3,64,1024]{3,2,1,0:T(8,128)} %bitcast.80, f32[3,64,512]{2,1,0:T(8,128)S(1)} %get-tuple-element.24, f32[3,64,512]{2,1,0:T(8,128)S(1)} %get-tuple-element.23, ...), kind=kLoop, calls=%fused_computation.30 | loop fusion | flops 4325376 | bytes 5111808 | tf_op jit(solution)/shard_map/reduce_sum | solution.py:172
  100.4 11.2 %all_to_all.34 = bf16[4,64,2,3,128]{4,1,3,2,0:T(8,128)(2,1)S(1)} all-to-all(bf16[4,64,2,3,128]{4,1,3,2,0:T(8,128)(2,1)S(1)} %copy.45), channel_id=1, replica_groups=mesh['blk'=128,'frq'=4] {'frq'}, dimensions={0} | all-to-all | bytes 786432 | tf_op jit(solution)/shard_map/all_to_all | solution.py:199
  111.9 1.1 reshape_reshape.11
  113.0 6.4 %all-to-all-start.4 = ((bf16[128,4,384]{2,1,0:T(4,128)(2,1)}), bf16[128,4,384]{2,1,0:T(4,128)(2,1)S(1)}, u32[]{:S(2)}, u32[]{:S(2)}) async-start(bf16[128,4,384]{2,1,0:T(4,128)(2,1)} %reshape_reshape.11), calls=%async_computation.4 | async-start | bytes 786432 | tf_op jit(solution)/shard_map/all_to_all | solution.py:57
  119.4 8.6 %sine_multiply_fusion = (f32[512,1024]{1,0:T(8,128)S(1)}, f32[512,1024]{1,0:T(8,128)S(1)}, f32[512,1024]{1,0:T(8,128)S(1)}) fusion(s32[512]{0:T(512)S(1)} %multiply_add_fusion.1), kind=kLoop, calls=%fused_computation.12 | loop fusion | flops 8912896 | bytes 6293504 | tf_op jit(solution)/shard_map/div | solution.py:185
  128.7 2.7 %fusion = f32[1024,48]{0,1:T(8,128)S(1)} fusion(f32[1024,48]{0,1:T(8,128)S(1)} %bitcast.88, f32[512,1024]{1,0:T(8,128)S(1)} %get-tuple-element.28, f32[512,1024]{1,0:T(8,128)S(1)} %get-tuple-element.29), kind=kOutput, calls=%fused_computation | convolution fusion | flops 605028352 | bytes 4587520 | tf_op jit(solution)/shard_map/dot_general | solution.py:187
  131.4 13.4 %all-to-all-done.4 = bf16[128,4,384]{2,1,0:T(4,128)(2,1)S(1)} async-done(((bf16[128,4,384]{2,1,0:T(4,128)(2,1)}), bf16[128,4,384]{2,1,0:T(4,128)(2,1)S(1)}, u32[]{:S(2)}, u32[]{:S(2)}) %all-to-all-start.4) | async-done | bytes 393248 | tf_op jit(solution)/shard_map/all_to_all | solution.py:57
  146.4 12.1 %all_to_all.35 = f32[4,256,3,16]{1,3,2,0:T(8,128)S(1)} all-to-all(f32[4,256,3,16]{1,3,2,0:T(8,128)S(1)} %copy.49), channel_id=1, replica_groups=mesh['blk'=128,'frq'=4] {'frq'}, dimensions={0} | all-to-all | bytes 393216 | tf_op jit(solution)/shard_map/all_to_all | solution.py:228
  (52 shorter events, 8.0 us)
Async XLA Ops:
  1.4 35.5 %all-to-all-start = ((s32[128,1,2]{2,1,0:T(1,128)}), s32[128,1,2]{2,1,0:T(1,128)S(1)}, u32[]{:S(2)}, u32[]{:S(2)}) async-start(s32[128,1,2]{2,1,0:T(1,128)} %bitcast.5), calls=%async_computation | async-start | bytes 131072 | tf_op jit(solution)/shard_map/all_to_all | solution.py:81
  22.7 23.1 %copy-start = (bf16[64,3,3,1024]{3,0,2,1:T(8,128)(2,1)S(1)}, bf16[64,3,3,1024]{3,0,2,1:T(8,128)(2,1)}, u32[]{:S(2)}) copy-start(bf16[64,3,3,1024]{3,0,2,1:T(8,128)(2,1)} %param.6) | copy-start | bytes 3538948
  39.7 30.1 %all-to-all-start.1 = ((bf16[128,4,384]{2,1,0:T(4,128)(2,1)}), bf16[128,4,384]{2,1,0:T(4,128)(2,1)S(1)}, u32[]{:S(2)}, u32[]{:S(2)}) async-start(bf16[128,4,384]{2,1,0:T(4,128)(2,1)} %reshape_reshape.9), calls=%async_computation.1 | async-start | bytes 786432 | tf_op jit(solution)/shard_map/all_to_all | solution.py:57
  70.4 10.4 %copy-start.1 = (s32[1,128,2]{1,2,0:T(2,128)S(1)}, s32[1,128,2]{1,2,0:T(2,128)}, u32[]{:S(2)}) copy-start(s32[1,128,2]{1,2,0:T(2,128)} %param.7) | copy-start | bytes 3076
  70.4 10.7 %copy-start.2 = (s32[1,128]{1,0:T(1,128)S(1)}, s32[1,128]{1,0:T(1,128)}, u32[]{:S(2)}) copy-start(s32[1,128]{1,0:T(1,128)} %param.9) | copy-start | bytes 1540
  71.3 18.7 %all-to-all-start.2 = ((bf16[4,80,2,3,128]{4,1,3,2,0:T(8,128)(2,1)}), bf16[4,80,2,3,128]{4,1,3,2,0:T(8,128)(2,1)S(1)}, u32[]{:S(2)}, u32[]{:S(2)}) async-start(bf16[4,80,2,3,128]{4,1,3,2,0:T(8,128)(2,1)} %copy.42), calls=%async_computation.2 | async-start | bytes 983040 | tf_op jit(solution)/shard_map/all_to_all | solution.py:123
  113.0 31.8 %all-to-all-start.4 = ((bf16[128,4,384]{2,1,0:T(4,128)(2,1)}), bf16[128,4,384]{2,1,0:T(4,128)(2,1)S(1)}, u32[]{:S(2)}, u32[]{:S(2)}) async-start(bf16[128,4,384]{2,1,0:T(4,128)(2,1)} %reshape_reshape.11), calls=%async_computation.4 | async-start | bytes 786432 | tf_op jit(solution)/shard_map/all_to_all | solution.py:57

commit v9 on v8

--- a/solution.py
+++ b/solution.py
@@ -195,7 +195,7 @@
     far_grad = jnp.transpose(jnp.stack([far_re, far_im]), (2, 0, 1, 3)).astype(jnp.bfloat16)
     back_sent = jnp.transpose(
         far_grad.reshape(item_count, 2, 3, band_total, freq_dev), (3, 0, 1, 2, 4)
-    )
+    ).reshape(band_total, item_count // slot_cap, 4, slot_cap * 2 * 3 * freq_dev // 4)
     band_back = lax.all_to_all(back_sent, "frq", split_axis=0, concat_axis=0, tiled=True)
     far_band = band_back.reshape(block_total, slot_cap * 2 * 3 * freq_dev)
     back_grad = blk_exchange(far_band).astype(jnp.float32)

time: 160 us -> 159 us (level)
  no operation moved by 1% of the time
where the time goes in v9:
time: 159 us
  waiting for transfers between devices  47.3 us (30%)
  starting transfers between devices  43.4 us (27%)
  other arithmetic  25.4 us (16%)
  blocking collectives  23.9 us (15%)
  matrix products  10.5 us (7%)
  local copies, waits for them, and re-layouts  8.08 us (5%)
    all_to_all x2, waiting for transfers between devices, blk_exchange(): lax.all_to_all(chunks.reshape(count, 4, width // 4), 'blk', split_axis=0,...  25.7 us
    all_to_all x1, starting transfers between devices, local(): lax.all_to_all(partner_local, 'blk', split_axis=0, concat_axis=0, tiled=T...  21.3 us
    all_to_all x1, waiting for transfers between devices, local(): lax.all_to_all(partner_local, 'blk', split_axis=0, concat_axis=0, tiled=T...  13.3 us
    all_to_all x2, starting transfers between devices, blk_exchange(): lax.all_to_all(chunks.reshape(count, 4, width // 4), 'blk', split_axis=0,...  12.5 us
    all_to_all x1, blocking collectives, local(): lax.all_to_all(product.reshape(band_total, NT // band_total, 3, per_block...  12.1 us
    all_to_all x1, blocking collectives, local(): lax.all_to_all(back_sent, 'frq', split_axis=0, concat_axis=0, tiled=True)  11.8 us
    all_to_all x1, starting transfers between devices, local(): lax.all_to_all(sent, 'frq', split_axis=0, concat_axis=0, tiled=True)  9.54 us
    div x1, other arithmetic, local(): sin_full = jnp.sin(phase_full) / math.sqrt(NF)  8.6 us
  transfers between devices with their start and end apart: 4, of which 4 were waited for; matrix products, arithmetic and copies ran while one was open for 16% of the time, Pallas kernels for 0%

profile of v9, /device:TPU:1, one launch (start us, length us, event | category | flops | bytes accessed | tf_op | source)
XLA Modules:
  0.0 159.0 jit_solution(7953319495853493082)
XLA Ops:
  0.0 1.4 copy.39
  1.4 21.3 %all-to-all-start = ((s32[128,1,2]{2,1,0:T(1,128)}), s32[128,1,2]{2,1,0:T(1,128)S(1)}, u32[]{:S(2)}, u32[]{:S(2)}) async-start(s32[128,1,2]{2,1,0:T(1,128)} %bitcast.5), calls=%async_computation | async-start | bytes 131072 | tf_op jit(solution)/shard_map/all_to_all | solution.py:81
  22.8 0.8 copy.40
  23.6 13.3 %all-to-all-done = s32[128,1,2]{2,1,0:T(1,128)S(1)} async-done(((s32[128,1,2]{2,1,0:T(1,128)}), s32[128,1,2]{2,1,0:T(1,128)S(1)}, u32[]{:S(2)}, u32[]{:S(2)}) %all-to-all-start) | async-done | bytes 1056 | tf_op jit(solution)/shard_map/all_to_all | solution.py:81
  37.4 0.8 reduce.3
  38.7 1.0 reshape_reshape.9
  39.7 6.2 %all-to-all-start.1 = ((bf16[128,4,384]{2,1,0:T(4,128)(2,1)}), bf16[128,4,384]{2,1,0:T(4,128)(2,1)S(1)}, u32[]{:S(2)}, u32[]{:S(2)}) async-start(bf16[128,4,384]{2,1,0:T(4,128)(2,1)} %reshape_reshape.9), calls=%async_computation.1 | async-start | bytes 786432 | tf_op jit(solution)/shard_map/all_to_all | solution.py:57
  46.7 4.3 %fusion.31 = bf16[512,448]{1,0:T(8,128)(2,1)S(1)} fusion(s32[448]{0:T(512)S(1)} %pad_add_fusion, s32[512]{0:T(512)S(1)} %multiply_add_fusion.1), kind=kLoop, calls=%fused_computation.57 | loop fusion | flops 4358144 | bytes 462592 | tf_op jit(solution)/shard_map/neg | solution.py:104
  50.9 4.2 %multiply_convert_fusion.1 = bf16[512,448]{1,0:T(8,128)(2,1)S(1)} fusion(s32[448]{0:T(512)S(1)} %pad_add_fusion, s32[512]{0:T(512)S(1)} %multiply_add_fusion.1), kind=kLoop, calls=%fused_computation.48 | loop fusion | flops 3670016 | bytes 462592 | tf_op jit(solution)/shard_map/convert_element_type | solution.py:103
  55.2 1.2 pad_maximum_fusion
  56.4 1.1 maximum_convert_fusion
  57.4 12.4 %all-to-all-done.1 = bf16[128,4,384]{2,1,0:T(4,128)(2,1)S(1)} async-done(((bf16[128,4,384]{2,1,0:T(4,128)(2,1)}), bf16[128,4,384]{2,1,0:T(4,128)(2,1)S(1)}, u32[]{:S(2)}, u32[]{:S(2)}) %all-to-all-start.1) | async-done | bytes 393248 | tf_op jit(solution)/shard_map/all_to_all | solution.py:57
  70.4 0.9 copy.42
  71.3 9.5 %all-to-all-start.2 = ((bf16[4,80,2,3,128]{4,1,3,2,0:T(8,128)(2,1)}), bf16[4,80,2,3,128]{4,1,3,2,0:T(8,128)(2,1)S(1)}, u32[]{:S(2)}, u32[]{:S(2)}) async-start(bf16[4,80,2,3,128]{4,1,3,2,0:T(8,128)(2,1)} %copy.42), calls=%async_computation.2 | async-start | bytes 983040 | tf_op jit(solution)/shard_map/all_to_all | solution.py:123
  81.7 8.3 %all-to-all-done.2 = bf16[4,80,2,3,128]{4,1,3,2,0:T(8,128)(2,1)S(1)} async-done(((bf16[4,80,2,3,128]{4,1,3,2,0:T(8,128)(2,1)}), bf16[4,80,2,3,128]{4,1,3,2,0:T(8,128)(2,1)S(1)}, u32[]{:S(2)}, u32[]{:S(2)}) %all-to-all-start.2) | async-done | bytes 491552 | tf_op jit(solution)/shard_map/all_to_all | solution.py:123
  90.6 1.4 multiply_add_fusion
  92.0 5.8 %convolution_reduce-precision_fusion = f32[576,1024]{1,0:T(8,128)} fusion(bf16[1024,448]{1,0:T(8,128)(2,1)} %pad_maximum_fusion, f32[576,448]{0,1:T(8,128)} %maximum_convert_fusion, f32[576,512]{1,0:T(8,128)} %bitcast.88, f32[576,512]{1,0:T(8,128)S(1)} %bitcast.87, f32[576]{0:T(1024)S(1)} %mul.259, f32[448]{0:T(512)S(1)} %and_convert_fusion, f32[576]{0:T(1024)S(1)} %mul.262), kind=kOutput, calls=%fused_computation.20 | convolution fusion | flops 1060356096 | bytes 6674688 | tf_op jit(solution)/shard_map/dot_general | solution.py:162
  97.8 2.4 %add_reduce_fusion = (bf16[3,64,512]{2,1,0:T(8,128)(2,1)S(1)}, bf16[3,64,512]{2,1,0:T(8,128)(2,1)S(1)}, f32[3,64,512]{2,1,0:T(8,128)S(1)}, f32[3,64,512]{2,1,0:T(8,128)S(1)}) fusion(f32[3,3,64,1024]{3,2,1,0:T(8,128)} %bitcast.81, f32[3,64,512]{2,1,0:T(8,128)S(1)} %get-tuple-element.24, f32[3,64,512]{2,1,0:T(8,128)S(1)} %get-tuple-element.23, ...), kind=kLoop, calls=%fused_computation.30 | loop fusion | flops 4325376 | bytes 5111808 | tf_op jit(solution)/shard_map/reduce_sum | solution.py:172
  101.0 11.8 %all_to_all.34 = bf16[4,32,4,384]{3,2,1,0:T(4,128)(2,1)} all-to-all(bf16[4,32,4,384]{3,2,1,0:T(4,128)(2,1)S(1)} %reshape.87), channel_id=1, replica_groups=mesh['blk'=128,'frq'=4] {'frq'}, dimensions={0} | all-to-all | bytes 786432 | tf_op jit(solution)/shard_map/all_to_all | solution.py:199
  112.9 6.4 %all-to-all-start.4 = ((bf16[128,4,384]{2,1,0:T(4,128)(2,1)}), bf16[128,4,384]{2,1,0:T(4,128)(2,1)S(1)}, u32[]{:S(2)}, u32[]{:S(2)}) async-start(bf16[128,4,384]{2,1,0:T(4,128)(2,1)} %bitcast.28), calls=%async_computation.4 | async-start | bytes 786432 | tf_op jit(solution)/shard_map/all_to_all | solution.py:57
  119.2 8.6 %sine_multiply_fusion = (f32[512,1024]{1,0:T(8,128)S(1)}, f32[512,1024]{1,0:T(8,128)S(1)}, f32[512,1024]{1,0:T(8,128)S(1)}) fusion(s32[512]{0:T(512)S(1)} %multiply_add_fusion.1), kind=kLoop, calls=%fused_computation.12 | loop fusion | flops 8912896 | bytes 6293504 | tf_op jit(solution)/shard_map/div | solution.py:185
  128.5 2.7 %fusion = f32[1024,48]{0,1:T(8,128)S(1)} fusion(f32[1024,48]{0,1:T(8,128)S(1)} %bitcast.89, f32[512,1024]{1,0:T(8,128)S(1)} %get-tuple-element.28, f32[512,1024]{1,0:T(8,128)S(1)} %get-tuple-element.29), kind=kOutput, calls=%fused_computation | convolution fusion | flops 605028352 | bytes 4587520 | tf_op jit(solution)/shard_map/dot_general | solution.py:187
  131.2 13.4 %all-to-all-done.4 = bf16[128,4,384]{2,1,0:T(4,128)(2,1)S(1)} async-done(((bf16[128,4,384]{2,1,0:T(4,128)(2,1)}), bf16[128,4,384]{2,1,0:T(4,128)(2,1)S(1)}, u32[]{:S(2)}, u32[]{:S(2)}) %all-to-all-start.4) | async-done | bytes 393248 | tf_op jit(solution)/shard_map/all_to_all | solution.py:57
  146.3 12.1 %all_to_all.35 = f32[4,256,3,16]{1,3,2,0:T(8,128)S(1)} all-to-all(f32[4,256,3,16]{1,3,2,0:T(8,128)S(1)} %copy.48), channel_id=1, replica_groups=mesh['blk'=128,'frq'=4] {'frq'}, dimensions={0} | all-to-all | bytes 393216 | tf_op jit(solution)/shard_map/all_to_all | solution.py:228
  (51 shorter events, 7.5 us)
Async XLA Ops:
  1.4 35.5 %all-to-all-start = ((s32[128,1,2]{2,1,0:T(1,128)}), s32[128,1,2]{2,1,0:T(1,128)S(1)}, u32[]{:S(2)}, u32[]{:S(2)}) async-start(s32[128,1,2]{2,1,0:T(1,128)} %bitcast.5), calls=%async_computation | async-start | bytes 131072 | tf_op jit(solution)/shard_map/all_to_all | solution.py:81
  22.7 23.1 %copy-start = (bf16[64,3,3,1024]{3,0,2,1:T(8,128)(2,1)S(1)}, bf16[64,3,3,1024]{3,0,2,1:T(8,128)(2,1)}, u32[]{:S(2)}) copy-start(bf16[64,3,3,1024]{3,0,2,1:T(8,128)(2,1)} %param.6) | copy-start | bytes 3538948
  39.7 30.1 %all-to-all-start.1 = ((bf16[128,4,384]{2,1,0:T(4,128)(2,1)}), bf16[128,4,384]{2,1,0:T(4,128)(2,1)S(1)}, u32[]{:S(2)}, u32[]{:S(2)}) async-start(bf16[128,4,384]{2,1,0:T(4,128)(2,1)} %reshape_reshape.9), calls=%async_computation.1 | async-start | bytes 786432 | tf_op jit(solution)/shard_map/all_to_all | solution.py:57
  70.4 10.4 %copy-start.1 = (s32[1,128,2]{1,2,0:T(2,128)S(1)}, s32[1,128,2]{1,2,0:T(2,128)}, u32[]{:S(2)}) copy-start(s32[1,128,2]{1,2,0:T(2,128)} %param.7) | copy-start | bytes 3076
  70.4 10.7 %copy-start.2 = (s32[1,128]{1,0:T(1,128)S(1)}, s32[1,128]{1,0:T(1,128)}, u32[]{:S(2)}) copy-start(s32[1,128]{1,0:T(1,128)} %param.9) | copy-start | bytes 1540
  71.3 18.7 %all-to-all-start.2 = ((bf16[4,80,2,3,128]{4,1,3,2,0:T(8,128)(2,1)}), bf16[4,80,2,3,128]{4,1,3,2,0:T(8,128)(2,1)S(1)}, u32[]{:S(2)}, u32[]{:S(2)}) async-start(bf16[4,80,2,3,128]{4,1,3,2,0:T(8,128)(2,1)} %copy.42), calls=%async_computation.2 | async-start | bytes 983040 | tf_op jit(solution)/shard_map/all_to_all | solution.py:123
  112.9 31.8 %all-to-all-start.4 = ((bf16[128,4,384]{2,1,0:T(4,128)(2,1)}), bf16[128,4,384]{2,1,0:T(4,128)(2,1)S(1)}, u32[]{:S(2)}, u32[]{:S(2)}) async-start(bf16[128,4,384]{2,1,0:T(4,128)(2,1)} %bitcast.28), calls=%async_computation.4 | async-start | bytes 786432 | tf_op jit(solution)/shard_map/all_to_all | solution.py:57

commit v10 on v9

--- a/solution.py
+++ b/solution.py
@@ -86,7 +86,7 @@
         asked_onehot, spec_rows.reshape(per_block, -1), preferred_element_type=jnp.float32
     ).astype(spectra.dtype)
     rows_new = blk_exchange(asked_rows.reshape(block_total, -1)).reshape(
-        band_total, item_count, 2, 3, freq_dev
+        band_total, item_count // slot_cap, 4, -1
     )
     lag_low = NT // 32
     lag_high = NT // 4
@@ -118,9 +118,19 @@
     basis, observed_rows, window, rows_new = lax.optimization_barrier(
         (basis, observed_rows, window, rows_new)
     )
-    own_table = jnp.broadcast_to(spec_rows[None], (band_total, per_block, 2, 3, freq_dev))
+    own_table = jnp.broadcast_to(
+        spec_rows.reshape(1, per_block // 2, 4, -1), (band_total, per_block // 2, 4, 3 * freq_dev)
+    )
     sent = jnp.concatenate([rows_new, own_table], axis=1)
     whole_band = lax.all_to_all(sent, "frq", split_axis=0, concat_axis=0, tiled=True)
+    split_at = item_count // slot_cap
+    whole_band = jnp.concatenate(
+        [
+            whole_band[:, :split_at].reshape(band_total, item_count, 2, 3, freq_dev),
+            whole_band[:, split_at:].reshape(band_total, per_block, 2, 3, freq_dev),
+        ],
+        axis=1,
+    )
     whole_band = jnp.transpose(whole_band, (2, 3, 1, 0, 4)).reshape(
         2, 3, item_count + per_block, NF
     )

time: 159 us -> 161 us (1.013)
  other arithmetic: 25.4 us -> 27.1 us
where the time goes in v10:
time: 161 us; the launch traced here: 160 us
  waiting for transfers between devices  46.3 us (29%)
  starting transfers between devices  43.4 us (27%)
  other arithmetic  27.1 us (17%)
  blocking collectives  23.9 us (15%)
  matrix products  10.5 us (7%)
  local copies, waits for them, and re-layouts  8.6 us (5%)
    all_to_all x2, waiting for transfers between devices, blk_exchange(): lax.all_to_all(chunks.reshape(count, 4, width // 4), 'blk', split_axis=0,...  24.7 us
    all_to_all x1, starting transfers between devices, local(): lax.all_to_all(partner_local, 'blk', split_axis=0, concat_axis=0, tiled=T...  21.3 us
    all_to_all x1, waiting for transfers between devices, local(): lax.all_to_all(partner_local, 'blk', split_axis=0, concat_axis=0, tiled=T...  13.3 us
    all_to_all x2, starting transfers between devices, blk_exchange(): lax.all_to_all(chunks.reshape(count, 4, width // 4), 'blk', split_axis=0,...  12.6 us
    all_to_all x1, blocking collectives, local(): lax.all_to_all(product.reshape(band_total, NT // band_total, 3, per_block...  12.1 us
    all_to_all x1, blocking collectives, local(): lax.all_to_all(back_sent, 'frq', split_axis=0, concat_axis=0, tiled=True)  11.8 us
    all_to_all x1, starting transfers between devices, local(): lax.all_to_all(sent, 'frq', split_axis=0, concat_axis=0, tiled=True)  9.44 us
    div x1, other arithmetic, local(): sin_full = jnp.sin(phase_full) / math.sqrt(NF)  8.6 us
  transfers between devices with their start and end apart: 4, of which 4 were waited for; matrix products, arithmetic and copies ran while one was open for 16% of the time, Pallas kernels for 0%

profile of v10, /device:TPU:1, one launch (start us, length us, event | category | flops | bytes accessed | tf_op | source)
XLA Modules:
  0.0 160.2 jit_solution(7472070201460475669)
XLA Ops:
  0.0 1.4 copy.38
  1.4 21.3 %all-to-all-start = ((s32[128,1,2]{2,1,0:T(1,128)}), s32[128,1,2]{2,1,0:T(1,128)S(1)}, u32[]{:S(2)}, u32[]{:S(2)}) async-start(s32[128,1,2]{2,1,0:T(1,128)} %bitcast.5), calls=%async_computation | async-start | bytes 131072 | tf_op jit(solution)/shard_map/all_to_all | solution.py:81
  22.8 0.8 copy.39
  23.7 13.3 %all-to-all-done = s32[128,1,2]{2,1,0:T(1,128)S(1)} async-done(((s32[128,1,2]{2,1,0:T(1,128)}), s32[128,1,2]{2,1,0:T(1,128)S(1)}, u32[]{:S(2)}, u32[]{:S(2)}) %all-to-all-start) | async-done | bytes 1056 | tf_op jit(solution)/shard_map/all_to_all | solution.py:81
  37.5 0.8 reduce.3
  38.8 1.0 reshape_reshape.9
  39.8 6.2 %all-to-all-start.1 = ((bf16[128,4,384]{2,1,0:T(4,128)(2,1)}), bf16[128,4,384]{2,1,0:T(4,128)(2,1)S(1)}, u32[]{:S(2)}, u32[]{:S(2)}) async-start(bf16[128,4,384]{2,1,0:T(4,128)(2,1)} %reshape_reshape.9), calls=%async_computation.1 | async-start | bytes 786432 | tf_op jit(solution)/shard_map/all_to_all | solution.py:57
  47.4 4.3 %fusion.31 = bf16[512,448]{1,0:T(8,128)(2,1)S(1)} fusion(s32[448]{0:T(512)S(1)} %pad_add_fusion, s32[512]{0:T(512)S(1)} %multiply_add_fusion.1), kind=kLoop, calls=%fused_computation.57 | loop fusion | flops 4358144 | bytes 462592 | tf_op jit(solution)/shard_map/neg | solution.py:104
  51.6 4.2 %multiply_convert_fusion.1 = bf16[512,448]{1,0:T(8,128)(2,1)S(1)} fusion(s32[448]{0:T(512)S(1)} %pad_add_fusion, s32[512]{0:T(512)S(1)} %multiply_add_fusion.1), kind=kLoop, calls=%fused_computation.48 | loop fusion | flops 3670016 | bytes 462592 | tf_op jit(solution)/shard_map/convert_element_type | solution.py:103
  55.9 1.2 pad_maximum_fusion
  57.1 1.1 maximum_convert_fusion
  58.2 11.8 %all-to-all-done.1 = bf16[128,4,384]{2,1,0:T(4,128)(2,1)S(1)} async-done(((bf16[128,4,384]{2,1,0:T(4,128)(2,1)}), bf16[128,4,384]{2,1,0:T(4,128)(2,1)S(1)}, u32[]{:S(2)}, u32[]{:S(2)}) %all-to-all-start.1) | async-done | bytes 393248 | tf_op jit(solution)/shard_map/all_to_all | solution.py:57
  70.0 1.1 pad_maximum_fusion.1
  71.1 9.4 %all-to-all-start.2 = ((bf16[4,40,4,384]{3,2,1,0:T(4,128)(2,1)}), bf16[4,40,4,384]{3,2,1,0:T(4,128)(2,1)S(1)}, u32[]{:S(2)}, u32[]{:S(2)}) async-start(bf16[4,40,4,384]{3,2,1,0:T(4,128)(2,1)} %pad_maximum_fusion.1), calls=%async_computation.2 | async-start | bytes 983040 | tf_op jit(solution)/shard_map/all_to_all | solution.py:125
  81.4 8.3 %all-to-all-done.2 = bf16[4,40,4,384]{3,2,1,0:T(4,128)(2,1)S(1)} async-done(((bf16[4,40,4,384]{3,2,1,0:T(4,128)(2,1)}), bf16[4,40,4,384]{3,2,1,0:T(4,128)(2,1)S(1)}, u32[]{:S(2)}, u32[]{:S(2)}) %all-to-all-start.2) | async-done | bytes 491552 | tf_op jit(solution)/shard_map/all_to_all | solution.py:125
  91.8 1.4 multiply_add_fusion
  93.2 5.8 %convolution_reduce-precision_fusion = f32[576,1024]{1,0:T(8,128)} fusion(bf16[1024,448]{1,0:T(8,128)(2,1)} %pad_maximum_fusion, f32[576,448]{0,1:T(8,128)} %maximum_convert_fusion, f32[576,512]{1,0:T(8,128)} %bitcast.86, f32[576,512]{1,0:T(8,128)S(1)} %bitcast.85, f32[576]{0:T(1024)S(1)} %mul.259, f32[448]{0:T(512)S(1)} %copy-done.3, f32[576]{0:T(1024)S(1)} %mul.262), kind=kOutput, calls=%fused_computation.20 | convolution fusion | flops 1060356096 | bytes 6674688 | tf_op jit(solution)/shard_map/dot_general | solution.py:172
  99.0 2.4 %add_reduce_fusion = (bf16[3,64,512]{2,1,0:T(8,128)(2,1)S(1)}, bf16[3,64,512]{2,1,0:T(8,128)(2,1)S(1)}, f32[3,64,512]{2,1,0:T(8,128)S(1)}, f32[3,64,512]{2,1,0:T(8,128)S(1)}) fusion(f32[3,3,64,1024]{3,2,1,0:T(8,128)} %bitcast.78, f32[3,64,512]{2,1,0:T(8,128)S(1)} %get-tuple-element.24, f32[3,64,512]{2,1,0:T(8,128)S(1)} %get-tuple-element.23, ...), kind=kLoop, calls=%fused_computation.30 | loop fusion | flops 4325376 | bytes 5111808 | tf_op jit(solution)/shard_map/reduce_sum | solution.py:182
  102.2 11.8 %all_to_all.34 = bf16[4,32,4,384]{3,2,1,0:T(4,128)(2,1)} all-to-all(bf16[4,32,4,384]{3,2,1,0:T(4,128)(2,1)S(1)} %reshape.96), channel_id=1, replica_groups=mesh['blk'=128,'frq'=4] {'frq'}, dimensions={0} | all-to-all | bytes 786432 | tf_op jit(solution)/shard_map/all_to_all | solution.py:209
  114.1 6.4 %all-to-all-start.4 = ((bf16[128,4,384]{2,1,0:T(4,128)(2,1)}), bf16[128,4,384]{2,1,0:T(4,128)(2,1)S(1)}, u32[]{:S(2)}, u32[]{:S(2)}) async-start(bf16[128,4,384]{2,1,0:T(4,128)(2,1)} %bitcast.29), calls=%async_computation.4 | async-start | bytes 786432 | tf_op jit(solution)/shard_map/all_to_all | solution.py:57
  120.5 8.6 %sine_multiply_fusion = (f32[512,1024]{1,0:T(8,128)S(1)}, f32[512,1024]{1,0:T(8,128)S(1)}, f32[512,1024]{1,0:T(8,128)S(1)}) fusion(s32[512]{0:T(512)S(1)} %multiply_add_fusion.1), kind=kLoop, calls=%fused_computation.12 | loop fusion | flops 8912896 | bytes 6293504 | tf_op jit(solution)/shard_map/div | solution.py:195
  130.2 2.7 %fusion = f32[1024,48]{0,1:T(8,128)S(1)} fusion(f32[1024,48]{0,1:T(8,128)S(1)} %bitcast.87, f32[512,1024]{1,0:T(8,128)S(1)} %get-tuple-element.28, f32[512,1024]{1,0:T(8,128)S(1)} %get-tuple-element.29), kind=kOutput, calls=%fused_computation | convolution fusion | flops 605028352 | bytes 4587520 | tf_op jit(solution)/shard_map/dot_general | solution.py:197
  133.0 12.9 %all-to-all-done.4 = bf16[128,4,384]{2,1,0:T(4,128)(2,1)S(1)} async-done(((bf16[128,4,384]{2,1,0:T(4,128)(2,1)}), bf16[128,4,384]{2,1,0:T(4,128)(2,1)S(1)}, u32[]{:S(2)}, u32[]{:S(2)}) %all-to-all-start.4) | async-done | bytes 393248 | tf_op jit(solution)/shard_map/all_to_all | solution.py:57
  147.5 12.1 %all_to_all.35 = f32[4,256,3,16]{1,3,2,0:T(8,128)S(1)} all-to-all(f32[4,256,3,16]{1,3,2,0:T(8,128)S(1)} %copy.46), channel_id=1, replica_groups=mesh['blk'=128,'frq'=4] {'frq'}, dimensions={0} | all-to-all | bytes 393216 | tf_op jit(solution)/shard_map/all_to_all | solution.py:238
  (62 shorter events, 9.4 us)
Async XLA Ops:
  1.4 35.6 %all-to-all-start = ((s32[128,1,2]{2,1,0:T(1,128)}), s32[128,1,2]{2,1,0:T(1,128)S(1)}, u32[]{:S(2)}, u32[]{:S(2)}) async-start(s32[128,1,2]{2,1,0:T(1,128)} %bitcast.5), calls=%async_computation | async-start | bytes 131072 | tf_op jit(solution)/shard_map/all_to_all | solution.py:81
  22.8 23.2 %copy-start = (bf16[64,3,3,1024]{3,0,2,1:T(8,128)(2,1)S(1)}, bf16[64,3,3,1024]{3,0,2,1:T(8,128)(2,1)}, u32[]{:S(2)}) copy-start(bf16[64,3,3,1024]{3,0,2,1:T(8,128)(2,1)} %param.6) | copy-start | bytes 3538948
  39.8 30.2 %all-to-all-start.1 = ((bf16[128,4,384]{2,1,0:T(4,128)(2,1)}), bf16[128,4,384]{2,1,0:T(4,128)(2,1)S(1)}, u32[]{:S(2)}, u32[]{:S(2)}) async-start(bf16[128,4,384]{2,1,0:T(4,128)(2,1)} %reshape_reshape.9), calls=%async_computation.1 | async-start | bytes 786432 | tf_op jit(solution)/shard_map/all_to_all | solution.py:57
  58.2 22.4 %copy-start.4 = (s32[1,128,2]{1,2,0:T(2,128)S(1)}, s32[1,128,2]{1,2,0:T(2,128)}, u32[]{:S(2)}) copy-start(s32[1,128,2]{1,2,0:T(2,128)} %param.7) | copy-start | bytes 3076
  58.2 22.7 %copy-start.5 = (s32[1,128]{1,0:T(1,128)S(1)}, s32[1,128]{1,0:T(1,128)}, u32[]{:S(2)}) copy-start(s32[1,128]{1,0:T(1,128)} %param.9) | copy-start | bytes 1540
  71.1 18.6 %all-to-all-start.2 = ((bf16[4,40,4,384]{3,2,1,0:T(4,128)(2,1)}), bf16[4,40,4,384]{3,2,1,0:T(4,128)(2,1)S(1)}, u32[]{:S(2)}, u32[]{:S(2)}) async-start(bf16[4,40,4,384]{3,2,1,0:T(4,128)(2,1)} %pad_maximum_fusion.1), calls=%async_computation.2 | async-start | bytes 983040 | tf_op jit(solution)/shard_map/all_to_all | solution.py:125
  81.1 10.2 %copy-start.1 = (s32[64]{0:T(128)}, s32[64]{0:T(128)S(1)}, u32[]{:S(2)}) copy-start(s32[64]{0:T(128)S(1)} %dynamic_slice.12) | copy-start | bytes 772
  91.8 1.4 copy-start.3
  114.1 31.8 %all-to-all-start.4 = ((bf16[128,4,384]{2,1,0:T(4,128)(2,1)}), bf16[128,4,384]{2,1,0:T(4,128)(2,1)S(1)}, u32[]{:S(2)}, u32[]{:S(2)}) async-start(bf16[128,4,384]{2,1,0:T(4,128)(2,1)} %bitcast.29), calls=%async_computation.4 | async-start | bytes 786432 | tf_op jit(solution)/shard_map/all_to_all | solution.py:57
  129.1 0.6 copy-start.2

commit v11 on v9

--- a/solution.py
+++ b/solution.py
@@ -78,7 +78,13 @@
         .reshape(slot_total)
         .astype(jnp.float32)
     )
-    asked_ids = lax.all_to_all(partner_local, "blk", split_axis=0, concat_axis=0, tiled=True)
+    asked_ids = lax.all_to_all(
+        jnp.pad(partner_local[:, None, :], ((0, 0), (0, 0), (0, 128 - slot_cap))),
+        "blk",
+        split_axis=0,
+        concat_axis=0,
+        tiled=True,
+    )[:, 0, :slot_cap]
     asked_onehot = (
         asked_ids.reshape(slot_total)[:, None] == lax.iota(jnp.int32, per_block)[None, :]
     ).astype(spectra.dtype)

time: 159 us -> 158 us (level)
  no operation moved by 1% of the time
where the time goes in v11:
time: 158 us
  waiting for transfers between devices  47.3 us (30%)
  starting transfers between devices  43.4 us (27%)
  other arithmetic  24.6 us (16%)
  blocking collectives  23.9 us (15%)
  matrix products  10.5 us (7%)
  local copies, waits for them, and re-layouts  7.79 us (5%)
    all_to_all x2, waiting for transfers between devices, blk_exchange(): lax.all_to_all(chunks.reshape(count, 4, width // 4), 'blk', split_axis=0,...  25.7 us
    all_to_all x1, starting transfers between devices, local(): lax.all_to_all(jnp.pad(partner_local[:, None, :], ((0, 0), (0, 0), (0, 12...  21.3 us
    all_to_all x1, waiting for transfers between devices, local(): lax.all_to_all(jnp.pad(partner_local[:, None, :], ((0, 0), (0, 0), (0, 12...  13.3 us
    all_to_all x2, starting transfers between devices, blk_exchange(): lax.all_to_all(chunks.reshape(count, 4, width // 4), 'blk', split_axis=0,...  12.5 us
    all_to_all x1, blocking collectives, local(): lax.all_to_all(product.reshape(band_total, NT // band_total, 3, per_block...  12.1 us
    all_to_all x1, blocking collectives, local(): lax.all_to_all(back_sent, 'frq', split_axis=0, concat_axis=0, tiled=True)  11.9 us
    all_to_all x1, starting transfers between devices, local(): lax.all_to_all(sent, 'frq', split_axis=0, concat_axis=0, tiled=True)  9.54 us
    div x1, other arithmetic, local(): sin_full = jnp.sin(phase_full) / math.sqrt(NF)  8.6 us
  transfers between devices with their start and end apart: 4, of which 4 were waited for; matrix products, arithmetic and copies ran while one was open for 16% of the time, Pallas kernels for 0%

profile of v11, /device:TPU:1, one launch (start us, length us, event | category | flops | bytes accessed | tf_op | source)
XLA Modules:
  0.0 157.9 jit_solution(17686543532922327230)
XLA Ops:
  0.0 0.8 copy.39
  1.4 21.3 %all-to-all-start = ((s32[128,1,128]{2,1,0:T(1,128)}), s32[128,1,128]{2,1,0:T(1,128)S(1)}, u32[]{:S(2)}, u32[]{:S(2)}) async-start(s32[128,1,128]{2,1,0:T(1,128)} %pad.4), calls=%async_computation | async-start | bytes 131072 | tf_op jit(solution)/shard_map/all_to_all | solution.py:81
  22.8 0.8 copy.40
  23.7 13.3 %all-to-all-done = s32[128,1,128]{2,1,0:T(1,128)S(1)} async-done(((s32[128,1,128]{2,1,0:T(1,128)}), s32[128,1,128]{2,1,0:T(1,128)S(1)}, u32[]{:S(2)}, u32[]{:S(2)}) %all-to-all-start) | async-done | bytes 65568 | tf_op jit(solution)/shard_map/all_to_all | solution.py:81
  37.6 1.0 reshape_reshape.9
  38.6 6.2 %all-to-all-start.1 = ((bf16[128,4,384]{2,1,0:T(4,128)(2,1)}), bf16[128,4,384]{2,1,0:T(4,128)(2,1)S(1)}, u32[]{:S(2)}, u32[]{:S(2)}) async-start(bf16[128,4,384]{2,1,0:T(4,128)(2,1)} %reshape_reshape.9), calls=%async_computation.1 | async-start | bytes 786432 | tf_op jit(solution)/shard_map/all_to_all | solution.py:57
  45.6 4.3 %fusion.31 = bf16[512,448]{1,0:T(8,128)(2,1)S(1)} fusion(s32[448]{0:T(512)S(1)} %pad_add_fusion, s32[512]{0:T(512)S(1)} %multiply_add_fusion.1), kind=kLoop, calls=%fused_computation.57 | loop fusion | flops 4358144 | bytes 462592 | tf_op jit(solution)/shard_map/neg | solution.py:110
  49.8 4.2 %multiply_convert_fusion.1 = bf16[512,448]{1,0:T(8,128)(2,1)S(1)} fusion(s32[448]{0:T(512)S(1)} %pad_add_fusion, s32[512]{0:T(512)S(1)} %multiply_add_fusion.1), kind=kLoop, calls=%fused_computation.48 | loop fusion | flops 3670016 | bytes 462592 | tf_op jit(solution)/shard_map/convert_element_type | solution.py:109
  54.1 1.2 pad_maximum_fusion
  55.3 1.1 maximum_convert_fusion
  56.3 12.4 %all-to-all-done.1 = bf16[128,4,384]{2,1,0:T(4,128)(2,1)S(1)} async-done(((bf16[128,4,384]{2,1,0:T(4,128)(2,1)}), bf16[128,4,384]{2,1,0:T(4,128)(2,1)S(1)}, u32[]{:S(2)}, u32[]{:S(2)}) %all-to-all-start.1) | async-done | bytes 393248 | tf_op jit(solution)/shard_map/all_to_all | solution.py:57
  69.3 0.9 copy.42
  70.2 9.5 %all-to-all-start.2 = ((bf16[4,80,2,3,128]{4,1,3,2,0:T(8,128)(2,1)}), bf16[4,80,2,3,128]{4,1,3,2,0:T(8,128)(2,1)S(1)}, u32[]{:S(2)}, u32[]{:S(2)}) async-start(bf16[4,80,2,3,128]{4,1,3,2,0:T(8,128)(2,1)} %copy.42), calls=%async_computation.2 | async-start | bytes 983040 | tf_op jit(solution)/shard_map/all_to_all | solution.py:129
  80.6 8.3 %all-to-all-done.2 = bf16[4,80,2,3,128]{4,1,3,2,0:T(8,128)(2,1)S(1)} async-done(((bf16[4,80,2,3,128]{4,1,3,2,0:T(8,128)(2,1)}), bf16[4,80,2,3,128]{4,1,3,2,0:T(8,128)(2,1)S(1)}, u32[]{:S(2)}, u32[]{:S(2)}) %all-to-all-start.2) | async-done | bytes 491552 | tf_op jit(solution)/shard_map/all_to_all | solution.py:129
  89.5 1.4 multiply_add_fusion
  90.9 5.8 %convolution_reduce-precision_fusion = f32[576,1024]{1,0:T(8,128)} fusion(bf16[1024,448]{1,0:T(8,128)(2,1)} %pad_maximum_fusion, f32[576,448]{0,1:T(8,128)} %maximum_convert_fusion, f32[576,512]{1,0:T(8,128)} %bitcast.88, f32[576,512]{1,0:T(8,128)S(1)} %bitcast.87, f32[576]{0:T(1024)S(1)} %mul.259, f32[448]{0:T(512)S(1)} %and_convert_fusion, f32[576]{0:T(1024)S(1)} %mul.262), kind=kOutput, calls=%fused_computation.20 | convolution fusion | flops 1060356096 | bytes 6674688 | tf_op jit(solution)/shard_map/dot_general | solution.py:168
  96.7 2.4 %add_reduce_fusion = (bf16[3,64,512]{2,1,0:T(8,128)(2,1)S(1)}, bf16[3,64,512]{2,1,0:T(8,128)(2,1)S(1)}, f32[3,64,512]{2,1,0:T(8,128)S(1)}, f32[3,64,512]{2,1,0:T(8,128)S(1)}) fusion(f32[3,3,64,1024]{3,2,1,0:T(8,128)} %bitcast.81, f32[3,64,512]{2,1,0:T(8,128)S(1)} %get-tuple-element.24, f32[3,64,512]{2,1,0:T(8,128)S(1)} %get-tuple-element.23, ...), kind=kLoop, calls=%fused_computation.30 | loop fusion | flops 4325376 | bytes 5111808 | tf_op jit(solution)/shard_map/reduce_sum | solution.py:178
  99.9 11.9 %all_to_all.30 = bf16[4,32,4,384]{3,2,1,0:T(4,128)(2,1)} all-to-all(bf16[4,32,4,384]{3,2,1,0:T(4,128)(2,1)S(1)} %reshape.82), channel_id=1, replica_groups=mesh['blk'=128,'frq'=4] {'frq'}, dimensions={0} | all-to-all | bytes 786432 | tf_op jit(solution)/shard_map/all_to_all | solution.py:205
  111.8 6.4 %all-to-all-start.4 = ((bf16[128,4,384]{2,1,0:T(4,128)(2,1)}), bf16[128,4,384]{2,1,0:T(4,128)(2,1)S(1)}, u32[]{:S(2)}, u32[]{:S(2)}) async-start(bf16[128,4,384]{2,1,0:T(4,128)(2,1)} %bitcast.28), calls=%async_computation.4 | async-start | bytes 786432 | tf_op jit(solution)/shard_map/all_to_all | solution.py:57
  118.1 8.6 %sine_multiply_fusion = (f32[512,1024]{1,0:T(8,128)S(1)}, f32[512,1024]{1,0:T(8,128)S(1)}, f32[512,1024]{1,0:T(8,128)S(1)}) fusion(s32[512]{0:T(512)S(1)} %multiply_add_fusion.1), kind=kLoop, calls=%fused_computation.12 | loop fusion | flops 8912896 | bytes 6293504 | tf_op jit(solution)/shard_map/div | solution.py:191
  127.4 2.7 %fusion = f32[1024,48]{0,1:T(8,128)S(1)} fusion(f32[1024,48]{0,1:T(8,128)S(1)} %bitcast.89, f32[512,1024]{1,0:T(8,128)S(1)} %get-tuple-element.28, f32[512,1024]{1,0:T(8,128)S(1)} %get-tuple-element.29), kind=kOutput, calls=%fused_computation | convolution fusion | flops 605028352 | bytes 4587520 | tf_op jit(solution)/shard_map/dot_general | solution.py:193
  130.2 13.4 %all-to-all-done.4 = bf16[128,4,384]{2,1,0:T(4,128)(2,1)S(1)} async-done(((bf16[128,4,384]{2,1,0:T(4,128)(2,1)}), bf16[128,4,384]{2,1,0:T(4,128)(2,1)S(1)}, u32[]{:S(2)}, u32[]{:S(2)}) %all-to-all-start.4) | async-done | bytes 393248 | tf_op jit(solution)/shard_map/all_to_all | solution.py:57
  144.2 0.8 fusion.16
  145.2 12.1 %all_to_all.31 = f32[4,256,3,16]{1,3,2,0:T(8,128)S(1)} all-to-all(f32[4,256,3,16]{1,3,2,0:T(8,128)S(1)} %copy.48), channel_id=1, replica_groups=mesh['blk'=128,'frq'=4] {'frq'}, dimensions={0} | all-to-all | bytes 393216 | tf_op jit(solution)/shard_map/all_to_all | solution.py:234
  (51 shorter events, 7.0 us)
Async XLA Ops:
  1.4 35.5 %all-to-all-start = ((s32[128,1,128]{2,1,0:T(1,128)}), s32[128,1,128]{2,1,0:T(1,128)S(1)}, u32[]{:S(2)}, u32[]{:S(2)}) async-start(s32[128,1,128]{2,1,0:T(1,128)} %pad.4), calls=%async_computation | async-start | bytes 131072 | tf_op jit(solution)/shard_map/all_to_all | solution.py:81
  22.8 22.0 %copy-start = (bf16[64,3,3,1024]{3,0,2,1:T(8,128)(2,1)S(1)}, bf16[64,3,3,1024]{3,0,2,1:T(8,128)(2,1)}, u32[]{:S(2)}) copy-start(bf16[64,3,3,1024]{3,0,2,1:T(8,128)(2,1)} %param.6) | copy-start | bytes 3538948
  38.6 30.1 %all-to-all-start.1 = ((bf16[128,4,384]{2,1,0:T(4,128)(2,1)}), bf16[128,4,384]{2,1,0:T(4,128)(2,1)S(1)}, u32[]{:S(2)}, u32[]{:S(2)}) async-start(bf16[128,4,384]{2,1,0:T(4,128)(2,1)} %reshape_reshape.9), calls=%async_computation.1 | async-start | bytes 786432 | tf_op jit(solution)/shard_map/all_to_all | solution.py:57
  69.3 10.4 %copy-start.1 = (s32[1,128,2]{1,2,0:T(2,128)S(1)}, s32[1,128,2]{1,2,0:T(2,128)}, u32[]{:S(2)}) copy-start(s32[1,128,2]{1,2,0:T(2,128)} %param.7) | copy-start | bytes 3076
  69.3 10.7 %copy-start.2 = (s32[1,128]{1,0:T(1,128)S(1)}, s32[1,128]{1,0:T(1,128)}, u32[]{:S(2)}) copy-start(s32[1,128]{1,0:T(1,128)} %param.9) | copy-start | bytes 1540
  70.2 18.7 %all-to-all-start.2 = ((bf16[4,80,2,3,128]{4,1,3,2,0:T(8,128)(2,1)}), bf16[4,80,2,3,128]{4,1,3,2,0:T(8,128)(2,1)S(1)}, u32[]{:S(2)}, u32[]{:S(2)}) async-start(bf16[4,80,2,3,128]{4,1,3,2,0:T(8,128)(2,1)} %copy.42), calls=%async_computation.2 | async-start | bytes 983040 | tf_op jit(solution)/shard_map/all_to_all | solution.py:129
  111.8 31.8 %all-to-all-start.4 = ((bf16[128,4,384]{2,1,0:T(4,128)(2,1)}), bf16[128,4,384]{2,1,0:T(4,128)(2,1)S(1)}, u32[]{:S(2)}, u32[]{:S(2)}) async-start(bf16[128,4,384]{2,1,0:T(4,128)(2,1)} %bitcast.28), calls=%async_computation.4 | async-start | bytes 786432 | tf_op jit(solution)/shard_map/all_to_all | solution.py:57

commit v12 on v11

--- a/solution.py
+++ b/solution.py
@@ -191,7 +191,7 @@
     sin_full = jnp.sin(phase_full) / math.sqrt(NF)
     own_matrix = jnp.transpose(grad_group, (1, 3, 2, 0)).reshape(2 * NF, 3 * per_block)
     product_own = lax.dot_general(
-        jnp.concatenate([cos_full, -sin_full], axis=0),
+        jnp.concatenate([cos_full, -sin_full], axis=0).reshape(2 * NF, band_total, -1),
         own_matrix,
         (((0,), (0,)), ((), ())),
         precision=lax.Precision.HIGHEST,
@@ -225,7 +225,7 @@
         axis=0,
     )
     product = product_own + lax.dot_general(
-        basis_part,
+        basis_part.reshape(2 * freq_dev, band_total, -1),
         grad_matrix,
         (((0,), (0,)), ((), ())),
         precision=lax.Precision.HIGHEST,

time: 158 us -> 161 us (1.019)
  waiting for transfers between devices: 47.3 us -> 40.8 us
  other arithmetic: 24.6 us -> 29.4 us
  matrix products: 10.5 us -> 13.1 us
    all_to_all x2, waiting for transfers between devices: 25.7 us -> 19 us  [blk_exchange(): lax.all_to_all(chunks.reshape(count, 4, width // 4), 'blk', split_axis=0,...]
    div x1 -> x2, other arithmetic: 8.6 us -> 11.6 us  [local(): cos_full = jnp.cos(phase_full) / math.sqrt(NF)]
    dot_general x2, matrix products: 3.5 us -> 6.07 us  [the longest x1 4.97 us: local(): lax.dot_general(jnp.concatenate([cos_full, -sin_full], axis=0).reshape(2...]
  transfers between devices with their start and end apart: 4 -> 4, of which waited for: 4 -> 4; matrix products, arithmetic and copies ran while one was open for 16% -> 20% of each run, Pallas kernels for 0% -> 0%
where the time goes in v12:
time: 161 us
  starting transfers between devices  44.4 us (28%)
  waiting for transfers between devices  40.8 us (25%)
  other arithmetic  29.4 us (18%)
  blocking collectives  23.9 us (15%)
  matrix products  13.1 us (8%)
  local copies, waits for them, and re-layouts  8.83 us (5%)
    all_to_all x1, starting transfers between devices, local(): lax.all_to_all(jnp.pad(partner_local[:, None, :], ((0, 0), (0, 0), (0, 12...  21.3 us
    all_to_all x2, waiting for transfers between devices, blk_exchange(): lax.all_to_all(chunks.reshape(count, 4, width // 4), 'blk', split_axis=0,...  19 us
    all_to_all x2, starting transfers between devices, blk_exchange(): lax.all_to_all(chunks.reshape(count, 4, width // 4), 'blk', split_axis=0,...  13.6 us
    all_to_all x1, waiting for transfers between devices, local(): lax.all_to_all(jnp.pad(partner_local[:, None, :], ((0, 0), (0, 0), (0, 12...  13.5 us
    all_to_all x1, blocking collectives, local(): lax.all_to_all(product.reshape(band_total, NT // band_total, 3, per_block...  12.1 us
    all_to_all x1, blocking collectives, local(): lax.all_to_all(back_sent, 'frq', split_axis=0, concat_axis=0, tiled=True)  11.9 us
    div x2, other arithmetic, local(): cos_full = jnp.cos(phase_full) / math.sqrt(NF)  11.6 us
    all_to_all x1, starting transfers between devices, local(): lax.all_to_all(sent, 'frq', split_axis=0, concat_axis=0, tiled=True)  9.46 us
  transfers between devices with their start and end apart: 4, of which 4 were waited for; matrix products, arithmetic and copies ran while one was open for 20% of the time, Pallas kernels for 0%

profile of v12, /device:TPU:1, one launch (start us, length us, event | category | flops | bytes accessed | tf_op | source)
XLA Modules:
  0.0 160.8 jit_solution(305569558437307542)
XLA Ops:
  1.5 21.3 %all-to-all-start = ((s32[128,1,128]{2,1,0:T(1,128)}), s32[128,1,128]{2,1,0:T(1,128)S(1)}, u32[]{:S(2)}, u32[]{:S(2)}) async-start(s32[128,1,128]{2,1,0:T(1,128)} %pad.4), calls=%async_computation | async-start | bytes 131072 | tf_op jit(solution)/shard_map/all_to_all | solution.py:81
  23.7 13.5 %all-to-all-done = s32[128,1,128]{2,1,0:T(1,128)S(1)} async-done(((s32[128,1,128]{2,1,0:T(1,128)}), s32[128,1,128]{2,1,0:T(1,128)S(1)}, u32[]{:S(2)}, u32[]{:S(2)}) %all-to-all-start) | async-done | bytes 65568 | tf_op jit(solution)/shard_map/all_to_all | solution.py:81
  37.8 1.0 reshape_reshape.9
  38.8 6.2 %all-to-all-start.1 = ((bf16[128,4,384]{2,1,0:T(4,128)(2,1)}), bf16[128,4,384]{2,1,0:T(4,128)(2,1)S(1)}, u32[]{:S(2)}, u32[]{:S(2)}) async-start(bf16[128,4,384]{2,1,0:T(4,128)(2,1)} %reshape_reshape.9), calls=%async_computation.1 | async-start | bytes 786432 | tf_op jit(solution)/shard_map/all_to_all | solution.py:57
  45.8 4.3 %fusion.30 = bf16[512,448]{1,0:T(8,128)(2,1)S(1)} fusion(s32[448]{0:T(512)S(1)} %pad_add_fusion, s32[512]{0:T(512)S(1)} %multiply_add_fusion.2), kind=kLoop, calls=%fused_computation.62 | loop fusion | flops 4358144 | bytes 462592 | tf_op jit(solution)/shard_map/neg | solution.py:110
  50.1 4.2 %multiply_convert_fusion.1 = bf16[512,448]{1,0:T(8,128)(2,1)S(1)} fusion(s32[448]{0:T(512)S(1)} %pad_add_fusion, s32[512]{0:T(512)S(1)} %multiply_add_fusion.2), kind=kLoop, calls=%fused_computation.54 | loop fusion | flops 3670016 | bytes 462592 | tf_op jit(solution)/shard_map/convert_element_type | solution.py:109
  54.3 1.2 pad_maximum_fusion
  55.5 1.1 maximum_convert_fusion
  56.5 12.4 %all-to-all-done.1 = bf16[128,4,384]{2,1,0:T(4,128)(2,1)S(1)} async-done(((bf16[128,4,384]{2,1,0:T(4,128)(2,1)}), bf16[128,4,384]{2,1,0:T(4,128)(2,1)S(1)}, u32[]{:S(2)}, u32[]{:S(2)}) %all-to-all-start.1) | async-done | bytes 393248 | tf_op jit(solution)/shard_map/all_to_all | solution.py:57
  70.5 9.5 %all-to-all-start.2 = ((bf16[4,80,2,3,128]{4,1,3,2,0:T(8,128)(2,1)}), bf16[4,80,2,3,128]{4,1,3,2,0:T(8,128)(2,1)S(1)}, u32[]{:S(2)}, u32[]{:S(2)}) async-start(bf16[4,80,2,3,128]{4,1,3,2,0:T(8,128)(2,1)} %copy.45), calls=%async_computation.2 | async-start | bytes 983040 | tf_op jit(solution)/shard_map/all_to_all | solution.py:129
  80.8 8.3 %all-to-all-done.2 = bf16[4,80,2,3,128]{4,1,3,2,0:T(8,128)(2,1)S(1)} async-done(((bf16[4,80,2,3,128]{4,1,3,2,0:T(8,128)(2,1)}), bf16[4,80,2,3,128]{4,1,3,2,0:T(8,128)(2,1)S(1)}, u32[]{:S(2)}, u32[]{:S(2)}) %all-to-all-start.2) | async-done | bytes 491552 | tf_op jit(solution)/shard_map/all_to_all | solution.py:129
  89.7 1.4 multiply_add_fusion
  91.1 5.8 %convolution_reduce-precision_fusion = f32[576,1024]{1,0:T(8,128)} fusion(bf16[1024,448]{1,0:T(8,128)(2,1)} %pad_maximum_fusion, f32[576,448]{0,1:T(8,128)} %maximum_convert_fusion, f32[576,512]{1,0:T(8,128)} %bitcast.83, f32[576,512]{1,0:T(8,128)S(1)} %bitcast.82, f32[576]{0:T(1024)S(1)} %mul.278, f32[448]{0:T(512)S(1)} %and_convert_fusion, f32[576]{0:T(1024)S(1)} %mul.281), kind=kOutput, calls=%fused_computation.28 | convolution fusion | flops 1060356096 | bytes 6674688 | tf_op jit(solution)/shard_map/dot_general | solution.py:168
  96.9 3.1 %add_reduce_fusion = (bf16[3,64,512]{2,1,0:T(8,128)(2,1)S(1)}, bf16[3,64,512]{2,1,0:T(8,128)(2,1)S(1)}, f32[3,64,512]{2,1,0:T(8,128)S(1)}, f32[3,64,512]{2,1,0:T(8,128)}) fusion(f32[3,3,64,1024]{3,2,1,0:T(8,128)} %bitcast.76, f32[3,64,512]{2,1,0:T(8,128)S(1)} %get-tuple-element.26, f32[3,64,512]{2,1,0:T(8,128)S(1)} %get-tuple-element.25, ...), kind=kLoop, calls=%fused_computation.38 | loop fusion | flops 4325376 | bytes 5111808 | tf_op jit(solution)/shard_map/reduce_sum | solution.py:178
  100.8 11.9 %all_to_all.30 = bf16[4,32,4,384]{3,2,1,0:T(4,128)(2,1)} all-to-all(bf16[4,32,4,384]{3,2,1,0:T(4,128)(2,1)S(1)} %reshape.111), channel_id=1, replica_groups=mesh['blk'=128,'frq'=4] {'frq'}, dimensions={0} | all-to-all | bytes 786432 | tf_op jit(solution)/shard_map/all_to_all | solution.py:205
  112.7 7.4 %all-to-all-start.4 = ((bf16[128,4,384]{2,1,0:T(4,128)(2,1)}), bf16[128,4,384]{2,1,0:T(4,128)(2,1)}, u32[]{:S(2)}, u32[]{:S(2)}) async-start(bf16[128,4,384]{2,1,0:T(4,128)(2,1)} %bitcast.29), calls=%async_computation.4 | async-start | bytes 786432 | tf_op jit(solution)/shard_map/all_to_all | solution.py:57
  120.2 1.0 fusion.9
  121.2 1.9 %cosine_multiply_fusion.1 = (f32[128,1024]{0,1:T(8,128)S(1)}, f32[128,1024]{0,1:T(8,128)S(1)}) fusion(f32[512,1024]{0,1:T(8,128)S(1)} %fusion.9, s32[]{:T(128)S(6)} %select_n.33), kind=kLoop, calls=%fused_computation.64 | loop fusion | flops 393216 | bytes 1572868 | tf_op jit(solution)/shard_map/div | solution.py:190
  123.2 9.7 %cosine_multiply_fusion = (f32[512,4,256]{2,0,1:T(8,128)S(1)}, f32[512,4,256]{2,0,1:T(8,128)}) fusion(s32[4,256]{1,0:T(4,128)S(1)} %multiply_add_fusion.1, s32[512]{0:T(512)S(1)} %multiply_add_fusion.2), kind=kLoop, calls=%fused_computation.23 | loop fusion | flops 8912896 | bytes 4200448 | tf_op jit(solution)/shard_map/div | solution.py:190
  133.6 5.0 %fusion = f32[4,256,48]{1,2,0:T(8,128)} fusion(f32[1024,48,1]{0,1,2:T(8,128)S(1)} %reshape.117, f32[512,4,256]{2,0,1:T(8,128)} %get-tuple-element.30, f32[512,4,256]{2,0,1:T(8,128)S(1)} %get-tuple-element.29), kind=kOutput, calls=%fused_computation | convolution fusion | flops 605028352 | bytes 4587520 | tf_op jit(solution)/shard_map/dot_general | solution.py:193
  138.6 6.6 %all-to-all-done.4 = bf16[128,4,384]{2,1,0:T(4,128)(2,1)} async-done(((bf16[128,4,384]{2,1,0:T(4,128)(2,1)}), bf16[128,4,384]{2,1,0:T(4,128)(2,1)}, u32[]{:S(2)}, u32[]{:S(2)}) %all-to-all-start.4) | async-done | bytes 393248 | tf_op jit(solution)/shard_map/all_to_all | solution.py:57
  145.2 1.2 reshape.112
  147.0 1.1 fusion.19
  148.1 12.1 %all_to_all.31 = f32[4,256,3,16]{1,3,2,0:T(8,128)S(1)} all-to-all(f32[4,256,3,16]{1,3,2,0:T(8,128)S(1)} %bitcast.86), channel_id=1, replica_groups=mesh['blk'=128,'frq'=4] {'frq'}, dimensions={0} | all-to-all | bytes 393216 | tf_op jit(solution)/shard_map/all_to_all | solution.py:234
  (57 shorter events, 9.3 us)
Async XLA Ops:
  0.0 45.0 %copy-start.2 = (bf16[64,3,3,1024]{3,0,2,1:T(8,128)(2,1)S(1)}, bf16[64,3,3,1024]{3,0,2,1:T(8,128)(2,1)}, u32[]{:S(2)}) copy-start(bf16[64,3,3,1024]{3,0,2,1:T(8,128)(2,1)} %param.6) | copy-start | bytes 3538948
  1.5 35.6 %all-to-all-start = ((s32[128,1,128]{2,1,0:T(1,128)}), s32[128,1,128]{2,1,0:T(1,128)S(1)}, u32[]{:S(2)}, u32[]{:S(2)}) async-start(s32[128,1,128]{2,1,0:T(1,128)} %pad.4), calls=%async_computation | async-start | bytes 131072 | tf_op jit(solution)/shard_map/all_to_all | solution.py:81
  38.8 30.2 %all-to-all-start.1 = ((bf16[128,4,384]{2,1,0:T(4,128)(2,1)}), bf16[128,4,384]{2,1,0:T(4,128)(2,1)S(1)}, u32[]{:S(2)}, u32[]{:S(2)}) async-start(bf16[128,4,384]{2,1,0:T(4,128)(2,1)} %reshape_reshape.9), calls=%async_computation.1 | async-start | bytes 786432 | tf_op jit(solution)/shard_map/all_to_all | solution.py:57
  56.5 23.4 %copy-start.3 = (s32[1,128,2]{1,2,0:T(2,128)S(1)}, s32[1,128,2]{1,2,0:T(2,128)}, u32[]{:S(2)}) copy-start(s32[1,128,2]{1,2,0:T(2,128)} %param.7) | copy-start | bytes 3076
  69.2 11.1 %copy-start.4 = (s32[1,128]{1,0:T(1,128)S(1)}, s32[1,128]{1,0:T(1,128)}, u32[]{:S(2)}) copy-start(s32[1,128]{1,0:T(1,128)} %param.9) | copy-start | bytes 1540
  70.5 18.6 %all-to-all-start.2 = ((bf16[4,80,2,3,128]{4,1,3,2,0:T(8,128)(2,1)}), bf16[4,80,2,3,128]{4,1,3,2,0:T(8,128)(2,1)S(1)}, u32[]{:S(2)}, u32[]{:S(2)}) async-start(bf16[4,80,2,3,128]{4,1,3,2,0:T(8,128)(2,1)} %copy.45), calls=%async_computation.2 | async-start | bytes 983040 | tf_op jit(solution)/shard_map/all_to_all | solution.py:129
  112.7 32.5 %all-to-all-start.4 = ((bf16[128,4,384]{2,1,0:T(4,128)(2,1)}), bf16[128,4,384]{2,1,0:T(4,128)(2,1)}, u32[]{:S(2)}, u32[]{:S(2)}) async-start(bf16[128,4,384]{2,1,0:T(4,128)(2,1)} %bitcast.29), calls=%async_computation.4 | async-start | bytes 786432 | tf_op jit(solution)/shard_map/all_to_all | solution.py:57
  123.2 9.8 %copy-start = (f32[3,64,512]{2,1,0:T(8,128)S(1)}, f32[3,64,512]{2,1,0:T(8,128)}, u32[]{:S(2)}) copy-start(f32[3,64,512]{2,1,0:T(8,128)} %get-tuple-element.18) | copy-start | bytes 1179652
  138.6 8.4 %copy-start.1 = (f32[4,256,48]{1,2,0:T(8,128)S(1)}, f32[4,256,48]{1,2,0:T(8,128)}, u32[]{:S(2)}) copy-start(f32[4,256,48]{1,2,0:T(8,128)} %fusion) | copy-start | bytes 589828

commit v13 on v11

--- a/solution.py
+++ b/solution.py
@@ -211,7 +211,6 @@
     station_grad = jnp.dot(
         back_onehot,
         back_grad.reshape(slot_total, 6 * freq_dev),
-        precision=lax.Precision.HIGHEST,
         preferred_element_type=jnp.float32,
     )
     grad_matrix = jnp.transpose(
@@ -228,7 +227,7 @@
         basis_part,
         grad_matrix,
         (((0,), (0,)), ((), ())),
-        precision=lax.Precision.HIGHEST,
+        precision=lax.Precision.HIGH,
         preferred_element_type=jnp.float32,
     )
     lag_parts = lax.all_to_all(

time: 158 us -> 158 us (level)
  no operation moved by 1% of the time
where the time goes in v13:
time: 158 us
  waiting for transfers between devices  47.3 us (30%)
  starting transfers between devices  43.4 us (27%)
  other arithmetic  24.6 us (16%)
  blocking collectives  23.9 us (15%)
  matrix products  10.1 us (6%)
  local copies, waits for them, and re-layouts  7.79 us (5%)
    all_to_all x2, waiting for transfers between devices, blk_exchange(): lax.all_to_all(chunks.reshape(count, 4, width // 4), 'blk', split_axis=0,...  25.7 us
    all_to_all x1, starting transfers between devices, local(): lax.all_to_all(jnp.pad(partner_local[:, None, :], ((0, 0), (0, 0), (0, 12...  21.3 us
    all_to_all x1, waiting for transfers between devices, local(): lax.all_to_all(jnp.pad(partner_local[:, None, :], ((0, 0), (0, 0), (0, 12...  13.3 us
    all_to_all x2, starting transfers between devices, blk_exchange(): lax.all_to_all(chunks.reshape(count, 4, width // 4), 'blk', split_axis=0,...  12.5 us
    all_to_all x1, blocking collectives, local(): lax.all_to_all(product.reshape(band_total, NT // band_total, 3, per_block...  12.1 us
    all_to_all x1, blocking collectives, local(): lax.all_to_all(back_sent, 'frq', split_axis=0, concat_axis=0, tiled=True)  11.9 us
    all_to_all x1, starting transfers between devices, local(): lax.all_to_all(sent, 'frq', split_axis=0, concat_axis=0, tiled=True)  9.54 us
    div x1, other arithmetic, local(): sin_full = jnp.sin(phase_full) / math.sqrt(NF)  8.6 us
  transfers between devices with their start and end apart: 4, of which 4 were waited for; matrix products, arithmetic and copies ran while one was open for 16% of the time, Pallas kernels for 0%

profile of v13, /device:TPU:1, one launch (start us, length us, event | category | flops | bytes accessed | tf_op | source)
XLA Modules:
  0.0 157.6 jit_solution(17953428416312537583)
XLA Ops:
  0.0 0.8 copy.39
  0.8 0.7 pad.4
  1.4 21.3 %all-to-all-start = ((s32[128,1,128]{2,1,0:T(1,128)}), s32[128,1,128]{2,1,0:T(1,128)S(1)}, u32[]{:S(2)}, u32[]{:S(2)}) async-start(s32[128,1,128]{2,1,0:T(1,128)} %pad.4), calls=%async_computation | async-start | bytes 131072 | tf_op jit(solution)/shard_map/all_to_all | solution.py:81
  22.8 0.8 copy.40
  23.7 13.3 %all-to-all-done = s32[128,1,128]{2,1,0:T(1,128)S(1)} async-done(((s32[128,1,128]{2,1,0:T(1,128)}), s32[128,1,128]{2,1,0:T(1,128)S(1)}, u32[]{:S(2)}, u32[]{:S(2)}) %all-to-all-start) | async-done | bytes 65568 | tf_op jit(solution)/shard_map/all_to_all | solution.py:81
  37.6 1.0 reshape_reshape.9
  38.6 6.2 %all-to-all-start.1 = ((bf16[128,4,384]{2,1,0:T(4,128)(2,1)}), bf16[128,4,384]{2,1,0:T(4,128)(2,1)S(1)}, u32[]{:S(2)}, u32[]{:S(2)}) async-start(bf16[128,4,384]{2,1,0:T(4,128)(2,1)} %reshape_reshape.9), calls=%async_computation.1 | async-start | bytes 786432 | tf_op jit(solution)/shard_map/all_to_all | solution.py:57
  45.6 4.3 %fusion.31 = bf16[512,448]{1,0:T(8,128)(2,1)S(1)} fusion(s32[448]{0:T(512)S(1)} %pad_add_fusion, s32[512]{0:T(512)S(1)} %multiply_add_fusion.1), kind=kLoop, calls=%fused_computation.57 | loop fusion | flops 4358144 | bytes 462592 | tf_op jit(solution)/shard_map/neg | solution.py:110
  49.8 4.2 %multiply_convert_fusion.1 = bf16[512,448]{1,0:T(8,128)(2,1)S(1)} fusion(s32[448]{0:T(512)S(1)} %pad_add_fusion, s32[512]{0:T(512)S(1)} %multiply_add_fusion.1), kind=kLoop, calls=%fused_computation.48 | loop fusion | flops 3670016 | bytes 462592 | tf_op jit(solution)/shard_map/convert_element_type | solution.py:109
  54.1 1.2 pad_maximum_fusion
  55.3 1.1 maximum_convert_fusion
  56.3 12.4 %all-to-all-done.1 = bf16[128,4,384]{2,1,0:T(4,128)(2,1)S(1)} async-done(((bf16[128,4,384]{2,1,0:T(4,128)(2,1)}), bf16[128,4,384]{2,1,0:T(4,128)(2,1)S(1)}, u32[]{:S(2)}, u32[]{:S(2)}) %all-to-all-start.1) | async-done | bytes 393248 | tf_op jit(solution)/shard_map/all_to_all | solution.py:57
  69.3 0.9 copy.42
  70.2 9.5 %all-to-all-start.2 = ((bf16[4,80,2,3,128]{4,1,3,2,0:T(8,128)(2,1)}), bf16[4,80,2,3,128]{4,1,3,2,0:T(8,128)(2,1)S(1)}, u32[]{:S(2)}, u32[]{:S(2)}) async-start(bf16[4,80,2,3,128]{4,1,3,2,0:T(8,128)(2,1)} %copy.42), calls=%async_computation.2 | async-start | bytes 983040 | tf_op jit(solution)/shard_map/all_to_all | solution.py:129
  80.6 8.3 %all-to-all-done.2 = bf16[4,80,2,3,128]{4,1,3,2,0:T(8,128)(2,1)S(1)} async-done(((bf16[4,80,2,3,128]{4,1,3,2,0:T(8,128)(2,1)}), bf16[4,80,2,3,128]{4,1,3,2,0:T(8,128)(2,1)S(1)}, u32[]{:S(2)}, u32[]{:S(2)}) %all-to-all-start.2) | async-done | bytes 491552 | tf_op jit(solution)/shard_map/all_to_all | solution.py:129
  89.5 1.4 multiply_add_fusion
  90.9 5.8 %convolution_reduce-precision_fusion = f32[576,1024]{1,0:T(8,128)} fusion(bf16[1024,448]{1,0:T(8,128)(2,1)} %pad_maximum_fusion, f32[576,448]{0,1:T(8,128)} %maximum_convert_fusion, f32[576,512]{1,0:T(8,128)} %bitcast.88, f32[576,512]{1,0:T(8,128)S(1)} %bitcast.87, f32[576]{0:T(1024)S(1)} %mul.259, f32[448]{0:T(512)S(1)} %and_convert_fusion, f32[576]{0:T(1024)S(1)} %mul.262), kind=kOutput, calls=%fused_computation.20 | convolution fusion | flops 1060356096 | bytes 6674688 | tf_op jit(solution)/shard_map/dot_general | solution.py:168
  96.7 2.4 %add_reduce_fusion = (bf16[3,64,512]{2,1,0:T(8,128)(2,1)S(1)}, bf16[3,64,512]{2,1,0:T(8,128)(2,1)S(1)}, f32[3,64,512]{2,1,0:T(8,128)S(1)}, f32[3,64,512]{2,1,0:T(8,128)S(1)}) fusion(f32[3,3,64,1024]{3,2,1,0:T(8,128)} %bitcast.81, f32[3,64,512]{2,1,0:T(8,128)S(1)} %get-tuple-element.24, f32[3,64,512]{2,1,0:T(8,128)S(1)} %get-tuple-element.23, ...), kind=kLoop, calls=%fused_computation.30 | loop fusion | flops 4325376 | bytes 5111808 | tf_op jit(solution)/shard_map/reduce_sum | solution.py:178
  99.9 11.9 %all_to_all.30 = bf16[4,32,4,384]{3,2,1,0:T(4,128)(2,1)} all-to-all(bf16[4,32,4,384]{3,2,1,0:T(4,128)(2,1)S(1)} %reshape.82), channel_id=1, replica_groups=mesh['blk'=128,'frq'=4] {'frq'}, dimensions={0} | all-to-all | bytes 786432 | tf_op jit(solution)/shard_map/all_to_all | solution.py:205
  111.8 6.4 %all-to-all-start.4 = ((bf16[128,4,384]{2,1,0:T(4,128)(2,1)}), bf16[128,4,384]{2,1,0:T(4,128)(2,1)S(1)}, u32[]{:S(2)}, u32[]{:S(2)}) async-start(bf16[128,4,384]{2,1,0:T(4,128)(2,1)} %bitcast.28), calls=%async_computation.4 | async-start | bytes 786432 | tf_op jit(solution)/shard_map/all_to_all | solution.py:57
  118.1 8.6 %sine_multiply_fusion = (f32[512,1024]{1,0:T(8,128)S(1)}, f32[512,1024]{1,0:T(8,128)S(1)}, f32[512,1024]{1,0:T(8,128)S(1)}) fusion(s32[512]{0:T(512)S(1)} %multiply_add_fusion.1), kind=kLoop, calls=%fused_computation.12 | loop fusion | flops 8912896 | bytes 6293504 | tf_op jit(solution)/shard_map/div | solution.py:191
  127.4 2.7 %fusion = f32[1024,48]{0,1:T(8,128)S(1)} fusion(f32[1024,48]{0,1:T(8,128)S(1)} %bitcast.89, f32[512,1024]{1,0:T(8,128)S(1)} %get-tuple-element.28, f32[512,1024]{1,0:T(8,128)S(1)} %get-tuple-element.29), kind=kOutput, calls=%fused_computation | convolution fusion | flops 605028352 | bytes 4587520 | tf_op jit(solution)/shard_map/dot_general | solution.py:193
  130.2 13.4 %all-to-all-done.4 = bf16[128,4,384]{2,1,0:T(4,128)(2,1)S(1)} async-done(((bf16[128,4,384]{2,1,0:T(4,128)(2,1)}), bf16[128,4,384]{2,1,0:T(4,128)(2,1)S(1)}, u32[]{:S(2)}, u32[]{:S(2)}) %all-to-all-start.4) | async-done | bytes 393248 | tf_op jit(solution)/shard_map/all_to_all | solution.py:57
  144.8 12.1 %all_to_all.31 = f32[4,256,3,16]{1,3,2,0:T(8,128)S(1)} all-to-all(f32[4,256,3,16]{1,3,2,0:T(8,128)S(1)} %copy.48), channel_id=1, replica_groups=mesh['blk'=128,'frq'=4] {'frq'}, dimensions={0} | all-to-all | bytes 393216 | tf_op jit(solution)/shard_map/all_to_all | solution.py:233
  (51 shorter events, 6.8 us)
Async XLA Ops:
  1.4 35.5 %all-to-all-start = ((s32[128,1,128]{2,1,0:T(1,128)}), s32[128,1,128]{2,1,0:T(1,128)S(1)}, u32[]{:S(2)}, u32[]{:S(2)}) async-start(s32[128,1,128]{2,1,0:T(1,128)} %pad.4), calls=%async_computation | async-start | bytes 131072 | tf_op jit(solution)/shard_map/all_to_all | solution.py:81
  22.8 22.0 %copy-start = (bf16[64,3,3,1024]{3,0,2,1:T(8,128)(2,1)S(1)}, bf16[64,3,3,1024]{3,0,2,1:T(8,128)(2,1)}, u32[]{:S(2)}) copy-start(bf16[64,3,3,1024]{3,0,2,1:T(8,128)(2,1)} %param.6) | copy-start | bytes 3538948
  38.6 30.1 %all-to-all-start.1 = ((bf16[128,4,384]{2,1,0:T(4,128)(2,1)}), bf16[128,4,384]{2,1,0:T(4,128)(2,1)S(1)}, u32[]{:S(2)}, u32[]{:S(2)}) async-start(bf16[128,4,384]{2,1,0:T(4,128)(2,1)} %reshape_reshape.9), calls=%async_computation.1 | async-start | bytes 786432 | tf_op jit(solution)/shard_map/all_to_all | solution.py:57
  69.3 10.4 %copy-start.1 = (s32[1,128,2]{1,2,0:T(2,128)S(1)}, s32[1,128,2]{1,2,0:T(2,128)}, u32[]{:S(2)}) copy-start(s32[1,128,2]{1,2,0:T(2,128)} %param.7) | copy-start | bytes 3076
  69.3 10.7 %copy-start.2 = (s32[1,128]{1,0:T(1,128)S(1)}, s32[1,128]{1,0:T(1,128)}, u32[]{:S(2)}) copy-start(s32[1,128]{1,0:T(1,128)} %param.9) | copy-start | bytes 1540
  70.2 18.7 %all-to-all-start.2 = ((bf16[4,80,2,3,128]{4,1,3,2,0:T(8,128)(2,1)}), bf16[4,80,2,3,128]{4,1,3,2,0:T(8,128)(2,1)S(1)}, u32[]{:S(2)}, u32[]{:S(2)}) async-start(bf16[4,80,2,3,128]{4,1,3,2,0:T(8,128)(2,1)} %copy.42), calls=%async_computation.2 | async-start | bytes 983040 | tf_op jit(solution)/shard_map/all_to_all | solution.py:129
  111.8 31.8 %all-to-all-start.4 = ((bf16[128,4,384]{2,1,0:T(4,128)(2,1)}), bf16[128,4,384]{2,1,0:T(4,128)(2,1)S(1)}, u32[]{:S(2)}, u32[]{:S(2)}) async-start(bf16[128,4,384]{2,1,0:T(4,128)(2,1)} %bitcast.28), calls=%async_computation.4 | async-start | bytes 786432 | tf_op jit(solution)/shard_map/all_to_all | solution.py:57

commit v14 on v11

--- a/solution.py
+++ b/solution.py
@@ -164,13 +164,14 @@
     residual = (
         (correlation - observed_rows) * jnp.tile(alive_band, 9)[:, None] * window[None, :]
     ).astype(jnp.bfloat16)
-    adjoint_rows = lax.reduce_precision(
+    adjoint_rows = (
         lax.dot_general(
             residual, basis, (((1,), (1,)), ((), ())), preferred_element_type=jnp.float32
-        ),
-        exponent_bits=8,
-        mantissa_bits=7,
-    ).reshape(3, 3, item_count, 2 * NF)
+        )
+        .astype(jnp.bfloat16)
+        .astype(jnp.float32)
+        .reshape(3, 3, item_count, 2 * NF)
+    )
     adj_re = adjoint_rows[..., :NF]
     adj_im = adjoint_rows[..., NF:]
     own_re = jnp.sum(adj_re * second_re - adj_im * second_im, axis=1)

time: 158 us -> 156 us (0.987)
    reduce_sum x1, other arithmetic: 2.38 us -> 0.68 us  [local(): far_re = jnp.sum(adj_re * first_re + adj_im * first_im, axis=0)]
where the time goes in v14:
time: 156 us
  waiting for transfers between devices  47.4 us (30%)
  starting transfers between devices  43.4 us (28%)
  blocking collectives  23.9 us (15%)
  other arithmetic  23.5 us (15%)
  matrix products  9.43 us (6%)
  local copies, waits for them, and re-layouts  7.79 us (5%)
    all_to_all x2, waiting for transfers between devices, blk_exchange(): lax.all_to_all(chunks.reshape(count, 4, width // 4), 'blk', split_axis=0,...  25.8 us
    all_to_all x1, starting transfers between devices, local(): lax.all_to_all(jnp.pad(partner_local[:, None, :], ((0, 0), (0, 0), (0, 12...  21.3 us
    all_to_all x1, waiting for transfers between devices, local(): lax.all_to_all(jnp.pad(partner_local[:, None, :], ((0, 0), (0, 0), (0, 12...  13.3 us
    all_to_all x2, starting transfers between devices, blk_exchange(): lax.all_to_all(chunks.reshape(count, 4, width // 4), 'blk', split_axis=0,...  12.5 us
    all_to_all x1, blocking collectives, local(): lax.all_to_all(product.reshape(band_total, NT // band_total, 3, per_block...  12.1 us
    all_to_all x1, blocking collectives, local(): lax.all_to_all(back_sent, 'frq', split_axis=0, concat_axis=0, tiled=True)  11.8 us
    all_to_all x1, starting transfers between devices, local(): lax.all_to_all(sent, 'frq', split_axis=0, concat_axis=0, tiled=True)  9.54 us
    div x1, other arithmetic, local(): sin_full = jnp.sin(phase_full) / math.sqrt(NF)  8.6 us
  transfers between devices with their start and end apart: 4, of which 4 were waited for; matrix products, arithmetic and copies ran while one was open for 16% of the time, Pallas kernels for 0%

profile of v14, /device:TPU:1, one launch (start us, length us, event | category | flops | bytes accessed | tf_op | source)
XLA Modules:
  0.0 155.8 jit_solution(4452497379608101311)
XLA Ops:
  0.0 0.8 copy.39
  1.4 21.3 %all-to-all-start = ((s32[128,1,128]{2,1,0:T(1,128)}), s32[128,1,128]{2,1,0:T(1,128)S(1)}, u32[]{:S(2)}, u32[]{:S(2)}) async-start(s32[128,1,128]{2,1,0:T(1,128)} %pad.4), calls=%async_computation | async-start | bytes 131072 | tf_op jit(solution)/shard_map/all_to_all | solution.py:81
  22.8 0.8 copy.40
  23.7 13.3 %all-to-all-done = s32[128,1,128]{2,1,0:T(1,128)S(1)} async-done(((s32[128,1,128]{2,1,0:T(1,128)}), s32[128,1,128]{2,1,0:T(1,128)S(1)}, u32[]{:S(2)}, u32[]{:S(2)}) %all-to-all-start) | async-done | bytes 65568 | tf_op jit(solution)/shard_map/all_to_all | solution.py:81
  37.6 1.0 reshape_reshape.9
  38.6 6.2 %all-to-all-start.1 = ((bf16[128,4,384]{2,1,0:T(4,128)(2,1)}), bf16[128,4,384]{2,1,0:T(4,128)(2,1)S(1)}, u32[]{:S(2)}, u32[]{:S(2)}) async-start(bf16[128,4,384]{2,1,0:T(4,128)(2,1)} %reshape_reshape.9), calls=%async_computation.1 | async-start | bytes 786432 | tf_op jit(solution)/shard_map/all_to_all | solution.py:57
  45.6 4.3 %fusion.31 = bf16[512,448]{1,0:T(8,128)(2,1)S(1)} fusion(s32[448]{0:T(512)S(1)} %pad_add_fusion, s32[512]{0:T(512)S(1)} %multiply_add_fusion.1), kind=kLoop, calls=%fused_computation.57 | loop fusion | flops 4358144 | bytes 462592 | tf_op jit(solution)/shard_map/neg | solution.py:110
  49.8 4.2 %multiply_convert_fusion.1 = bf16[512,448]{1,0:T(8,128)(2,1)S(1)} fusion(s32[448]{0:T(512)S(1)} %pad_add_fusion, s32[512]{0:T(512)S(1)} %multiply_add_fusion.1), kind=kLoop, calls=%fused_computation.48 | loop fusion | flops 3670016 | bytes 462592 | tf_op jit(solution)/shard_map/convert_element_type | solution.py:109
  54.1 1.1 pad_maximum_fusion
  55.2 1.1 maximum_convert_fusion
  56.3 12.4 %all-to-all-done.1 = bf16[128,4,384]{2,1,0:T(4,128)(2,1)S(1)} async-done(((bf16[128,4,384]{2,1,0:T(4,128)(2,1)}), bf16[128,4,384]{2,1,0:T(4,128)(2,1)S(1)}, u32[]{:S(2)}, u32[]{:S(2)}) %all-to-all-start.1) | async-done | bytes 393248 | tf_op jit(solution)/shard_map/all_to_all | solution.py:57
  69.3 0.9 copy.42
  70.2 9.5 %all-to-all-start.2 = ((bf16[4,80,2,3,128]{4,1,3,2,0:T(8,128)(2,1)}), bf16[4,80,2,3,128]{4,1,3,2,0:T(8,128)(2,1)S(1)}, u32[]{:S(2)}, u32[]{:S(2)}) async-start(bf16[4,80,2,3,128]{4,1,3,2,0:T(8,128)(2,1)} %copy.42), calls=%async_computation.2 | async-start | bytes 983040 | tf_op jit(solution)/shard_map/all_to_all | solution.py:129
  80.6 8.3 %all-to-all-done.2 = bf16[4,80,2,3,128]{4,1,3,2,0:T(8,128)(2,1)S(1)} async-done(((bf16[4,80,2,3,128]{4,1,3,2,0:T(8,128)(2,1)}), bf16[4,80,2,3,128]{4,1,3,2,0:T(8,128)(2,1)S(1)}, u32[]{:S(2)}, u32[]{:S(2)}) %all-to-all-start.2) | async-done | bytes 491552 | tf_op jit(solution)/shard_map/all_to_all | solution.py:129
  89.5 1.8 %multiply_add_fusion = (f32[3,3,64,512]{3,2,1,0:T(8,128)}, f32[3,3,64,512]{3,2,1,0:T(8,128)}) fusion(f32[3,64,512]{2,1,0:T(8,128)S(1)} %get-tuple-element.26, f32[3,64,512]{2,1,0:T(8,128)S(1)} %get-tuple-element.24, f32[3,64,512]{2,1,0:T(8,128)S(1)} %get-tuple-element.25, f32[3,64,512]{2,1,0:T(8,128)S(1)} %get-tuple-element.23), kind=kLoop, calls=%fused_computation.35 | loop fusion | flops 1769472 | bytes 3932160 | tf_op jit(solution)/shard_map/add | solution.py:153
  91.3 4.7 %convolution_convert_fusion = bf16[576,1024]{1,0:T(8,128)(2,1)S(1)} fusion(bf16[1024,448]{1,0:T(8,128)(2,1)} %pad_maximum_fusion, f32[576,448]{0,1:T(8,128)} %maximum_convert_fusion, f32[576,512]{1,0:T(8,128)} %bitcast.89, f32[576,512]{1,0:T(8,128)} %bitcast.88, f32[576]{0:T(1024)S(1)} %mul.259, f32[448]{0:T(512)S(1)} %and_convert_fusion, f32[576]{0:T(1024)S(1)} %mul.262), kind=kOutput, calls=%fused_computation.22 | convolution fusion | flops 1060356096 | bytes 5495040 | tf_op jit(solution)/shard_map/dot_general | solution.py:168
  96.3 0.7 add_reduce_fusion
  97.8 11.8 %all_to_all.30 = bf16[4,32,4,384]{3,2,1,0:T(4,128)(2,1)} all-to-all(bf16[4,32,4,384]{3,2,1,0:T(4,128)(2,1)S(1)} %reshape.86), channel_id=1, replica_groups=mesh['blk'=128,'frq'=4] {'frq'}, dimensions={0} | all-to-all | bytes 786432 | tf_op jit(solution)/shard_map/all_to_all | solution.py:206
  109.7 6.4 %all-to-all-start.4 = ((bf16[128,4,384]{2,1,0:T(4,128)(2,1)}), bf16[128,4,384]{2,1,0:T(4,128)(2,1)S(1)}, u32[]{:S(2)}, u32[]{:S(2)}) async-start(bf16[128,4,384]{2,1,0:T(4,128)(2,1)} %bitcast.29), calls=%async_computation.4 | async-start | bytes 786432 | tf_op jit(solution)/shard_map/all_to_all | solution.py:57
  116.0 8.6 %sine_multiply_fusion = (f32[512,1024]{1,0:T(8,128)S(1)}, f32[512,1024]{1,0:T(8,128)S(1)}, f32[512,1024]{1,0:T(8,128)S(1)}) fusion(s32[512]{0:T(512)S(1)} %multiply_add_fusion.1), kind=kLoop, calls=%fused_computation.12 | loop fusion | flops 8912896 | bytes 6293504 | tf_op jit(solution)/shard_map/div | solution.py:192
  125.3 2.7 %fusion = f32[1024,48]{0,1:T(8,128)S(1)} fusion(f32[1024,48]{0,1:T(8,128)S(1)} %bitcast.90, f32[512,1024]{1,0:T(8,128)S(1)} %get-tuple-element.28, f32[512,1024]{1,0:T(8,128)S(1)} %get-tuple-element.29), kind=kOutput, calls=%fused_computation | convolution fusion | flops 605028352 | bytes 4587520 | tf_op jit(solution)/shard_map/dot_general | solution.py:194
  128.0 13.4 %all-to-all-done.4 = bf16[128,4,384]{2,1,0:T(4,128)(2,1)S(1)} async-done(((bf16[128,4,384]{2,1,0:T(4,128)(2,1)}), bf16[128,4,384]{2,1,0:T(4,128)(2,1)S(1)}, u32[]{:S(2)}, u32[]{:S(2)}) %all-to-all-start.4) | async-done | bytes 393248 | tf_op jit(solution)/shard_map/all_to_all | solution.py:57
  142.1 0.8 fusion.16
  143.1 12.1 %all_to_all.31 = f32[4,256,3,16]{1,3,2,0:T(8,128)S(1)} all-to-all(f32[4,256,3,16]{1,3,2,0:T(8,128)S(1)} %copy.48), channel_id=1, replica_groups=mesh['blk'=128,'frq'=4] {'frq'}, dimensions={0} | all-to-all | bytes 393216 | tf_op jit(solution)/shard_map/all_to_all | solution.py:235
  (52 shorter events, 7.3 us)
Async XLA Ops:
  1.4 35.5 %all-to-all-start = ((s32[128,1,128]{2,1,0:T(1,128)}), s32[128,1,128]{2,1,0:T(1,128)S(1)}, u32[]{:S(2)}, u32[]{:S(2)}) async-start(s32[128,1,128]{2,1,0:T(1,128)} %pad.4), calls=%async_computation | async-start | bytes 131072 | tf_op jit(solution)/shard_map/all_to_all | solution.py:81
  22.8 22.0 %copy-start = (bf16[64,3,3,1024]{3,0,2,1:T(8,128)(2,1)S(1)}, bf16[64,3,3,1024]{3,0,2,1:T(8,128)(2,1)}, u32[]{:S(2)}) copy-start(bf16[64,3,3,1024]{3,0,2,1:T(8,128)(2,1)} %param.6) | copy-start | bytes 3538948
  38.6 30.1 %all-to-all-start.1 = ((bf16[128,4,384]{2,1,0:T(4,128)(2,1)}), bf16[128,4,384]{2,1,0:T(4,128)(2,1)S(1)}, u32[]{:S(2)}, u32[]{:S(2)}) async-start(bf16[128,4,384]{2,1,0:T(4,128)(2,1)} %reshape_reshape.9), calls=%async_computation.1 | async-start | bytes 786432 | tf_op jit(solution)/shard_map/all_to_all | solution.py:57
  69.3 10.4 %copy-start.1 = (s32[1,128,2]{1,2,0:T(2,128)S(1)}, s32[1,128,2]{1,2,0:T(2,128)}, u32[]{:S(2)}) copy-start(s32[1,128,2]{1,2,0:T(2,128)} %param.7) | copy-start | bytes 3076
  69.3 10.7 %copy-start.2 = (s32[1,128]{1,0:T(1,128)S(1)}, s32[1,128]{1,0:T(1,128)}, u32[]{:S(2)}) copy-start(s32[1,128]{1,0:T(1,128)} %param.9) | copy-start | bytes 1540
  70.2 18.7 %all-to-all-start.2 = ((bf16[4,80,2,3,128]{4,1,3,2,0:T(8,128)(2,1)}), bf16[4,80,2,3,128]{4,1,3,2,0:T(8,128)(2,1)S(1)}, u32[]{:S(2)}, u32[]{:S(2)}) async-start(bf16[4,80,2,3,128]{4,1,3,2,0:T(8,128)(2,1)} %copy.42), calls=%async_computation.2 | async-start | bytes 983040 | tf_op jit(solution)/shard_map/all_to_all | solution.py:129
  109.7 31.8 %all-to-all-start.4 = ((bf16[128,4,384]{2,1,0:T(4,128)(2,1)}), bf16[128,4,384]{2,1,0:T(4,128)(2,1)S(1)}, u32[]{:S(2)}, u32[]{:S(2)}) async-start(bf16[128,4,384]{2,1,0:T(4,128)(2,1)} %bitcast.29), calls=%async_computation.4 | async-start | bytes 786432 | tf_op jit(solution)/shard_map/all_to_all | solution.py:57

commit v15 on v14

--- a/solution.py
+++ b/solution.py
@@ -212,7 +212,6 @@
     station_grad = jnp.dot(
         back_onehot,
         back_grad.reshape(slot_total, 6 * freq_dev),
-        precision=lax.Precision.HIGHEST,
         preferred_element_type=jnp.float32,
     )
     grad_matrix = jnp.transpose(
@@ -229,7 +228,7 @@
         basis_part,
         grad_matrix,
         (((0,), (0,)), ((), ())),
-        precision=lax.Precision.HIGHEST,
+        precision=lax.Precision.HIGH,
         preferred_element_type=jnp.float32,
     )
     lag_parts = lax.all_to_all(

time: 156 us -> 156 us (level)
  no operation moved by 1% of the time
where the time goes in v15:
time: 156 us; the launch traced here: 155 us
  waiting for transfers between devices  47.4 us (30%)
  starting transfers between devices  43.4 us (28%)
  blocking collectives  23.9 us (15%)
  other arithmetic  23.5 us (15%)
  matrix products  9.08 us (6%)
  local copies, waits for them, and re-layouts  7.79 us (5%)
    all_to_all x2, waiting for transfers between devices, blk_exchange(): lax.all_to_all(chunks.reshape(count, 4, width // 4), 'blk', split_axis=0,...  25.8 us
    all_to_all x1, starting transfers between devices, local(): lax.all_to_all(jnp.pad(partner_local[:, None, :], ((0, 0), (0, 0), (0, 12...  21.3 us
    all_to_all x1, waiting for transfers between devices, local(): lax.all_to_all(jnp.pad(partner_local[:, None, :], ((0, 0), (0, 0), (0, 12...  13.3 us
    all_to_all x2, starting transfers between devices, blk_exchange(): lax.all_to_all(chunks.reshape(count, 4, width // 4), 'blk', split_axis=0,...  12.5 us
    all_to_all x1, blocking collectives, local(): lax.all_to_all(product.reshape(band_total, NT // band_total, 3, per_block...  12.1 us
    all_to_all x1, blocking collectives, local(): lax.all_to_all(back_sent, 'frq', split_axis=0, concat_axis=0, tiled=True)  11.8 us
    all_to_all x1, starting transfers between devices, local(): lax.all_to_all(sent, 'frq', split_axis=0, concat_axis=0, tiled=True)  9.54 us
    div x1, other arithmetic, local(): sin_full = jnp.sin(phase_full) / math.sqrt(NF)  8.6 us
  transfers between devices with their start and end apart: 4, of which 4 were waited for; matrix products, arithmetic and copies ran while one was open for 16% of the time, Pallas kernels for 0%

profile of v15, /device:TPU:1, one launch (start us, length us, event | category | flops | bytes accessed | tf_op | source)
XLA Modules:
  0.0 155.4 jit_solution(10223456173367534544)
XLA Ops:
  0.0 0.8 copy.39
  0.8 0.7 pad.4
  1.4 21.3 %all-to-all-start = ((s32[128,1,128]{2,1,0:T(1,128)}), s32[128,1,128]{2,1,0:T(1,128)S(1)}, u32[]{:S(2)}, u32[]{:S(2)}) async-start(s32[128,1,128]{2,1,0:T(1,128)} %pad.4), calls=%async_computation | async-start | bytes 131072 | tf_op jit(solution)/shard_map/all_to_all | solution.py:81
  22.8 0.8 copy.40
  23.7 13.3 %all-to-all-done = s32[128,1,128]{2,1,0:T(1,128)S(1)} async-done(((s32[128,1,128]{2,1,0:T(1,128)}), s32[128,1,128]{2,1,0:T(1,128)S(1)}, u32[]{:S(2)}, u32[]{:S(2)}) %all-to-all-start) | async-done | bytes 65568 | tf_op jit(solution)/shard_map/all_to_all | solution.py:81
  37.6 1.0 reshape_reshape.9
  38.6 6.2 %all-to-all-start.1 = ((bf16[128,4,384]{2,1,0:T(4,128)(2,1)}), bf16[128,4,384]{2,1,0:T(4,128)(2,1)S(1)}, u32[]{:S(2)}, u32[]{:S(2)}) async-start(bf16[128,4,384]{2,1,0:T(4,128)(2,1)} %reshape_reshape.9), calls=%async_computation.1 | async-start | bytes 786432 | tf_op jit(solution)/shard_map/all_to_all | solution.py:57
  45.6 4.3 %fusion.31 = bf16[512,448]{1,0:T(8,128)(2,1)S(1)} fusion(s32[448]{0:T(512)S(1)} %pad_add_fusion, s32[512]{0:T(512)S(1)} %multiply_add_fusion.1), kind=kLoop, calls=%fused_computation.57 | loop fusion | flops 4358144 | bytes 462592 | tf_op jit(solution)/shard_map/neg | solution.py:110
  49.8 4.2 %multiply_convert_fusion.1 = bf16[512,448]{1,0:T(8,128)(2,1)S(1)} fusion(s32[448]{0:T(512)S(1)} %pad_add_fusion, s32[512]{0:T(512)S(1)} %multiply_add_fusion.1), kind=kLoop, calls=%fused_computation.48 | loop fusion | flops 3670016 | bytes 462592 | tf_op jit(solution)/shard_map/convert_element_type | solution.py:109
  54.1 1.1 pad_maximum_fusion
  55.2 1.1 maximum_convert_fusion
  56.3 12.4 %all-to-all-done.1 = bf16[128,4,384]{2,1,0:T(4,128)(2,1)S(1)} async-done(((bf16[128,4,384]{2,1,0:T(4,128)(2,1)}), bf16[128,4,384]{2,1,0:T(4,128)(2,1)S(1)}, u32[]{:S(2)}, u32[]{:S(2)}) %all-to-all-start.1) | async-done | bytes 393248 | tf_op jit(solution)/shard_map/all_to_all | solution.py:57
  69.3 0.9 copy.42
  70.2 9.5 %all-to-all-start.2 = ((bf16[4,80,2,3,128]{4,1,3,2,0:T(8,128)(2,1)}), bf16[4,80,2,3,128]{4,1,3,2,0:T(8,128)(2,1)S(1)}, u32[]{:S(2)}, u32[]{:S(2)}) async-start(bf16[4,80,2,3,128]{4,1,3,2,0:T(8,128)(2,1)} %copy.42), calls=%async_computation.2 | async-start | bytes 983040 | tf_op jit(solution)/shard_map/all_to_all | solution.py:129
  80.6 8.3 %all-to-all-done.2 = bf16[4,80,2,3,128]{4,1,3,2,0:T(8,128)(2,1)S(1)} async-done(((bf16[4,80,2,3,128]{4,1,3,2,0:T(8,128)(2,1)}), bf16[4,80,2,3,128]{4,1,3,2,0:T(8,128)(2,1)S(1)}, u32[]{:S(2)}, u32[]{:S(2)}) %all-to-all-start.2) | async-done | bytes 491552 | tf_op jit(solution)/shard_map/all_to_all | solution.py:129
  89.5 1.8 %multiply_add_fusion = (f32[3,3,64,512]{3,2,1,0:T(8,128)}, f32[3,3,64,512]{3,2,1,0:T(8,128)}) fusion(f32[3,64,512]{2,1,0:T(8,128)S(1)} %get-tuple-element.26, f32[3,64,512]{2,1,0:T(8,128)S(1)} %get-tuple-element.24, f32[3,64,512]{2,1,0:T(8,128)S(1)} %get-tuple-element.25, f32[3,64,512]{2,1,0:T(8,128)S(1)} %get-tuple-element.23), kind=kLoop, calls=%fused_computation.35 | loop fusion | flops 1769472 | bytes 3932160 | tf_op jit(solution)/shard_map/add | solution.py:153
  91.3 4.7 %convolution_convert_fusion = bf16[576,1024]{1,0:T(8,128)(2,1)S(1)} fusion(bf16[1024,448]{1,0:T(8,128)(2,1)} %pad_maximum_fusion, f32[576,448]{0,1:T(8,128)} %maximum_convert_fusion, f32[576,512]{1,0:T(8,128)} %bitcast.89, f32[576,512]{1,0:T(8,128)} %bitcast.88, f32[576]{0:T(1024)S(1)} %mul.259, f32[448]{0:T(512)S(1)} %and_convert_fusion, f32[576]{0:T(1024)S(1)} %mul.262), kind=kOutput, calls=%fused_computation.22 | convolution fusion | flops 1060356096 | bytes 5495040 | tf_op jit(solution)/shard_map/dot_general | solution.py:168
  96.3 0.7 add_reduce_fusion
  97.8 11.8 %all_to_all.30 = bf16[4,32,4,384]{3,2,1,0:T(4,128)(2,1)} all-to-all(bf16[4,32,4,384]{3,2,1,0:T(4,128)(2,1)S(1)} %reshape.86), channel_id=1, replica_groups=mesh['blk'=128,'frq'=4] {'frq'}, dimensions={0} | all-to-all | bytes 786432 | tf_op jit(solution)/shard_map/all_to_all | solution.py:206
  109.7 6.4 %all-to-all-start.4 = ((bf16[128,4,384]{2,1,0:T(4,128)(2,1)}), bf16[128,4,384]{2,1,0:T(4,128)(2,1)S(1)}, u32[]{:S(2)}, u32[]{:S(2)}) async-start(bf16[128,4,384]{2,1,0:T(4,128)(2,1)} %bitcast.29), calls=%async_computation.4 | async-start | bytes 786432 | tf_op jit(solution)/shard_map/all_to_all | solution.py:57
  116.0 8.6 %sine_multiply_fusion = (f32[512,1024]{1,0:T(8,128)S(1)}, f32[512,1024]{1,0:T(8,128)S(1)}, f32[512,1024]{1,0:T(8,128)S(1)}) fusion(s32[512]{0:T(512)S(1)} %multiply_add_fusion.1), kind=kLoop, calls=%fused_computation.12 | loop fusion | flops 8912896 | bytes 6293504 | tf_op jit(solution)/shard_map/div | solution.py:192
  125.3 2.7 %fusion = f32[1024,48]{0,1:T(8,128)S(1)} fusion(f32[1024,48]{0,1:T(8,128)S(1)} %bitcast.90, f32[512,1024]{1,0:T(8,128)S(1)} %get-tuple-element.28, f32[512,1024]{1,0:T(8,128)S(1)} %get-tuple-element.29), kind=kOutput, calls=%fused_computation | convolution fusion | flops 605028352 | bytes 4587520 | tf_op jit(solution)/shard_map/dot_general | solution.py:194
  128.0 13.4 %all-to-all-done.4 = bf16[128,4,384]{2,1,0:T(4,128)(2,1)S(1)} async-done(((bf16[128,4,384]{2,1,0:T(4,128)(2,1)}), bf16[128,4,384]{2,1,0:T(4,128)(2,1)S(1)}, u32[]{:S(2)}, u32[]{:S(2)}) %all-to-all-start.4) | async-done | bytes 393248 | tf_op jit(solution)/shard_map/all_to_all | solution.py:57
  142.7 12.1 %all_to_all.31 = f32[4,256,3,16]{1,3,2,0:T(8,128)S(1)} all-to-all(f32[4,256,3,16]{1,3,2,0:T(8,128)S(1)} %copy.48), channel_id=1, replica_groups=mesh['blk'=128,'frq'=4] {'frq'}, dimensions={0} | all-to-all | bytes 393216 | tf_op jit(solution)/shard_map/all_to_all | solution.py:234
  (52 shorter events, 7.1 us)
Async XLA Ops:
  1.4 35.5 %all-to-all-start = ((s32[128,1,128]{2,1,0:T(1,128)}), s32[128,1,128]{2,1,0:T(1,128)S(1)}, u32[]{:S(2)}, u32[]{:S(2)}) async-start(s32[128,1,128]{2,1,0:T(1,128)} %pad.4), calls=%async_computation | async-start | bytes 131072 | tf_op jit(solution)/shard_map/all_to_all | solution.py:81
  22.8 22.0 %copy-start = (bf16[64,3,3,1024]{3,0,2,1:T(8,128)(2,1)S(1)}, bf16[64,3,3,1024]{3,0,2,1:T(8,128)(2,1)}, u32[]{:S(2)}) copy-start(bf16[64,3,3,1024]{3,0,2,1:T(8,128)(2,1)} %param.6) | copy-start | bytes 3538948
  38.6 30.1 %all-to-all-start.1 = ((bf16[128,4,384]{2,1,0:T(4,128)(2,1)}), bf16[128,4,384]{2,1,0:T(4,128)(2,1)S(1)}, u32[]{:S(2)}, u32[]{:S(2)}) async-start(bf16[128,4,384]{2,1,0:T(4,128)(2,1)} %reshape_reshape.9), calls=%async_computation.1 | async-start | bytes 786432 | tf_op jit(solution)/shard_map/all_to_all | solution.py:57
  69.3 10.4 %copy-start.1 = (s32[1,128,2]{1,2,0:T(2,128)S(1)}, s32[1,128,2]{1,2,0:T(2,128)}, u32[]{:S(2)}) copy-start(s32[1,128,2]{1,2,0:T(2,128)} %param.7) | copy-start | bytes 3076
  69.3 10.7 %copy-start.2 = (s32[1,128]{1,0:T(1,128)S(1)}, s32[1,128]{1,0:T(1,128)}, u32[]{:S(2)}) copy-start(s32[1,128]{1,0:T(1,128)} %param.9) | copy-start | bytes 1540
  70.2 18.7 %all-to-all-start.2 = ((bf16[4,80,2,3,128]{4,1,3,2,0:T(8,128)(2,1)}), bf16[4,80,2,3,128]{4,1,3,2,0:T(8,128)(2,1)S(1)}, u32[]{:S(2)}, u32[]{:S(2)}) async-start(bf16[4,80,2,3,128]{4,1,3,2,0:T(8,128)(2,1)} %copy.42), calls=%async_computation.2 | async-start | bytes 983040 | tf_op jit(solution)/shard_map/all_to_all | solution.py:129
  109.7 31.8 %all-to-all-start.4 = ((bf16[128,4,384]{2,1,0:T(4,128)(2,1)}), bf16[128,4,384]{2,1,0:T(4,128)(2,1)S(1)}, u32[]{:S(2)}, u32[]{:S(2)}) async-start(bf16[128,4,384]{2,1,0:T(4,128)(2,1)} %bitcast.29), calls=%async_computation.4 | async-start | bytes 786432 | tf_op jit(solution)/shard_map/all_to_all | solution.py:57
